TPU v7x, 256 devices: a whole 4x4x8 slice. The times are simulated.
256 devices in a mesh: stn: 64 (over y, z, core), sec: 4 (over x).
Axes of the slice: x: 4, y: 4, z: 8, core: 2. Of those that a mesh axis runs over, the one named last changes fastest.
Arguments:
- voltages: bfloat16 [2, 1024, 569344], P(None, ('stn', 'sec')), may hold values from -6 to 6
- fir_taps: float32 [12, 4096], replicated, may hold values from -1.75 to 1.75
- cor_channels: int32 [256], replicated, may hold values from 0 to 4095, as said below
- beam_channels: int32 [256], replicated, may hold values from 1 to 4094, as said below
- cor_gain: float32 [256], replicated, as said below
- beam_gain: float32 [256], replicated, as said below
- beam_stations: int32 [16, 512], replicated, may hold values from 0 to 511
- beam_codes: int32 [16, 512], replicated, may hold values from 0 to 255
Outputs:
- visibilities: bfloat16 [256, 2, 1024, 1024], P(('stn', 'sec'))
- beams: bfloat16 [256, 16, 2, 256], P(('stn', 'sec'))
Inputs may be any that keep to these rules, and one draw needn't show every extreme that they name: cor_channels and beam_channels together are 512 distinct transform channels. None of beam_channels appears in cor_channels. `cor_gain`: positive. `beam_gain`: positive.
All inputs are finite; a program needn't handle non-finite values.
Results may differ from a plain program's by a relative error of at most 0.0085.
Values may be sent and summed in bfloat16 or wider, within the bound.
No kernel may reach another device: no remote copies, remote signals or barrier semaphores. Data moves between devices by JAX's collectives and lax.ppermute only.
A program may use at most 128 MiB of HBM per device.

v0:
```python
import math

import jax
import jax.numpy as jnp
from jax import lax
from jax.sharding import PartitionSpec as P

STATIONS = 512


epsilon = 1e-05


def make_tables(channel_of, points):
    sample_index = jnp.arange(points, dtype=jnp.int32)
    phase_turns = channel_of[:, None] * sample_index[None, :] % points
    phase_angle = phase_turns.astype(jnp.float32) * (2.0 * math.pi / points)
    table_scale = 1.0 / math.sqrt(points)
    cos_table = (jnp.cos(phase_angle) * table_scale).astype(jnp.bfloat16)
    sin_table = (jnp.sin(phase_angle) * table_scale).astype(jnp.bfloat16)
    return (cos_table, sin_table)


def make_weights(beam_stations, beam_codes, stations):
    station_ids = jnp.arange(stations, dtype=jnp.int32)
    onehot = (beam_stations[:, :, None] == station_ids[None, None, :]).astype(jnp.float32)
    amplitude = (1 + beam_codes // 64).astype(jnp.float32)
    phase_angle = (beam_codes % 64).astype(jnp.float32) * (2.0 * math.pi / 64.0)
    weight_re = jnp.einsum("bk,bks->bs", amplitude * jnp.cos(phase_angle), onehot)
    weight_im = jnp.einsum("bk,bks->bs", amplitude * jnp.sin(phase_angle), onehot)
    return (weight_re.astype(jnp.bfloat16), weight_im.astype(jnp.bfloat16))


def polyphase(in_block, fir_taps, spectra):
    tap_count, points = fir_taps.shape
    framed = in_block.reshape(in_block.shape[0], in_block.shape[1], -1, points)
    summed = jnp.zeros((framed.shape[0], framed.shape[1], spectra, points), jnp.float32)
    for tap_index in range(tap_count):
        summed = summed + fir_taps[tap_index] * framed[
            :, :, tap_index : tap_index + spectra, :
        ].astype(jnp.float32)
    return summed.astype(jnp.bfloat16)


def contract(left_rows, right_rows):
    contract_dims = (((1,), (1,)), ((), ()))
    return lax.dot_general(left_rows, right_rows, contract_dims, preferred_element_type=jnp.float32)


def spectrum(filtered, cos_table, sin_table, slot_gain):
    inputs_here, spectra, points = (filtered.shape[1], filtered.shape[2], filtered.shape[3])
    real_rows = filtered[0].reshape(inputs_here * spectra, points)
    imag_rows = filtered[1].reshape(inputs_here * spectra, points)
    spec_re = contract(cos_table, real_rows) + contract(sin_table, imag_rows)
    spec_im = contract(cos_table, imag_rows) - contract(sin_table, real_rows)
    combined = jnp.concatenate(
        [spec_re.reshape(-1, inputs_here, spectra), spec_im.reshape(-1, inputs_here, spectra)],
        axis=2,
    )
    return (combined * slot_gain[:, None, None]).astype(jnp.bfloat16)


def form_beams(beam_data, weight_re, weight_im):
    spectra = beam_data.shape[2] // 2
    samples = beam_data.reshape(beam_data.shape[0], -1, 2, beam_data.shape[2])
    with_re = jnp.einsum("bs,jspt->jbpt", weight_re, samples, preferred_element_type=jnp.float32)
    with_im = jnp.einsum("bs,jspt->jbpt", weight_im, samples, preferred_element_type=jnp.float32)
    out_re = with_re[..., :spectra] - with_im[..., spectra:]
    out_im = with_re[..., spectra:] + with_im[..., :spectra]
    return jnp.concatenate([out_re, out_im], axis=3)


def per_device(
    voltages, fir_taps, cor_channels, beam_channels, cor_gain, beam_gain, beam_stations, beam_codes
):
    tap_count, points = fir_taps.shape
    stn_count = lax.axis_size("stn")
    sec_count = lax.axis_size("sec")
    device_count = stn_count * sec_count
    inputs_here = voltages.shape[1]
    spectra = voltages.shape[2] // points - tap_count + 1
    filtered = polyphase(voltages, fir_taps, spectra)
    channel_of = jnp.concatenate([cor_channels, beam_channels])
    slot_gain = jnp.concatenate([cor_gain, beam_gain])
    cos_table, sin_table = make_tables(channel_of, points)
    weight_re, weight_im = make_weights(beam_stations, beam_codes, STATIONS)
    spectra_all = spectrum(filtered, cos_table, sin_table, slot_gain)
    outgoing = spectra_all.reshape(2, stn_count, sec_count, 1, 1, inputs_here, 2 * spectra)
    turned = lax.all_to_all(
        lax.all_to_all(outgoing, "stn", split_axis=1, concat_axis=3, tiled=True),
        "sec",
        split_axis=2,
        concat_axis=4,
        tiled=True,
    )
    received = turned.reshape(2, device_count * inputs_here, 2 * spectra)
    cor_data = received[0]
    beam_data = received[1:2]
    swapped = jnp.concatenate([cor_data[:, spectra:], -cor_data[:, :spectra]], axis=1)
    vis_re = contract(cor_data, cor_data) / spectra
    vis_im = contract(swapped, cor_data) / spectra
    visibilities = jnp.stack([vis_re, vis_im])[None].astype(jnp.bfloat16)
    raw_beams = form_beams(beam_data, weight_re, weight_im)
    local_power = jnp.sum(raw_beams * raw_beams, axis=(0, 2, 3))
    summed_power = lax.psum(local_power, ("stn", "sec"))
    beam_power = summed_power / (device_count * raw_beams.shape[2] * raw_beams.shape[3])
    beams = (raw_beams * lax.rsqrt(beam_power + epsilon)[None, :, None, None]).astype(jnp.bfloat16)
    return (visibilities, beams)


def solution(mesh):
    in_specs = (P(None, ("stn", "sec"), None), P(), P(), P(), P(), P(), P(), P())
    out_specs = (P(("stn", "sec"), None, None, None), P(("stn", "sec"), None, None, None))
    return jax.shard_map(
        per_device, mesh=mesh, in_specs=in_specs, out_specs=out_specs, check_vma=False
    )
```

profile of v0, /device:TPU:2, one launch (start us, length us, event | category | flops | bytes accessed | tf_op | source)
XLA Modules:
  0.0 347.0 jit_solution(4968068274849040461)
XLA Ops:
  0.6 1.8 fusion.60
  2.5 14.5 %reshape.175 = bf16[2,4,139,4096]{3,2,1,0:T(8,128)(2,1)} reshape(bf16[2,4,569344]{2,1,0:T(4,128)(2,1)} %param.8) | data formatting | bytes 18219008 | tf_op jit(solution)/shard_map/reshape | solution.py:36
  17.0 52.5 %add_convert_fusion = bf16[2,4,128,4096]{3,2,1,0:T(8,128)(2,1)} fusion(bf16[2,4,139,4096]{3,2,1,0:T(8,128)(2,1)} %reshape.175, f32[4096]{0:T(1024)S(1)} %bitcast.81, f32[4096]{0:T(1024)S(1)} %bitcast.82, f32[4096]{0:T(1024)S(1)} %bitcast.72, f32[4096]{0:T(1024)S(1)} %bitcast.73, f32[4096]{0:T(1024)S(1)} %bitcast.74, f32[4096]{0:T(1024)S(1)} %bitcast.75, ...), kind=kLoop, calls=%fused_computation.3 | loop fusion | flops 150994944 | bytes 109248512 | tf_op jit(solution)/shard_map/convert_element_type | solution.py:42
  69.5 0.0 copy-start.4
  69.5 0.0 copy-start.5
  69.5 4.0 %fusion.57 = (bf16[1,4,128,4096]{3,2,1,0:T(8,128)(2,1)S(1)}, bf16[1,4,128,4096]{3,2,1,0:T(8,128)(2,1)S(1)}) fusion(bf16[2,4,128,4096]{3,2,1,0:T(8,128)(2,1)} %add_convert_fusion), kind=kLoop, calls=%fused_computation.88 | loop fusion | bytes 16777216 | tf_op jit(solution)/shard_map/slice | solution.py:52
  73.5 0.0 copy-done.4
  73.5 0.0 copy-done.5
  73.5 0.0 copy-start
  73.6 31.8 %fusion.11 = f32[512,512]{1,0:T(8,128)S(1)} fusion(bf16[512,4096]{1,0:T(8,128)(2,1)S(1)} %bitcast.67, s32[512]{0:T(512)S(1)} %pad_add_fusion), kind=kOutput, calls=%fused_computation.21 | convolution fusion | flops 2181038080 | bytes 5244928 | tf_op jit(solution)/shard_map/dot_general | solution.py:47
  105.4 0.0 copy-done
  105.4 32.4 %fusion.10 = f32[512,512]{1,0:T(8,128)} fusion(bf16[512,4096]{1,0:T(8,128)(2,1)S(1)} %bitcast.69, s32[512]{0:T(512)S(1)} %pad_add_fusion), kind=kOutput, calls=%fused_computation.20 | convolution fusion | flops 2181038080 | bytes 5244928 | tf_op jit(solution)/shard_map/dot_general | solution.py:47
  137.7 32.1 %fusion.17 = f32[512,512]{1,0:T(8,128)S(1)} fusion(f32[512,512]{1,0:T(8,128)S(1)} %fusion.11, bf16[512,4096]{1,0:T(8,128)(2,1)S(1)} %bitcast.70, s32[512]{0:T(512)S(1)} %pad_add_fusion), kind=kOutput, calls=%fused_computation.29 | convolution fusion | flops 2181300224 | bytes 6293504 | tf_op jit(solution)/shard_map/dot_general | solution.py:47
  169.8 0.4 concatenate.56
  170.2 0.0 copy-start.2
  170.2 0.0 copy-start.3
  170.2 34.4 %fusion.18 = f32[512,512]{1,0:T(8,128)S(1)} fusion(f32[512,512]{1,0:T(8,128)} %fusion.10, bf16[512,4096]{1,0:T(8,128)(2,1)} %bitcast.68, s32[512]{0:T(512)S(1)} %pad_add_fusion), kind=kOutput, calls=%fused_computation.30 | convolution fusion | flops 2181300224 | bytes 6293504 | tf_op jit(solution)/shard_map/dot_general | solution.py:47
  204.7 0.0 copy-start.1
  204.7 0.0 copy-start.6
  204.7 0.4 concatenate.57
  205.0 0.0 copy-done.2
  205.1 0.1 concatenate.59
  205.2 0.0 copy-done.3
  205.2 0.1 concatenate.60
  205.3 0.1 copy.37
  205.4 0.7 fusion.14
  206.1 40.1 %all_to_all.33 = bf16[2,64,4,1,1,4,256]{6,5,2,0,4,3,1:T(4,128)(2,1)S(1)} all-to-all(bf16[2,64,4,1,1,4,256]{6,5,2,0,4,3,1:T(4,128)(2,1)S(1)} %fusion.14), channel_id=1, replica_groups=mesh['stn'=64,'sec'=4] {'stn'}, dimensions={1} | all-to-all | bytes 2097152 | tf_op jit(solution)/shard_map/all_to_all | solution.py:90
  246.2 1.4 copy.38
  247.6 4.8 %all-to-all-start.1 = ((bf16[2,1,4,64,1,4,256]{6,5,3,0,4,1,2:T(4,128)(2,1)}), bf16[2,1,4,64,1,4,256]{6,5,3,0,4,1,2:T(4,128)(2,1)S(1)}, u32[]{:S(2)}, u32[]{:S(2)}) async-start(bf16[2,1,4,64,1,4,256]{6,5,3,0,4,1,2:T(4,128)(2,1)} %copy.38), calls=%async_computation.1 | async-start | bytes 2097152 | tf_op jit(solution)/shard_map/all_to_all | solution.py:89
  252.4 0.0 copy-done.1
  252.4 0.2 multiply_bitcast_fusion.1
  252.6 0.0 copy-done.6
  252.6 3.2 fusion
  255.8 3.2 fusion.1
  259.0 7.6 %all-to-all-done.1 = bf16[2,1,4,64,1,4,256]{6,5,3,0,4,1,2:T(4,128)(2,1)S(1)} async-done(((bf16[2,1,4,64,1,4,256]{6,5,3,0,4,1,2:T(4,128)(2,1)}), bf16[2,1,4,64,1,4,256]{6,5,3,0,4,1,2:T(4,128)(2,1)S(1)}, u32[]{:S(2)}, u32[]{:S(2)}) %all-to-all-start.1) | async-done | bytes 1048608 | tf_op jit(solution)/shard_map/all_to_all | solution.py:89
  266.7 0.4 fusion.58
  267.0 0.2 copy.40
  267.2 0.3 reshape.176
  267.5 0.2 convolution_bitcast_fusion
  267.7 0.2 convolution_bitcast_fusion.1
  267.8 0.2 copy.39
  268.0 0.1 squeeze.3
  268.2 0.1 fusion.59
  268.3 0.1 multiply_reduce_fusion
  268.4 0.7 fusion.15
  269.1 73.8 %psum.7 = f32[16]{0:T(128)S(1)} all-reduce(f32[16]{0:T(128)S(1)} %multiply_reduce_fusion), channel_id=1, replica_groups=mesh['stn'=64,'sec'=4] {'stn','sec'}, use_global_device_ids=true, to_apply=%region_1.2 | all-reduce | flops 16 | bytes 128 | tf_op jit(solution)/shard_map/psum | solution.py:105
  343.0 0.1 multiply_convert_fusion.12
  343.0 0.6 copy.43
  343.7 0.7 fusion.16
  344.4 2.4 pad_maximum_fusion
  (4 shorter events, 0.0 us)
Async XLA Ops:
  69.5 4.0 %copy-start.4 = (s32[256]{0:T(256)S(1)}, s32[256]{0:T(256)}, u32[]{:S(2)}) copy-start(s32[256]{0:T(256)} %param.11) | copy-start | bytes 3076
  69.5 4.0 %copy-start.5 = (s32[256]{0:T(256)S(1)}, s32[256]{0:T(256)}, u32[]{:S(2)}) copy-start(s32[256]{0:T(256)} %param.10) | copy-start | bytes 3076
  73.5 31.8 %copy-start = (bf16[1,4,128,4096]{3,2,1,0:T(8,128)(2,1)}, bf16[1,4,128,4096]{3,2,1,0:T(8,128)(2,1)S(1)}, u32[]{:S(2)}) copy-start(bf16[1,4,128,4096]{3,2,1,0:T(8,128)(2,1)S(1)} %get-tuple-element.12) | copy-start | bytes 12582916
  170.2 34.8 %copy-start.2 = (f32[256]{0:T(256)S(1)}, f32[256]{0:T(256)}, u32[]{:S(2)}) copy-start(f32[256]{0:T(256)} %param.12) | copy-start | bytes 3076
  170.2 35.0 %copy-start.3 = (f32[256]{0:T(256)S(1)}, f32[256]{0:T(256)}, u32[]{:S(2)}) copy-start(f32[256]{0:T(256)} %param.13) | copy-start | bytes 3076
  204.7 47.8 %copy-start.1 = (s32[16,512]{1,0:T(8,128)S(1)}, s32[16,512]{1,0:T(8,128)}, u32[]{:S(2)}) copy-start(s32[16,512]{1,0:T(8,128)} %param.15) | copy-start | bytes 98308
  204.7 47.9 %copy-start.6 = (s32[16,512]{1,0:T(8,128)S(1)}, s32[16,512]{1,0:T(8,128)}, u32[]{:S(2)}) copy-start(s32[16,512]{1,0:T(8,128)} %param.14) | copy-start | bytes 98308
  247.6 19.1 %all-to-all-start.1 = ((bf16[2,1,4,64,1,4,256]{6,5,3,0,4,1,2:T(4,128)(2,1)}), bf16[2,1,4,64,1,4,256]{6,5,3,0,4,1,2:T(4,128)(2,1)S(1)}, u32[]{:S(2)}, u32[]{:S(2)}) async-start(bf16[2,1,4,64,1,4,256]{6,5,3,0,4,1,2:T(4,128)(2,1)} %copy.38), calls=%async_computation.1 | async-start | bytes 2097152 | tf_op jit(solution)/shard_map/all_to_all | solution.py:89
where the time goes:
time: 352 us; the launch traced here: 347 us
  matrix products  139 us (39%)
  blocking collectives  114 us (32%)
  other arithmetic  56.1 us (16%)
  local copies, waits for them, and re-layouts  24.4 us (7%)
  waiting for transfers between devices  7.63 us (2%)
  starting transfers between devices  4.82 us (1%)
    dot_general x6, matrix products, contract(): lax.dot_general(left_rows, right_rows, contract_dims, preferred_element_t...  132 us
    psum x1, blocking collectives, per_device(): summed_power = lax.psum(local_power, ('stn', 'sec'))  73.8 us
    convert_element_type x1, other arithmetic, polyphase(): return summed.astype(jnp.bfloat16)  52.5 us
    all_to_all x1, blocking collectives, per_device(): lax.all_to_all(outgoing, 'stn', split_axis=1, concat_axis=3, tiled=True)  40.1 us
    reshape x1, local copies, waits for them, and re-layouts, polyphase(): framed = in_block.reshape(in_block.shape[0], in_block.shape[1], -1, points)  14.5 us
    all_to_all x1, waiting for transfers between devices, per_device(): lax.all_to_all(lax.all_to_all(outgoing, 'stn', split_axis=1, concat_axis=...  7.63 us
  transfers between devices with their start and end apart: 1, of which 1 were waited for; matrix products, arithmetic and copies ran while one was open for 2% of the time, Pallas kernels for 0%

commit v1 on v0

--- a/solution.py
+++ b/solution.py
@@ -10,15 +10,27 @@
 
 epsilon = 1e-05
 
+STN_AXES = ("y", "z", "core")
+PHYSICAL_AXES = ("core", "x", "y", "z")
+
 
 def make_tables(channel_of, points):
-    sample_index = jnp.arange(points, dtype=jnp.int32)
-    phase_turns = channel_of[:, None] * sample_index[None, :] % points
-    phase_angle = phase_turns.astype(jnp.float32) * (2.0 * math.pi / points)
+    outer = 64
+    inner = points // outer
+    step = 2.0 * math.pi / points
+    a_index = jnp.arange(inner, dtype=jnp.int32)
+    b_index = jnp.arange(outer, dtype=jnp.int32)
+    a_turns = (channel_of[:, None] * a_index[None, :] % inner) * outer
+    b_turns = channel_of[:, None] * b_index[None, :] % points
+    a_angle = a_turns.astype(jnp.float32) * step
+    b_angle = b_turns.astype(jnp.float32) * step
+    ca, sa = jnp.cos(a_angle)[:, :, None], jnp.sin(a_angle)[:, :, None]
+    cb, sb = jnp.cos(b_angle)[:, None, :], jnp.sin(b_angle)[:, None, :]
     table_scale = 1.0 / math.sqrt(points)
-    cos_table = (jnp.cos(phase_angle) * table_scale).astype(jnp.bfloat16)
-    sin_table = (jnp.sin(phase_angle) * table_scale).astype(jnp.bfloat16)
-    return (cos_table, sin_table)
+    cos_table = ((ca * cb - sa * sb) * table_scale).astype(jnp.bfloat16)
+    sin_table = ((sa * cb + ca * sb) * table_scale).astype(jnp.bfloat16)
+    slots = channel_of.shape[0]
+    return (cos_table.reshape(slots, points), sin_table.reshape(slots, points))
 
 
 def make_weights(beam_stations, beam_codes, stations):
@@ -49,10 +61,14 @@
 
 def spectrum(filtered, cos_table, sin_table, slot_gain):
     inputs_here, spectra, points = (filtered.shape[1], filtered.shape[2], filtered.shape[3])
-    real_rows = filtered[0].reshape(inputs_here * spectra, points)
-    imag_rows = filtered[1].reshape(inputs_here * spectra, points)
-    spec_re = contract(cos_table, real_rows) + contract(sin_table, imag_rows)
-    spec_im = contract(cos_table, imag_rows) - contract(sin_table, real_rows)
+    rows = inputs_here * spectra
+    slots = cos_table.shape[0]
+    tables = jnp.concatenate([cos_table, sin_table], axis=0)
+    products = contract(tables, filtered.reshape(2 * rows, points))
+    cos_re, cos_im = products[:slots, :rows], products[:slots, rows:]
+    sin_re, sin_im = products[slots:, :rows], products[slots:, rows:]
+    spec_re = cos_re + sin_im
+    spec_im = cos_im - sin_re
     combined = jnp.concatenate(
         [spec_re.reshape(-1, inputs_here, spectra), spec_im.reshape(-1, inputs_here, spectra)],
         axis=2,
@@ -74,21 +90,21 @@
     voltages, fir_taps, cor_channels, beam_channels, cor_gain, beam_gain, beam_stations, beam_codes
 ):
     tap_count, points = fir_taps.shape
-    stn_count = lax.axis_size("stn")
-    sec_count = lax.axis_size("sec")
+    stn_count = lax.axis_size(STN_AXES)
+    sec_count = lax.axis_size("x")
     device_count = stn_count * sec_count
     inputs_here = voltages.shape[1]
     spectra = voltages.shape[2] // points - tap_count + 1
     filtered = polyphase(voltages, fir_taps, spectra)
     channel_of = jnp.concatenate([cor_channels, beam_channels])
     slot_gain = jnp.concatenate([cor_gain, beam_gain])
-    cos_table, sin_table = make_tables(channel_of, points)
+    cos_table, sin_table = lax.optimization_barrier(make_tables(channel_of, points))
     weight_re, weight_im = make_weights(beam_stations, beam_codes, STATIONS)
     spectra_all = spectrum(filtered, cos_table, sin_table, slot_gain)
     outgoing = spectra_all.reshape(2, stn_count, sec_count, 1, 1, inputs_here, 2 * spectra)
     turned = lax.all_to_all(
-        lax.all_to_all(outgoing, "stn", split_axis=1, concat_axis=3, tiled=True),
-        "sec",
+        lax.all_to_all(outgoing, STN_AXES, split_axis=1, concat_axis=3, tiled=True),
+        "x",
         split_axis=2,
         concat_axis=4,
         tiled=True,
@@ -102,15 +118,24 @@
     visibilities = jnp.stack([vis_re, vis_im])[None].astype(jnp.bfloat16)
     raw_beams = form_beams(beam_data, weight_re, weight_im)
     local_power = jnp.sum(raw_beams * raw_beams, axis=(0, 2, 3))
-    summed_power = lax.psum(local_power, ("stn", "sec"))
+    summed_power = local_power
+    for axis in PHYSICAL_AXES:
+        summed_power = lax.psum(summed_power, axis)
     beam_power = summed_power / (device_count * raw_beams.shape[2] * raw_beams.shape[3])
     beams = (raw_beams * lax.rsqrt(beam_power + epsilon)[None, :, None, None]).astype(jnp.bfloat16)
     return (visibilities, beams)
 
 
 def solution(mesh):
-    in_specs = (P(None, ("stn", "sec"), None), P(), P(), P(), P(), P(), P(), P())
-    out_specs = (P(("stn", "sec"), None, None, None), P(("stn", "sec"), None, None, None))
+    stn_count, sec_count = mesh.devices.shape
+    cores = 2
+    y_count = 4
+    z_count = stn_count // (y_count * cores)
+    devices = mesh.devices.reshape(y_count, z_count, cores, sec_count)
+    fine = jax.sharding.Mesh(devices, ("y", "z", "core", "x"))
+    spread = ("y", "z", "core", "x")
+    in_specs = (P(None, spread, None), P(), P(), P(), P(), P(), P(), P())
+    out_specs = (P(spread, None, None, None), P(spread, None, None, None))
     return jax.shard_map(
-        per_device, mesh=mesh, in_specs=in_specs, out_specs=out_specs, check_vma=False
+        per_device, mesh=fine, in_specs=in_specs, out_specs=out_specs, check_vma=False
     )

time: 352 us -> 201 us (0.57); the launches traced: 347 us -> 200 us
  matrix products: 139 us -> 23.1 us
  blocking collectives: 114 us -> 77.1 us
  other arithmetic: 56.1 us -> 63.6 us
    dot_general x6 -> x3, matrix products: 132 us -> 16.3 us  [contract(): lax.dot_general(left_rows, right_rows, contract_dims, preferred_element_t...]
    psum x1 -> x4, blocking collectives: 73.8 us -> 37 us  [per_device(): summed_power = lax.psum(summed_power, axis)]
    convert_element_type x0 -> x1, other arithmetic: none -> 5.33 us  [make_tables(): sin_table = ((sa * cb + ca * sb) * table_scale).astype(jnp.bfloat16)]
    slice x1 -> x0, local copies, waits for them, and re-layouts: 3.97 us -> none  [spectrum(): real_rows = filtered[0].reshape(inputs_here * spectra, points)]
  transfers between devices with their start and end apart: 1 -> 1, of which waited for: 1 -> 1; matrix products, arithmetic and copies ran while one was open for 2% -> 3% of each run, Pallas kernels for 0% -> 0%
where the time goes in v1:
time: 201 us; the launch traced here: 200 us
  blocking collectives  77.1 us (38%)
  other arithmetic  63.6 us (32%)
  local copies, waits for them, and re-layouts  23.1 us (11%)
  matrix products  23.1 us (11%)
  waiting for transfers between devices  7.63 us (4%)
  starting transfers between devices  4.82 us (2%)
    convert_element_type x1, other arithmetic, polyphase(): return summed.astype(jnp.bfloat16)  52.5 us
    all_to_all x1, blocking collectives, per_device(): lax.all_to_all(outgoing, STN_AXES, split_axis=1, concat_axis=3, tiled=True)  40.1 us
    psum x4, blocking collectives, per_device(): summed_power = lax.psum(summed_power, axis)  37 us
    dot_general x3, matrix products, contract(): lax.dot_general(left_rows, right_rows, contract_dims, preferred_element_t...  16.3 us
    reshape x1, local copies, waits for them, and re-layouts, polyphase(): framed = in_block.reshape(in_block.shape[0], in_block.shape[1], -1, points)  14.5 us
    all_to_all x1, waiting for transfers between devices, per_device(): lax.all_to_all(lax.all_to_all(outgoing, STN_AXES, split_axis=1, concat_ax...  7.63 us
    convert_element_type x1, other arithmetic, make_tables(): sin_table = ((sa * cb + ca * sb) * table_scale).astype(jnp.bfloat16)  5.33 us
    all_to_all x1, starting transfers between devices, per_device(): lax.all_to_all(lax.all_to_all(outgoing, STN_AXES, split_axis=1, concat_ax...  4.82 us
  transfers between devices with their start and end apart: 1, of which 1 were waited for; matrix products, arithmetic and copies ran while one was open for 3% of the time, Pallas kernels for 0%

profile of v1, /device:TPU:2, one launch (start us, length us, event | category | flops | bytes accessed | tf_op | source)
XLA Modules:
  0.0 200.2 jit_solution(11601812369316442316)
XLA Ops:
  0.6 2.1 %fusion.48 = (f32[1,4096]{1,0:T(1,128)S(1)}, f32[1,4096]{1,0:T(1,128)S(1)}, f32[1,4096]{1,0:T(1,128)S(1)}, f32[1,4096]{1,0:T(1,128)S(1)}, f32[1,4096]{1,0:T(1,12...) fusion(f32[12,4096]{1,0:T(8,128)} %param.9), kind=kLoop, calls=%fused_computation.84 | loop fusion | bytes 393216 | tf_op jit(solution)/shard_map/slice | solution.py:51
  2.8 0.0 copy-start.3
  2.8 0.0 copy-start.4
  2.8 14.5 %reshape.296 = bf16[2,4,139,4096]{3,2,1,0:T(8,128)(2,1)} reshape(bf16[2,4,569344]{2,1,0:T(4,128)(2,1)} %param.8) | data formatting | bytes 18219008 | tf_op jit(solution)/shard_map/reshape | solution.py:48
  17.3 0.0 copy-done.3
  17.3 0.0 copy-done.4
  17.3 1.0 fusion.31
  18.3 5.3 %multiply_convert_fusion = (bf16[512,64,64]{0,2,1:T(8,128)(2,1)}, bf16[512,64,64]{0,2,1:T(8,128)(2,1)}) fusion(f32[512,64]{0,1:T(8,128)S(1)} %get-tuple-element.42, f32[512,64]{0,1:T(8,128)S(1)} %get-tuple-element.41, f32[512,64]{0,1:T(8,128)S(1)} %get-tuple-element.43, f32[512,64]{0,1:T(8,128)S(1)} %get-tuple-element.40), kind=kLoop, calls=%fused_computation.10 | loop fusion | flops 20971520 | bytes 8912896 | tf_op jit(solution)/shard_map/convert_element_type | solution.py:31
  23.6 52.5 %add_convert_fusion = bf16[2,4,128,4096]{3,2,1,0:T(8,128)(2,1)} fusion(bf16[2,4,139,4096]{3,2,1,0:T(8,128)(2,1)} %reshape.296, f32[4096]{0:T(1024)S(1)} %bitcast.78, f32[4096]{0:T(1024)S(1)} %bitcast.79, f32[4096]{0:T(1024)S(1)} %bitcast.69, f32[4096]{0:T(1024)S(1)} %bitcast.70, f32[4096]{0:T(1024)S(1)} %bitcast.71, f32[4096]{0:T(1024)S(1)} %bitcast.72, ...), kind=kLoop, calls=%fused_computation.3 | loop fusion | flops 150994944 | bytes 109248512 | tf_op jit(solution)/shard_map/convert_element_type | solution.py:54
  76.1 13.9 %fusion.2 = f32[1024,1024]{1,0:T(8,128)S(1)} fusion(bf16[1024,4096]{1,0:T(8,128)(2,1)} %bitcast.63, bf16[512,4096]{0,1:T(8,128)(2,1)} %bitcast.64, bf16[512,4096]{0,1:T(8,128)(2,1)} %bitcast.65), kind=kOutput, calls=%fused_computation.4 | convolution fusion | flops 8606711808 | bytes 20971520 | tf_op jit(solution)/shard_map/dot_general | solution.py:59
  90.0 0.0 copy-start.1
  90.1 0.0 copy-start.2
  90.1 0.5 slice_add_fusion
  90.6 0.0 copy-start
  90.6 0.0 copy-start.5
  90.6 0.4 concatenate.60
  91.0 0.4 concatenate.61
  91.3 0.0 copy-done.1
  91.3 0.1 concatenate.63
  91.4 0.0 copy-done.2
  91.4 0.1 concatenate.64
  91.6 0.1 copy.37
  91.6 0.7 fusion.8
  92.4 40.1 %all_to_all.33 = bf16[2,64,4,1,1,4,256]{6,5,2,0,4,3,1:T(4,128)(2,1)S(1)} all-to-all(bf16[2,64,4,1,1,4,256]{6,5,2,0,4,3,1:T(4,128)(2,1)S(1)} %fusion.8), channel_id=1, replica_groups=mesh['y'=4,'z'=8,'core'=2,'x'=4] {'y','z','core'}, dimensions={1} | all-to-all | bytes 2097152 | tf_op jit(solution)/shard_map/all_to_all | solution.py:106
  132.5 1.4 copy.38
  133.9 4.8 %all-to-all-start.1 = ((bf16[2,1,4,64,1,4,256]{6,5,3,0,4,1,2:T(4,128)(2,1)}), bf16[2,1,4,64,1,4,256]{6,5,3,0,4,1,2:T(4,128)(2,1)S(1)}, u32[]{:S(2)}, u32[]{:S(2)}) async-start(bf16[2,1,4,64,1,4,256]{6,5,3,0,4,1,2:T(4,128)(2,1)} %copy.38), calls=%async_computation.1 | async-start | bytes 2097152 | tf_op jit(solution)/shard_map/all_to_all | solution.py:105
  138.7 0.0 copy-done
  138.7 0.2 multiply_bitcast_fusion.1
  138.8 0.0 copy-done.5
  138.9 3.2 %fusion = bf16[16,1,512]{2,1,0:T(2,128)(2,1)S(1)} fusion(s32[16,512]{1,0:T(8,128)S(1)} %copy-done.5, bf16[16,512,1]{1,0,2:T(8,128)(2,1)S(1)} %get-tuple-element.39), kind=kOutput, calls=%fused_computation.1 | convolution fusion | flops 12582912 | bytes 65536 | tf_op jit(solution)/shard_map/bk,bks->bs/dot_general | solution.py:42
  142.1 3.2 %fusion.1 = bf16[16,1,512]{2,1,0:T(2,128)(2,1)S(1)} fusion(s32[16,512]{1,0:T(8,128)S(1)} %copy-done.5, bf16[16,512,1]{1,0,2:T(8,128)(2,1)S(1)} %get-tuple-element.38), kind=kOutput, calls=%fused_computation.2 | convolution fusion | flops 12582912 | bytes 65536 | tf_op jit(solution)/shard_map/bk,bks->bs/dot_general | solution.py:41
  145.3 7.6 %all-to-all-done.1 = bf16[2,1,4,64,1,4,256]{6,5,3,0,4,1,2:T(4,128)(2,1)S(1)} async-done(((bf16[2,1,4,64,1,4,256]{6,5,3,0,4,1,2:T(4,128)(2,1)}), bf16[2,1,4,64,1,4,256]{6,5,3,0,4,1,2:T(4,128)(2,1)S(1)}, u32[]{:S(2)}, u32[]{:S(2)}) %all-to-all-start.1) | async-done | bytes 1048608 | tf_op jit(solution)/shard_map/all_to_all | solution.py:105
  152.9 0.4 fusion.46
  153.3 0.2 copy.39
  153.5 0.1 squeeze.3
  153.6 0.8 fusion.47
  154.4 0.7 fusion.9
  155.1 1.0 copy.40
  156.1 1.8 reshape.298
  157.9 0.2 convolution_bitcast_fusion
  158.1 0.2 convolution_bitcast_fusion.1
  158.3 0.1 multiply_reduce_fusion
  158.4 2.5 %psum.28 = f32[16]{0:T(128)S(1)} all-reduce(f32[16]{0:T(128)S(1)} %multiply_reduce_fusion), channel_id=1, replica_groups=mesh['y'=4,'z'=8,'core'=2,'x'=4] {'core'}, use_global_device_ids=true, to_apply=%region_1.2 | all-reduce | flops 16 | bytes 128 | tf_op jit(solution)/shard_map/psum | solution.py:123
  160.9 9.2 %psum.29 = f32[16]{0:T(128)S(1)} all-reduce(f32[16]{0:T(128)S(1)} %psum.28), channel_id=1, replica_groups=mesh['y'=4,'z'=8,'core'=2,'x'=4] {'x'}, use_global_device_ids=true, to_apply=%region_2.3 | all-reduce | flops 16 | bytes 128 | tf_op jit(solution)/shard_map/psum | solution.py:123
  170.0 9.5 %psum.30 = f32[16]{0:T(128)S(1)} all-reduce(f32[16]{0:T(128)S(1)} %psum.29), channel_id=1, replica_groups=mesh['y'=4,'z'=8,'core'=2,'x'=4] {'y'}, use_global_device_ids=true, to_apply=%region_3.4 | all-reduce | flops 16 | bytes 128 | tf_op jit(solution)/shard_map/psum | solution.py:123
  179.5 15.9 %psum.31 = f32[16]{0:T(128)S(1)} all-reduce(f32[16]{0:T(128)S(1)} %psum.30), channel_id=1, replica_groups=mesh['y'=4,'z'=8,'core'=2,'x'=4] {'z'}, use_global_device_ids=true, to_apply=%region_4.5 | all-reduce | flops 16 | bytes 128 | tf_op jit(solution)/shard_map/psum | solution.py:123
  195.4 0.1 multiply_convert_fusion.4
  195.5 0.6 copy.43
  196.1 1.7 fusion.10
  197.8 2.4 %pad_maximum_fusion = bf16[1,2,1024,1024]{3,2,1,0:T(8,128)(2,1)} fusion(bf16[1,1,1024,1024]{3,2,1,0:T(8,128)(2,1)S(1)} %fusion.10, bf16[1,1,1024,1024]{3,2,1,0:T(8,128)(2,1)S(1)} %fusion.9), kind=kLoop, calls=%fused_computation.12 | loop fusion | flops 2097152 | bytes 8388608 | tf_op jit(solution)/shard_map/stack | solution.py:118
  (4 shorter events, 0.0 us)
Async XLA Ops:
  2.8 14.5 %copy-start.3 = (s32[256]{0:T(256)S(1)}, s32[256]{0:T(256)}, u32[]{:S(2)}) copy-start(s32[256]{0:T(256)} %param.11) | copy-start | bytes 3076
  2.8 14.5 %copy-start.4 = (s32[256]{0:T(256)S(1)}, s32[256]{0:T(256)}, u32[]{:S(2)}) copy-start(s32[256]{0:T(256)} %param.10) | copy-start | bytes 3076
  90.0 1.3 copy-start.1
  90.1 1.4 copy-start.2
  90.6 48.1 %copy-start = (s32[16,512]{1,0:T(8,128)S(1)}, s32[16,512]{1,0:T(8,128)}, u32[]{:S(2)}) copy-start(s32[16,512]{1,0:T(8,128)} %param.15) | copy-start | bytes 98308
  90.6 48.3 %copy-start.5 = (s32[16,512]{1,0:T(8,128)S(1)}, s32[16,512]{1,0:T(8,128)}, u32[]{:S(2)}) copy-start(s32[16,512]{1,0:T(8,128)} %param.14) | copy-start | bytes 98308
  133.9 19.1 %all-to-all-start.1 = ((bf16[2,1,4,64,1,4,256]{6,5,3,0,4,1,2:T(4,128)(2,1)}), bf16[2,1,4,64,1,4,256]{6,5,3,0,4,1,2:T(4,128)(2,1)S(1)}, u32[]{:S(2)}, u32[]{:S(2)}) async-start(bf16[2,1,4,64,1,4,256]{6,5,3,0,4,1,2:T(4,128)(2,1)} %copy.38), calls=%async_computation.1 | async-start | bytes 2097152 | tf_op jit(solution)/shard_map/all_to_all | solution.py:105

commit v2 on v1

--- a/solution.py
+++ b/solution.py
@@ -3,6 +3,7 @@
 import jax
 import jax.numpy as jnp
 from jax import lax
+from jax.experimental import pallas as pl
 from jax.sharding import PartitionSpec as P
 
 STATIONS = 512
@@ -43,15 +44,46 @@
     return (weight_re.astype(jnp.bfloat16), weight_im.astype(jnp.bfloat16))
 
 
+def fir_kernel(x_ref, h_ref, o_ref):
+    tap_count = h_ref.shape[0]
+    rows = x_ref.shape[1]
+    width = h_ref.shape[1]
+    taps = [jnp.broadcast_to(h_ref[pl.ds(t, 1), :], (rows, width)) for t in range(tap_count)]
+
+    def body(j, carry):
+        first = 2 * j
+        frames = [x_ref[first + f] for f in range(tap_count + 1)]
+        pair = []
+        for k in range(2):
+            acc = taps[0] * frames[k]
+            for t in range(1, tap_count):
+                acc = acc + taps[t] * frames[k + t]
+            pair.append(acc)
+        o_ref[j] = jnp.concatenate(pair, axis=0).astype(o_ref.dtype)
+        return carry
+
+    lax.fori_loop(0, o_ref.shape[0], body, 0)
+
+
 def polyphase(in_block, fir_taps, spectra):
     tap_count, points = fir_taps.shape
-    framed = in_block.reshape(in_block.shape[0], in_block.shape[1], -1, points)
-    summed = jnp.zeros((framed.shape[0], framed.shape[1], spectra, points), jnp.float32)
-    for tap_index in range(tap_count):
-        summed = summed + fir_taps[tap_index] * framed[
-            :, :, tap_index : tap_index + spectra, :
-        ].astype(jnp.float32)
-    return summed.astype(jnp.bfloat16)
+    components, inputs_here = in_block.shape[0], in_block.shape[1]
+    rows = components * inputs_here
+    frames = in_block.shape[2] // points
+    framed = in_block.reshape(components, inputs_here, frames, points)
+    framed = jnp.transpose(framed, (2, 0, 1, 3)).reshape(frames, rows, points)
+    framed = framed.astype(jnp.float32)
+    width = 256
+    return pl.pallas_call(
+        fir_kernel,
+        grid=(points // width,),
+        in_specs=[
+            pl.BlockSpec((frames, rows, width), lambda n: (0, 0, n)),
+            pl.BlockSpec((tap_count, width), lambda n: (0, n)),
+        ],
+        out_specs=pl.BlockSpec((spectra // 2, 2 * rows, width), lambda n: (0, 0, n)),
+        out_shape=jax.ShapeDtypeStruct((spectra // 2, 2 * rows, points), jnp.bfloat16),
+    )(framed, fir_taps)
 
 
 def contract(left_rows, right_rows):
@@ -59,20 +91,18 @@
     return lax.dot_general(left_rows, right_rows, contract_dims, preferred_element_type=jnp.float32)
 
 
-def spectrum(filtered, cos_table, sin_table, slot_gain):
-    inputs_here, spectra, points = (filtered.shape[1], filtered.shape[2], filtered.shape[3])
-    rows = inputs_here * spectra
+def spectrum(filtered, cos_table, sin_table, slot_gain, inputs_here):
+    points = filtered.shape[2]
+    spectra = 2 * filtered.shape[0]
     slots = cos_table.shape[0]
     tables = jnp.concatenate([cos_table, sin_table], axis=0)
-    products = contract(tables, filtered.reshape(2 * rows, points))
-    cos_re, cos_im = products[:slots, :rows], products[:slots, rows:]
-    sin_re, sin_im = products[slots:, :rows], products[slots:, rows:]
-    spec_re = cos_re + sin_im
-    spec_im = cos_im - sin_re
-    combined = jnp.concatenate(
-        [spec_re.reshape(-1, inputs_here, spectra), spec_im.reshape(-1, inputs_here, spectra)],
-        axis=2,
-    )
+    products = contract(tables, filtered.reshape(-1, points))
+    products = products.reshape(2, slots, spectra, 2, inputs_here)
+    cos_re, cos_im = products[0, :, :, 0], products[0, :, :, 1]
+    sin_re, sin_im = products[1, :, :, 0], products[1, :, :, 1]
+    spec_re = jnp.transpose(cos_re + sin_im, (0, 2, 1))
+    spec_im = jnp.transpose(cos_im - sin_re, (0, 2, 1))
+    combined = jnp.concatenate([spec_re, spec_im], axis=2)
     return (combined * slot_gain[:, None, None]).astype(jnp.bfloat16)
 
 
@@ -100,7 +130,7 @@
     slot_gain = jnp.concatenate([cor_gain, beam_gain])
     cos_table, sin_table = lax.optimization_barrier(make_tables(channel_of, points))
     weight_re, weight_im = make_weights(beam_stations, beam_codes, STATIONS)
-    spectra_all = spectrum(filtered, cos_table, sin_table, slot_gain)
+    spectra_all = spectrum(filtered, cos_table, sin_table, slot_gain, inputs_here)
     outgoing = spectra_all.reshape(2, stn_count, sec_count, 1, 1, inputs_here, 2 * spectra)
     turned = lax.all_to_all(
         lax.all_to_all(outgoing, STN_AXES, split_axis=1, concat_axis=3, tiled=True),

time: 201 us -> 232 us (1.15)
  local copies, waits for them, and re-layouts: 23.1 us -> 67.8 us
  other arithmetic: 63.6 us -> 19.4 us
  Pallas kernels: 0 us -> 23.5 us
  matrix products: 23.1 us -> 29.7 us
    convert_element_type x1 -> x0, other arithmetic: 52.5 us -> none  [polyphase(): return summed.astype(jnp.bfloat16)]
    convert_element_type x0 -> x2, local copies, waits for them, and re-layouts: none -> 35.7 us  [polyphase(): framed = framed.astype(jnp.float32)]
    pallas_call x0 -> x1, Pallas kernels: none -> 23.5 us  [polyphase(): pl.pallas_call(fir_kernel, grid=(points // width,), in_specs=[pl.BlockSpe...]
    reshape x1 -> x0, local copies, waits for them, and re-layouts: 14.5 us -> none  [polyphase(): framed = in_block.reshape(in_block.shape[0], in_block.shape[1], -1, points)]
    dot_general x0 -> x1, local copies, waits for them, and re-layouts: none -> 13.1 us  [contract(): lax.dot_general(left_rows, right_rows, contract_dims, preferred_element_t...]
    concatenate x2 -> x3, local copies, waits for them, and re-layouts: 0.72 us -> 13.4 us  [the longest x1 12 us: spectrum(): tables = jnp.concatenate([cos_table, sin_table], axis=0)]
    concatenate x0 -> x1, other arithmetic: none -> 7.86 us  [spectrum(): tables = jnp.concatenate([cos_table, sin_table], axis=0)]
    dot_general x3, matrix products: 16.3 us -> 22.9 us  [contract(): lax.dot_general(left_rows, right_rows, contract_dims, preferred_element_t...]
where the time goes in v2:
time: 232 us; the launch traced here: 231 us
  blocking collectives  77.1 us (33%)
  local copies, waits for them, and re-layouts  67.8 us (29%)
  matrix products  29.7 us (13%)
  Pallas kernels  23.5 us (10%)
  other arithmetic  19.4 us (8%)
  waiting for transfers between devices  7.63 us (3%)
  starting transfers between devices  4.83 us (2%)
    all_to_all x1, blocking collectives, per_device(): lax.all_to_all(outgoing, STN_AXES, split_axis=1, concat_axis=3, tiled=True)  40.1 us
    psum x4, blocking collectives, per_device(): summed_power = lax.psum(summed_power, axis)  37 us
    convert_element_type x2, local copies, waits for them, and re-layouts, polyphase(): framed = framed.astype(jnp.float32)  35.7 us
    pallas_call x1, Pallas kernels, polyphase(): pl.pallas_call(fir_kernel, grid=(points // width,), in_specs=[pl.BlockSpe...  23.5 us
    dot_general x3, matrix products, contract(): lax.dot_general(left_rows, right_rows, contract_dims, preferred_element_t...  22.9 us
    dot_general x1, local copies, waits for them, and re-layouts, contract(): lax.dot_general(left_rows, right_rows, contract_dims, preferred_element_t...  13.1 us
    concatenate x1, local copies, waits for them, and re-layouts, spectrum(): tables = jnp.concatenate([cos_table, sin_table], axis=0)  12 us
    concatenate x1, other arithmetic, spectrum(): tables = jnp.concatenate([cos_table, sin_table], axis=0)  7.86 us
  transfers between devices with their start and end apart: 1, of which 1 were waited for; matrix products, arithmetic and copies ran while one was open for 3% of the time, Pallas kernels for 0%

profile of v2, /device:TPU:2, one launch (start us, length us, event | category | flops | bytes accessed | tf_op | source)
XLA Modules:
  0.0 230.8 jit_solution(9835316369217823819)
XLA Ops:
  0.6 0.7 pad_add_fusion
  1.3 1.0 fusion.30
  2.4 5.3 %multiply_convert_fusion = (bf16[512,64,64]{0,2,1:T(8,128)(2,1)}, bf16[512,64,64]{0,2,1:T(8,128)(2,1)}) fusion(f32[512,64]{0,1:T(8,128)S(1)} %get-tuple-element.28, f32[512,64]{0,1:T(8,128)S(1)} %get-tuple-element.27, f32[512,64]{0,1:T(8,128)S(1)} %get-tuple-element.29, f32[512,64]{0,1:T(8,128)S(1)} %get-tuple-element.26), kind=kLoop, calls=%fused_computation.9 | loop fusion | flops 20971520 | bytes 8912896 | tf_op jit(solution)/shard_map/convert_element_type | solution.py:32
  7.7 7.9 %pad_maximum_fusion = bf16[1024,4096]{0,1:T(8,128)(2,1)} fusion(bf16[512,4096]{0,1:T(8,128)(2,1)} %bitcast.72, bf16[512,4096]{0,1:T(8,128)(2,1)} %bitcast.73), kind=kLoop, calls=%fused_computation.3 | loop fusion | flops 16777216 | bytes 16777216 | tf_op jit(solution)/shard_map/concatenate | solution.py:98
  15.5 12.0 %copy.35 = bf16[1024,4096]{1,0:T(8,128)(2,1)} copy(bf16[1024,4096]{0,1:T(8,128)(2,1)} %pad_maximum_fusion) | data formatting | bytes 16777216 | tf_op jit(solution)/shard_map/concatenate | solution.py:98
  27.5 16.6 %reshape.289 = f32[2,4,139,4096]{3,2,1,0:T(8,128)} reshape(bf16[2,4,569344]{2,1,0:T(4,128)(2,1)} %param.8) | data formatting | bytes 27328512 | tf_op jit(solution)/shard_map/convert_element_type | solution.py:75
  44.1 19.1 %copy.52.x_ref = f32[139,8,4096]{2,1,0:T(8,128)} copy(f32[139,8,4096]{2,0,1:T(8,128)} %bitcast.71) | data formatting | bytes 36438016 | tf_op jit(solution)/shard_map/convert_element_type | solution.py:75
  63.2 23.5 %shard_map.95 = bf16[64,16,4096]{2,1,0:T(8,128)(2,1)} custom-call(f32[139,8,4096]{2,1,0:T(8,128)} %copy.52.x_ref, f32[12,4096]{1,0:T(8,128)} %h_ref.1), custom_call_target="tpu_custom_call" | custom-call | tf_op jit(solution)/shard_map/pallas_call | solution.py:77
  86.7 13.1 %dot_general.30 = bf16[128,2,4,4096]{3,2,1,0:T(4,128)(2,1)} reshape(bf16[64,16,4096]{2,1,0:T(8,128)(2,1)} %shard_map.95) | data formatting | bytes 16777216 | tf_op jit(solution)/shard_map/dot_general | solution.py:91
  99.8 20.5 %fusion.2 = f32[2,512,128,2,4]{2,1,4,3,0:T(8,128)S(1)} fusion(bf16[2,512,4096,1,1]{2,1,4,3,0:T(8,128)(2,1)} %bitcast.74, bf16[128,2,4,4096]{3,2,1,0:T(4,128)(2,1)} %dot_general.30), kind=kOutput, calls=%fused_computation.4 | convolution fusion | flops 8589934592 | bytes 20971520 | tf_op jit(solution)/shard_map/dot_general | solution.py:91
  120.3 0.0 copy-start.1
  120.3 0.0 copy-start.2
  120.3 0.2 slice_add_fusion
  120.5 0.0 copy-start
  120.5 0.0 copy-start.3
  120.5 0.7 copy.38
  121.2 0.7 copy.39
  121.9 0.0 copy-done.1
  121.9 0.1 concatenate.63
  122.0 0.0 copy-done.2
  122.0 0.1 concatenate.64
  122.1 0.1 copy.40
  122.2 0.8 fusion.7
  123.0 40.1 %all_to_all.33 = bf16[2,64,4,1,1,4,256]{6,5,2,0,4,3,1:T(4,128)(2,1)S(1)} all-to-all(bf16[2,64,4,1,1,4,256]{6,5,2,0,4,3,1:T(4,128)(2,1)S(1)} %fusion.7), channel_id=1, replica_groups=mesh['y'=4,'z'=8,'core'=2,'x'=4] {'y','z','core'}, dimensions={1} | all-to-all | bytes 2097152 | tf_op jit(solution)/shard_map/all_to_all | solution.py:136
  163.1 1.4 copy.41
  164.4 4.8 %all-to-all-start.1 = ((bf16[2,1,4,64,1,4,256]{6,5,3,0,4,1,2:T(4,128)(2,1)}), bf16[2,1,4,64,1,4,256]{6,5,3,0,4,1,2:T(4,128)(2,1)S(1)}, u32[]{:S(2)}, u32[]{:S(2)}) async-start(bf16[2,1,4,64,1,4,256]{6,5,3,0,4,1,2:T(4,128)(2,1)} %copy.41), calls=%async_computation.1 | async-start | bytes 2097152 | tf_op jit(solution)/shard_map/all_to_all | solution.py:135
  169.3 0.0 copy-done
  169.3 0.2 multiply_bitcast_fusion.1
  169.4 0.0 copy-done.3
  169.4 3.2 %fusion = bf16[16,1,512]{2,1,0:T(2,128)(2,1)S(1)} fusion(s32[16,512]{1,0:T(8,128)S(1)} %copy-done.3, bf16[16,512,1]{1,0,2:T(8,128)(2,1)S(1)} %get-tuple-element.25), kind=kOutput, calls=%fused_computation.1 | convolution fusion | flops 12582912 | bytes 65536 | tf_op jit(solution)/shard_map/bk,bks->bs/dot_general | solution.py:43
  172.7 3.2 %fusion.1 = bf16[16,1,512]{2,1,0:T(2,128)(2,1)S(1)} fusion(s32[16,512]{1,0:T(8,128)S(1)} %copy-done.3, bf16[16,512,1]{1,0,2:T(8,128)(2,1)S(1)} %get-tuple-element.24), kind=kOutput, calls=%fused_computation.2 | convolution fusion | flops 12582912 | bytes 65536 | tf_op jit(solution)/shard_map/bk,bks->bs/dot_general | solution.py:42
  175.9 7.6 %all-to-all-done.1 = bf16[2,1,4,64,1,4,256]{6,5,3,0,4,1,2:T(4,128)(2,1)S(1)} async-done(((bf16[2,1,4,64,1,4,256]{6,5,3,0,4,1,2:T(4,128)(2,1)}), bf16[2,1,4,64,1,4,256]{6,5,3,0,4,1,2:T(4,128)(2,1)S(1)}, u32[]{:S(2)}, u32[]{:S(2)}) %all-to-all-start.1) | async-done | bytes 1048608 | tf_op jit(solution)/shard_map/all_to_all | solution.py:135
  183.5 0.4 fusion.44
  183.9 0.2 copy.42
  184.1 0.1 squeeze.2
  184.2 0.8 fusion.45
  185.0 0.7 fusion.8
  185.7 1.0 copy.43
  186.7 1.8 reshape.287
  188.5 0.2 convolution_bitcast_fusion
  188.7 0.2 convolution_bitcast_fusion.1
  188.9 0.1 multiply_reduce_fusion
  189.0 2.5 %psum.28 = f32[16]{0:T(128)S(1)} all-reduce(f32[16]{0:T(128)S(1)} %multiply_reduce_fusion), channel_id=1, replica_groups=mesh['y'=4,'z'=8,'core'=2,'x'=4] {'core'}, use_global_device_ids=true, to_apply=%region_1.2 | all-reduce | flops 16 | bytes 128 | tf_op jit(solution)/shard_map/psum | solution.py:153
  191.5 9.1 %psum.29 = f32[16]{0:T(128)S(1)} all-reduce(f32[16]{0:T(128)S(1)} %psum.28), channel_id=1, replica_groups=mesh['y'=4,'z'=8,'core'=2,'x'=4] {'x'}, use_global_device_ids=true, to_apply=%region_2.3 | all-reduce | flops 16 | bytes 128 | tf_op jit(solution)/shard_map/psum | solution.py:153
  200.6 9.5 %psum.30 = f32[16]{0:T(128)S(1)} all-reduce(f32[16]{0:T(128)S(1)} %psum.29), channel_id=1, replica_groups=mesh['y'=4,'z'=8,'core'=2,'x'=4] {'y'}, use_global_device_ids=true, to_apply=%region_3.4 | all-reduce | flops 16 | bytes 128 | tf_op jit(solution)/shard_map/psum | solution.py:153
  210.1 15.9 %psum.31 = f32[16]{0:T(128)S(1)} all-reduce(f32[16]{0:T(128)S(1)} %psum.30), channel_id=1, replica_groups=mesh['y'=4,'z'=8,'core'=2,'x'=4] {'z'}, use_global_device_ids=true, to_apply=%region_4.5 | all-reduce | flops 16 | bytes 128 | tf_op jit(solution)/shard_map/psum | solution.py:153
  226.0 0.1 multiply_convert_fusion.4
  226.1 0.6 copy.46
  226.7 1.7 fusion.9
  228.4 2.4 %pad_maximum_fusion.1 = bf16[1,2,1024,1024]{3,2,1,0:T(8,128)(2,1)} fusion(bf16[1,1,1024,1024]{3,2,1,0:T(8,128)(2,1)S(1)} %fusion.9, bf16[1,1,1024,1024]{3,2,1,0:T(8,128)(2,1)S(1)} %fusion.8), kind=kLoop, calls=%fused_computation.11 | loop fusion | flops 2097152 | bytes 8388608 | tf_op jit(solution)/shard_map/stack | solution.py:148
  (3 shorter events, 0.0 us)
Async XLA Ops:
  120.3 1.6 copy-start.1
  120.3 1.7 copy-start.2
  120.5 48.8 %copy-start = (s32[16,512]{1,0:T(8,128)S(1)}, s32[16,512]{1,0:T(8,128)}, u32[]{:S(2)}) copy-start(s32[16,512]{1,0:T(8,128)} %param.15) | copy-start | bytes 98308
  120.5 48.9 %copy-start.3 = (s32[16,512]{1,0:T(8,128)S(1)}, s32[16,512]{1,0:T(8,128)}, u32[]{:S(2)}) copy-start(s32[16,512]{1,0:T(8,128)} %param.14) | copy-start | bytes 98308
  164.4 19.1 %all-to-all-start.1 = ((bf16[2,1,4,64,1,4,256]{6,5,3,0,4,1,2:T(4,128)(2,1)}), bf16[2,1,4,64,1,4,256]{6,5,3,0,4,1,2:T(4,128)(2,1)S(1)}, u32[]{:S(2)}, u32[]{:S(2)}) async-start(bf16[2,1,4,64,1,4,256]{6,5,3,0,4,1,2:T(4,128)(2,1)} %copy.41), calls=%async_computation.1 | async-start | bytes 2097152 | tf_op jit(solution)/shard_map/all_to_all | solution.py:135

commit v3 on v1

--- a/solution.py
+++ b/solution.py
@@ -12,6 +12,7 @@
 
 STN_AXES = ("y", "z", "core")
 PHYSICAL_AXES = ("core", "x", "y", "z")
+POWER_PAD = 65536
 
 
 def make_tables(channel_of, points):
@@ -101,26 +102,30 @@
     cos_table, sin_table = lax.optimization_barrier(make_tables(channel_of, points))
     weight_re, weight_im = make_weights(beam_stations, beam_codes, STATIONS)
     spectra_all = spectrum(filtered, cos_table, sin_table, slot_gain)
-    outgoing = spectra_all.reshape(2, stn_count, sec_count, 1, 1, inputs_here, 2 * spectra)
-    turned = lax.all_to_all(
-        lax.all_to_all(outgoing, STN_AXES, split_axis=1, concat_axis=3, tiled=True),
-        "x",
-        split_axis=2,
-        concat_axis=4,
-        tiled=True,
-    )
-    received = turned.reshape(2, device_count * inputs_here, 2 * spectra)
-    cor_data = received[0]
-    beam_data = received[1:2]
+    slots = spectra_all.shape[0] // 2
+
+    def exchange(part):
+        outgoing = part.reshape(stn_count, sec_count, 1, 1, inputs_here, 2 * spectra)
+        turned = lax.all_to_all(
+            lax.all_to_all(outgoing, STN_AXES, split_axis=0, concat_axis=2, tiled=True),
+            "x",
+            split_axis=1,
+            concat_axis=3,
+            tiled=True,
+        )
+        return turned.reshape(device_count * inputs_here, 2 * spectra)
+
+    beam_data = exchange(spectra_all[slots:])[None]
+    raw_beams = form_beams(beam_data, weight_re, weight_im)
+    local_power = jnp.sum(raw_beams * raw_beams, axis=(0, 2, 3))
+    padded = jnp.zeros((POWER_PAD,), jnp.float32).at[: local_power.shape[0]].set(local_power)
+    padded, cor_part = lax.optimization_barrier((padded, spectra_all[:slots]))
+    summed_power = lax.psum(padded, PHYSICAL_AXES)[: local_power.shape[0]]
+    cor_data = exchange(cor_part)
     swapped = jnp.concatenate([cor_data[:, spectra:], -cor_data[:, :spectra]], axis=1)
     vis_re = contract(cor_data, cor_data) / spectra
     vis_im = contract(swapped, cor_data) / spectra
     visibilities = jnp.stack([vis_re, vis_im])[None].astype(jnp.bfloat16)
-    raw_beams = form_beams(beam_data, weight_re, weight_im)
-    local_power = jnp.sum(raw_beams * raw_beams, axis=(0, 2, 3))
-    summed_power = local_power
-    for axis in PHYSICAL_AXES:
-        summed_power = lax.psum(summed_power, axis)
     beam_power = summed_power / (device_count * raw_beams.shape[2] * raw_beams.shape[3])
     beams = (raw_beams * lax.rsqrt(beam_power + epsilon)[None, :, None, None]).astype(jnp.bfloat16)
     return (visibilities, beams)

time: 201 us -> 423 us (2.10)
  waiting for transfers between devices: 7.63 us -> 270 us
  blocking collectives: 77.1 us -> 0 us
  starting transfers between devices: 4.82 us -> 28 us
  between operations: 0.84 us -> 14.2 us
    psum x0 -> x1, waiting for transfers between devices: none -> 234 us  [per_device(): summed_power = lax.psum(padded, PHYSICAL_AXES)[:local_power.shape[0]]]
    all_to_all x1 -> x0, blocking collectives: 40.1 us -> none  [per_device(): lax.all_to_all(outgoing, STN_AXES, split_axis=1, concat_axis=3, tiled=True)]
    psum x4 -> x0, blocking collectives: 37 us -> none  [per_device(): summed_power = lax.psum(summed_power, axis)]
    all_to_all x1 -> x4, waiting for transfers between devices: 7.63 us -> 35.4 us  [the longest x2 33.5 us: exchange(): lax.all_to_all(outgoing, STN_AXES, split_axis=0, concat_axis=2, tiled=True)]
    all_to_all x1 -> x4, starting transfers between devices: 4.82 us -> 27.9 us  [the longest x2 18.2 us: exchange(): lax.all_to_all(outgoing, STN_AXES, split_axis=0, concat_axis=2, tiled=True)]
  transfers between devices with their start and end apart: 1 -> 5, of which waited for: 1 -> 4; matrix products, arithmetic and copies ran while one was open for 3% -> 2% of each run, Pallas kernels for 0% -> 0%
where the time goes in v3:
time: 423 us; the launch traced here: 422 us
  waiting for transfers between devices  270 us (64%)
  other arithmetic  64.7 us (15%)
  starting transfers between devices  28 us (7%)
  local copies, waits for them, and re-layouts  22.8 us (5%)
  matrix products  22.7 us (5%)
  between operations  14.2 us (3%)
    psum x1, waiting for transfers between devices, per_device(): summed_power = lax.psum(padded, PHYSICAL_AXES)[:local_power.shape[0]]  234 us
    convert_element_type x1, other arithmetic, polyphase(): return summed.astype(jnp.bfloat16)  52.8 us
    all_to_all x2, waiting for transfers between devices, exchange(): lax.all_to_all(outgoing, STN_AXES, split_axis=0, concat_axis=2, tiled=True)  33.5 us
    all_to_all x2, starting transfers between devices, exchange(): lax.all_to_all(outgoing, STN_AXES, split_axis=0, concat_axis=2, tiled=True)  18.2 us
    dot_general x3, matrix products, contract(): lax.dot_general(left_rows, right_rows, contract_dims, preferred_element_t...  15.9 us
    reshape x1, local copies, waits for them, and re-layouts, polyphase(): framed = in_block.reshape(in_block.shape[0], in_block.shape[1], -1, points)  14.5 us
    all_to_all x2, starting transfers between devices, exchange(): lax.all_to_all(lax.all_to_all(outgoing, STN_AXES, split_axis=0, concat_ax...  9.74 us
  transfers between devices with their start and end apart: 5, of which 4 were waited for; matrix products, arithmetic and copies ran while one was open for 2% of the time, Pallas kernels for 0%

profile of v3, /device:TPU:2, one launch (start us, length us, event | category | flops | bytes accessed | tf_op | source)
XLA Modules:
  0.0 422.2 jit_solution(2404482997663256584)
XLA Ops:
  7.2 2.1 fusion.50
  9.3 0.0 copy-start.1
  9.3 0.0 copy-start.2
  9.3 14.5 %reshape.287 = bf16[2,4,139,4096]{3,2,1,0:T(8,128)(2,1)} reshape(bf16[2,4,569344]{2,1,0:T(4,128)(2,1)} %param.10) | data formatting | bytes 18219008 | tf_op jit(solution)/shard_map/reshape | solution.py:49
  23.8 0.0 copy-done.1
  23.8 0.0 copy-done.2
  23.9 1.0 fusion.31
  24.9 5.3 %multiply_convert_fusion = (bf16[512,64,64]{0,2,1:T(8,128)(2,1)}, bf16[512,64,64]{0,2,1:T(8,128)(2,1)}) fusion(f32[512,64]{0,1:T(8,128)S(1)} %get-tuple-element.54, f32[512,64]{0,1:T(8,128)S(1)} %get-tuple-element.53, f32[512,64]{0,1:T(8,128)S(1)} %get-tuple-element.55, f32[512,64]{0,1:T(8,128)S(1)} %get-tuple-element.52), kind=kLoop, calls=%fused_computation.10 | loop fusion | flops 20971520 | bytes 8912896 | tf_op jit(solution)/shard_map/convert_element_type | solution.py:32
  30.2 52.8 %add_convert_fusion = bf16[2,4,128,4096]{3,2,1,0:T(8,128)(2,1)} fusion(bf16[2,4,139,4096]{3,2,1,0:T(8,128)(2,1)} %reshape.287, f32[4096]{0:T(1024)S(1)} %bitcast.98, f32[4096]{0:T(1024)S(1)} %bitcast.99, f32[4096]{0:T(1024)S(1)} %bitcast.89, f32[4096]{0:T(1024)S(1)} %bitcast.90, f32[4096]{0:T(1024)S(1)} %bitcast.91, f32[4096]{0:T(1024)S(1)} %bitcast.92, ...), kind=kLoop, calls=%fused_computation.3 | loop fusion | flops 150994944 | bytes 109248512 | tf_op jit(solution)/shard_map/convert_element_type | solution.py:55
  83.0 14.4 %fusion.2 = f32[1024,1024]{0,1:T(8,128)S(1)} fusion(bf16[1024,4096]{1,0:T(8,128)(2,1)} %bitcast.79, bf16[512,4096]{0,1:T(8,128)(2,1)} %bitcast.80, bf16[512,4096]{0,1:T(8,128)(2,1)} %bitcast.81), kind=kOutput, calls=%fused_computation.4 | convolution fusion | flops 8606711808 | bytes 20971520 | tf_op jit(solution)/shard_map/dot_general | solution.py:60
  97.5 0.0 copy-start.3
  97.5 0.0 copy-start.4
  97.5 0.0 copy-start
  97.5 0.0 copy-start.5
  97.5 0.5 slice_add_fusion
  98.0 0.4 copy.16
  98.4 0.4 copy.17
  98.8 0.0 copy-done.3
  98.8 0.0 copy-done.4
  98.8 1.5 fusion.8
  100.4 1.3 fusion.48
  101.7 12.1 %all-to-all-start = ((bf16[64,4,1,1,4,256]{5,4,1,3,2,0:T(4,128)(2,1)}), bf16[64,4,1,1,4,256]{5,4,1,3,2,0:T(4,128)(2,1)S(1)}, u32[]{:S(2)}, u32[]{:S(2)}) async-start(bf16[64,4,1,1,4,256]{5,4,1,3,2,0:T(4,128)(2,1)} %bitcast.18), calls=%async_computation | async-start | bytes 1048576 | tf_op jit(solution)/shard_map/all_to_all | solution.py:110
  113.8 0.0 copy-done
  113.8 0.2 multiply_bitcast_fusion.1
  114.0 17.0 %all-to-all-done = bf16[64,4,1,1,4,256]{5,4,1,3,2,0:T(4,128)(2,1)S(1)} async-done(((bf16[64,4,1,1,4,256]{5,4,1,3,2,0:T(4,128)(2,1)}), bf16[64,4,1,1,4,256]{5,4,1,3,2,0:T(4,128)(2,1)S(1)}, u32[]{:S(2)}, u32[]{:S(2)}) %all-to-all-start) | async-done | bytes 524320 | tf_op jit(solution)/shard_map/all_to_all | solution.py:110
  131.0 1.0 copy.19
  132.0 4.8 %all-to-all-start.1 = ((bf16[1,4,64,1,4,256]{5,4,2,3,0,1:T(4,128)(2,1)}), bf16[1,4,64,1,4,256]{5,4,2,3,0,1:T(4,128)(2,1)S(1)}, u32[]{:S(2)}, u32[]{:S(2)}) async-start(bf16[1,4,64,1,4,256]{5,4,2,3,0,1:T(4,128)(2,1)} %copy.19), calls=%async_computation.1 | async-start | bytes 1048576 | tf_op jit(solution)/shard_map/all_to_all | solution.py:109
  136.8 0.0 copy-done.5
  136.8 3.2 fusion
  140.0 3.2 fusion.1
  143.3 2.0 all-to-all-done.1
  145.2 0.2 copy.20
  145.4 0.3 reshape.292
  145.7 0.2 convolution_bitcast_fusion
  145.8 0.2 convolution_bitcast_fusion.1
  146.0 0.1 multiply_reduce_fusion
  146.2 0.7 scatter.4
  146.9 6.1 %all-to-all-start.2 = ((bf16[64,4,1,1,4,256]{5,4,1,3,2,0:T(4,128)(2,1)}), bf16[64,4,1,1,4,256]{5,4,1,3,2,0:T(4,128)(2,1)S(1)}, u32[]{:S(2)}, u32[]{:S(2)}) async-start(bf16[64,4,1,1,4,256]{5,4,1,3,2,0:T(4,128)(2,1)} %bitcast.37), calls=%async_computation.2 | async-start | bytes 1048576 | tf_op jit(solution)/shard_map/all_to_all | solution.py:110
  153.0 0.0 all-reduce.3.cloned.1.call-start
  153.0 0.7 all-reduce.3.cloned.1.call-update
  153.7 16.5 %all-to-all-done.2 = bf16[64,4,1,1,4,256]{5,4,1,3,2,0:T(4,128)(2,1)S(1)} async-done(((bf16[64,4,1,1,4,256]{5,4,1,3,2,0:T(4,128)(2,1)}), bf16[64,4,1,1,4,256]{5,4,1,3,2,0:T(4,128)(2,1)S(1)}, u32[]{:S(2)}, u32[]{:S(2)}) %all-to-all-start.2) | async-done | bytes 524320 | tf_op jit(solution)/shard_map/all_to_all | solution.py:110
  170.2 1.0 copy.24
  171.1 4.9 %all-to-all-start.3 = ((bf16[1,4,64,1,4,256]{5,4,2,3,0,1:T(4,128)(2,1)}), bf16[1,4,64,1,4,256]{5,4,2,3,0,1:T(4,128)(2,1)S(1)}, u32[]{:S(2)}, u32[]{:S(2)}) async-start(bf16[1,4,64,1,4,256]{5,4,2,3,0,1:T(4,128)(2,1)} %copy.24), calls=%async_computation.3 | async-start | bytes 1048576 | tf_op jit(solution)/shard_map/all_to_all | solution.py:109
  176.0 233.7 %all-reduce.3.cloned.1.call-done = f32[65536]{0:T(1024)} async-done(((f32[65536]{0:T(1024)}), f32[65536]{0:T(1024)}) %all-reduce.3.cloned.1.call-update) | async-done | bytes 262160 | tf_op jit(solution)/shard_map/psum | solution.py:123
  409.7 0.7 fusion.45
  410.4 0.1 multiply_convert_fusion.4
  410.5 0.6 copy.26
  411.1 0.0 all-to-all-done.3
  411.1 0.2 copy.25
  411.3 0.1 reshape.294
  411.4 0.1 fusion.49
  411.5 0.7 fusion.9
  412.3 0.7 fusion.10
  413.0 2.4 pad_maximum_fusion
  (3 shorter events, 0.0 us)
Async XLA Ops:
  9.3 14.5 %copy-start.1 = (s32[256]{0:T(256)S(1)}, s32[256]{0:T(256)}, u32[]{:S(2)}) copy-start(s32[256]{0:T(256)} %param.13) | copy-start | bytes 3076
  9.3 14.5 %copy-start.2 = (s32[256]{0:T(256)S(1)}, s32[256]{0:T(256)}, u32[]{:S(2)}) copy-start(s32[256]{0:T(256)} %param.12) | copy-start | bytes 3076
  97.5 1.3 copy-start.3
  97.5 1.3 copy-start.4
  97.5 16.3 %copy-start = (s32[16,512]{1,0:T(8,128)S(1)}, s32[16,512]{1,0:T(8,128)}, u32[]{:S(2)}) copy-start(s32[16,512]{1,0:T(8,128)} %param.17) | copy-start | bytes 98308
  97.5 39.3 %copy-start.5 = (s32[16,512]{1,0:T(8,128)S(1)}, s32[16,512]{1,0:T(8,128)}, u32[]{:S(2)}) copy-start(s32[16,512]{1,0:T(8,128)} %param.16) | copy-start | bytes 98308
  101.7 29.3 %all-to-all-start = ((bf16[64,4,1,1,4,256]{5,4,1,3,2,0:T(4,128)(2,1)}), bf16[64,4,1,1,4,256]{5,4,1,3,2,0:T(4,128)(2,1)S(1)}, u32[]{:S(2)}, u32[]{:S(2)}) async-start(bf16[64,4,1,1,4,256]{5,4,1,3,2,0:T(4,128)(2,1)} %bitcast.18), calls=%async_computation | async-start | bytes 1048576 | tf_op jit(solution)/shard_map/all_to_all | solution.py:110
  132.0 13.2 %all-to-all-start.1 = ((bf16[1,4,64,1,4,256]{5,4,2,3,0,1:T(4,128)(2,1)}), bf16[1,4,64,1,4,256]{5,4,2,3,0,1:T(4,128)(2,1)S(1)}, u32[]{:S(2)}, u32[]{:S(2)}) async-start(bf16[1,4,64,1,4,256]{5,4,2,3,0,1:T(4,128)(2,1)} %copy.19), calls=%async_computation.1 | async-start | bytes 1048576 | tf_op jit(solution)/shard_map/all_to_all | solution.py:109
  146.9 23.3 %all-to-all-start.2 = ((bf16[64,4,1,1,4,256]{5,4,1,3,2,0:T(4,128)(2,1)}), bf16[64,4,1,1,4,256]{5,4,1,3,2,0:T(4,128)(2,1)S(1)}, u32[]{:S(2)}, u32[]{:S(2)}) async-start(bf16[64,4,1,1,4,256]{5,4,1,3,2,0:T(4,128)(2,1)} %bitcast.37), calls=%async_computation.2 | async-start | bytes 1048576 | tf_op jit(solution)/shard_map/all_to_all | solution.py:110
  153.0 256.8 %all-reduce.3.cloned.1.call-start = ((), (), s32[]{:S(2)}) async-start(), calls=%async_computation.4 | async-start | bytes 524288 | tf_op jit(solution)/shard_map/psum | solution.py:123
  171.1 240.0 %all-to-all-start.3 = ((bf16[1,4,64,1,4,256]{5,4,2,3,0,1:T(4,128)(2,1)}), bf16[1,4,64,1,4,256]{5,4,2,3,0,1:T(4,128)(2,1)S(1)}, u32[]{:S(2)}, u32[]{:S(2)}) async-start(bf16[1,4,64,1,4,256]{5,4,2,3,0,1:T(4,128)(2,1)} %copy.24), calls=%async_computation.3 | async-start | bytes 1048576 | tf_op jit(solution)/shard_map/all_to_all | solution.py:109
Sparse Core Ops, SparseCore 0:
  159.3 250.4 all-reduce.2

commit v4 on v1

--- a/solution.py
+++ b/solution.py
@@ -3,6 +3,8 @@
 import jax
 import jax.numpy as jnp
 from jax import lax
+from jax.experimental import pallas as pl
+from jax.experimental.pallas import tpu as pltpu
 from jax.sharding import PartitionSpec as P
 
 STATIONS = 512
@@ -43,15 +45,54 @@
     return (weight_re.astype(jnp.bfloat16), weight_im.astype(jnp.bfloat16))
 
 
+def fir_kernel(x_ref, h_ref, o_ref, xs_ref):
+    tap_count = h_ref.shape[0]
+    frames = x_ref.shape[2]
+    spectra = o_ref.shape[2]
+    lanes = 256
+    xs_ref[pl.ds(0, frames), :] = x_ref[0, 0].astype(jnp.float32)
+
+    def lane_body(lane_block, carry):
+        n0 = pl.multiple_of(lane_block * lanes, lanes)
+        taps = [
+            jnp.broadcast_to(h_ref[pl.ds(t, 1), pl.ds(n0, lanes)], (8, lanes))
+            for t in range(tap_count)
+        ]
+        for pair in range(spectra // 16):
+            halves = []
+            for half in range(2):
+                s0 = 16 * pair + 8 * half
+                acc = taps[0] * xs_ref[pl.ds(s0, 8), pl.ds(n0, lanes)]
+                for t in range(1, tap_count):
+                    acc = acc + taps[t] * xs_ref[pl.ds(s0 + t, 8), pl.ds(n0, lanes)]
+                halves.append(acc)
+            block = jnp.concatenate(halves, axis=0).astype(o_ref.dtype)
+            o_ref[0, 0, pl.ds(16 * pair, 16), pl.ds(n0, lanes)] = block
+        return carry
+
+    lax.fori_loop(0, xs_ref.shape[1] // lanes, lane_body, 0)
+
+
 def polyphase(in_block, fir_taps, spectra):
     tap_count, points = fir_taps.shape
-    framed = in_block.reshape(in_block.shape[0], in_block.shape[1], -1, points)
-    summed = jnp.zeros((framed.shape[0], framed.shape[1], spectra, points), jnp.float32)
-    for tap_index in range(tap_count):
-        summed = summed + fir_taps[tap_index] * framed[
-            :, :, tap_index : tap_index + spectra, :
-        ].astype(jnp.float32)
-    return summed.astype(jnp.bfloat16)
+    components, inputs_here = in_block.shape[0], in_block.shape[1]
+    frames = in_block.shape[2] // points
+    framed = in_block.reshape(components, inputs_here, frames, points)
+    return pl.pallas_call(
+        fir_kernel,
+        grid=(components * inputs_here,),
+        in_specs=[
+            pl.BlockSpec(
+                (1, 1, frames, points), lambda r: (r // inputs_here, r % inputs_here, 0, 0)
+            ),
+            pl.BlockSpec((tap_count, points), lambda r: (0, 0)),
+        ],
+        out_specs=pl.BlockSpec(
+            (1, 1, spectra, points), lambda r: (r // inputs_here, r % inputs_here, 0, 0)
+        ),
+        out_shape=jax.ShapeDtypeStruct((components, inputs_here, spectra, points), jnp.bfloat16),
+        scratch_shapes=[pltpu.VMEM((8 * pl.cdiv(frames, 8), points), jnp.float32)],
+    )(framed, fir_taps)
 
 
 def contract(left_rows, right_rows):

time: 201 us -> 186 us (0.925)
  other arithmetic: 63.6 us -> 11.1 us
  Pallas kernels: 0 us -> 39.2 us
    convert_element_type x1 -> x0, other arithmetic: 52.5 us -> none  [polyphase(): return summed.astype(jnp.bfloat16)]
    pallas_call x0 -> x1, Pallas kernels: none -> 39.2 us  [polyphase(): pl.pallas_call(fir_kernel, grid=(components * inputs_here,), in_specs=[pl...]
    slice x1 -> x0, local copies, waits for them, and re-layouts: 2.15 us -> none  [polyphase(): fir_taps[tap_index]]
  transfers between devices with their start and end apart: 1 -> 1, of which waited for: 1 -> 1; matrix products, arithmetic and copies ran while one was open for 3% -> 4% of each run, Pallas kernels for 0% -> 0%
where the time goes in v4:
time: 186 us
  blocking collectives  77.1 us (41%)
  Pallas kernels  39.2 us (21%)
  matrix products  22.9 us (12%)
  local copies, waits for them, and re-layouts  22.3 us (12%)
  other arithmetic  11.1 us (6%)
  waiting for transfers between devices  7.63 us (4%)
  starting transfers between devices  4.82 us (3%)
    all_to_all x1, blocking collectives, per_device(): lax.all_to_all(outgoing, STN_AXES, split_axis=1, concat_axis=3, tiled=True)  40.1 us
    pallas_call x1, Pallas kernels, polyphase(): pl.pallas_call(fir_kernel, grid=(components * inputs_here,), in_specs=[pl...  39.2 us
    psum x4, blocking collectives, per_device(): summed_power = lax.psum(summed_power, axis)  37 us
    dot_general x3, matrix products, contract(): lax.dot_general(left_rows, right_rows, contract_dims, preferred_element_t...  16.1 us
    reshape x1, local copies, waits for them, and re-layouts, polyphase(): framed = in_block.reshape(components, inputs_here, frames, points)  14.5 us
    all_to_all x1, waiting for transfers between devices, per_device(): lax.all_to_all(lax.all_to_all(outgoing, STN_AXES, split_axis=1, concat_ax...  7.63 us
    convert_element_type x1, other arithmetic, make_tables(): sin_table = ((sa * cb + ca * sb) * table_scale).astype(jnp.bfloat16)  5.32 us
    all_to_all x1, starting transfers between devices, per_device(): lax.all_to_all(lax.all_to_all(outgoing, STN_AXES, split_axis=1, concat_ax...  4.82 us
  transfers between devices with their start and end apart: 1, of which 1 were waited for; matrix products, arithmetic and copies ran while one was open for 4% of the time, Pallas kernels for 0%

profile of v4, /device:TPU:2, one launch (start us, length us, event | category | flops | bytes accessed | tf_op | source)
XLA Modules:
  0.0 185.8 jit_solution(311619522387702054)
XLA Ops:
  0.6 0.8 concatenate.64
  1.4 0.8 concatenate.63
  2.2 0.1 copy.37
  2.3 0.0 copy-start.1
  2.3 0.0 copy-start.2
  2.3 14.5 %reshape.284.x_ref = bf16[2,4,139,4096]{3,2,1,0:T(8,128)(2,1)} reshape(bf16[2,4,569344]{2,1,0:T(4,128)(2,1)} %param.8) | data formatting | bytes 18219008 | tf_op jit(solution)/shard_map/reshape | solution.py:80
  16.8 0.0 copy-done.1
  16.8 0.0 copy-done.2
  16.8 1.0 fusion.31
  17.8 5.3 %multiply_convert_fusion = (bf16[512,64,64]{0,2,1:T(8,128)(2,1)}, bf16[512,64,64]{0,2,1:T(8,128)(2,1)}) fusion(f32[512,64]{0,1:T(8,128)S(1)} %get-tuple-element.30, f32[512,64]{0,1:T(8,128)S(1)} %get-tuple-element.29, f32[512,64]{0,1:T(8,128)S(1)} %get-tuple-element.31, f32[512,64]{0,1:T(8,128)S(1)} %get-tuple-element.28), kind=kLoop, calls=%fused_computation.9 | loop fusion | flops 20971520 | bytes 8912896 | tf_op jit(solution)/shard_map/convert_element_type | solution.py:33
  23.1 39.2 %shard_map.95 = bf16[2,4,128,4096]{3,2,1,0:T(8,128)(2,1)} custom-call(bf16[2,4,139,4096]{3,2,1,0:T(8,128)(2,1)} %reshape.284.x_ref, f32[12,4096]{1,0:T(8,128)} %h_ref.1), custom_call_target="tpu_custom_call" | custom-call | tf_op jit(solution)/shard_map/pallas_call | solution.py:81
  62.4 13.7 %fusion.2 = f32[1024,1024]{1,0:T(8,128)S(1)} fusion(bf16[1024,4096]{1,0:T(8,128)(2,1)} %bitcast.51, bf16[512,4096]{0,1:T(8,128)(2,1)} %bitcast.52, bf16[512,4096]{0,1:T(8,128)(2,1)} %bitcast.53), kind=kOutput, calls=%fused_computation.3 | convolution fusion | flops 8606711808 | bytes 20971520 | tf_op jit(solution)/shard_map/dot_general | solution.py:100
  76.1 0.5 slice_add_fusion
  76.5 0.4 concatenate.61
  76.9 0.4 concatenate.60
  77.3 0.0 copy-start
  77.3 0.0 copy-start.3
  77.3 0.7 fusion.8
  78.0 40.1 %all_to_all.33 = bf16[2,64,4,1,1,4,256]{6,5,2,0,4,3,1:T(4,128)(2,1)S(1)} all-to-all(bf16[2,64,4,1,1,4,256]{6,5,2,0,4,3,1:T(4,128)(2,1)S(1)} %fusion.8), channel_id=1, replica_groups=mesh['y'=4,'z'=8,'core'=2,'x'=4] {'y','z','core'}, dimensions={1} | all-to-all | bytes 2097152 | tf_op jit(solution)/shard_map/all_to_all | solution.py:147
  118.1 1.4 copy.38
  119.5 4.8 %all-to-all-start.1 = ((bf16[2,1,4,64,1,4,256]{6,5,3,0,4,1,2:T(4,128)(2,1)}), bf16[2,1,4,64,1,4,256]{6,5,3,0,4,1,2:T(4,128)(2,1)S(1)}, u32[]{:S(2)}, u32[]{:S(2)}) async-start(bf16[2,1,4,64,1,4,256]{6,5,3,0,4,1,2:T(4,128)(2,1)} %copy.38), calls=%async_computation.1 | async-start | bytes 2097152 | tf_op jit(solution)/shard_map/all_to_all | solution.py:146
  124.3 0.0 copy-done
  124.3 0.2 multiply_bitcast_fusion.1
  124.5 0.0 copy-done.3
  124.5 3.2 %fusion = bf16[16,1,512]{2,1,0:T(2,128)(2,1)S(1)} fusion(s32[16,512]{1,0:T(8,128)S(1)} %copy-done.3, bf16[16,512,1]{1,0,2:T(8,128)(2,1)S(1)} %get-tuple-element.27), kind=kOutput, calls=%fused_computation.1 | convolution fusion | flops 12582912 | bytes 65536 | tf_op jit(solution)/shard_map/bk,bks->bs/dot_general | solution.py:44
  127.7 3.2 %fusion.1 = bf16[16,1,512]{2,1,0:T(2,128)(2,1)S(1)} fusion(s32[16,512]{1,0:T(8,128)S(1)} %copy-done.3, bf16[16,512,1]{1,0,2:T(8,128)(2,1)S(1)} %get-tuple-element.26), kind=kOutput, calls=%fused_computation.2 | convolution fusion | flops 12582912 | bytes 65536 | tf_op jit(solution)/shard_map/bk,bks->bs/dot_general | solution.py:43
  130.9 7.6 %all-to-all-done.1 = bf16[2,1,4,64,1,4,256]{6,5,3,0,4,1,2:T(4,128)(2,1)S(1)} async-done(((bf16[2,1,4,64,1,4,256]{6,5,3,0,4,1,2:T(4,128)(2,1)}), bf16[2,1,4,64,1,4,256]{6,5,3,0,4,1,2:T(4,128)(2,1)S(1)}, u32[]{:S(2)}, u32[]{:S(2)}) %all-to-all-start.1) | async-done | bytes 1048608 | tf_op jit(solution)/shard_map/all_to_all | solution.py:146
  138.6 0.4 fusion.46
  138.9 0.2 copy.39
  139.1 0.1 squeeze.3
  139.3 0.8 fusion.47
  140.0 0.7 fusion.9
  140.8 1.0 copy.40
  141.7 1.8 reshape.286
  143.6 0.2 convolution_bitcast_fusion
  143.7 0.2 convolution_bitcast_fusion.1
  143.9 0.1 multiply_reduce_fusion
  144.1 2.5 %psum.28 = f32[16]{0:T(128)S(1)} all-reduce(f32[16]{0:T(128)S(1)} %multiply_reduce_fusion), channel_id=1, replica_groups=mesh['y'=4,'z'=8,'core'=2,'x'=4] {'core'}, use_global_device_ids=true, to_apply=%region_1.2 | all-reduce | flops 16 | bytes 128 | tf_op jit(solution)/shard_map/psum | solution.py:164
  146.5 9.2 %psum.29 = f32[16]{0:T(128)S(1)} all-reduce(f32[16]{0:T(128)S(1)} %psum.28), channel_id=1, replica_groups=mesh['y'=4,'z'=8,'core'=2,'x'=4] {'x'}, use_global_device_ids=true, to_apply=%region_2.3 | all-reduce | flops 16 | bytes 128 | tf_op jit(solution)/shard_map/psum | solution.py:164
  155.7 9.5 %psum.30 = f32[16]{0:T(128)S(1)} all-reduce(f32[16]{0:T(128)S(1)} %psum.29), channel_id=1, replica_groups=mesh['y'=4,'z'=8,'core'=2,'x'=4] {'y'}, use_global_device_ids=true, to_apply=%region_3.4 | all-reduce | flops 16 | bytes 128 | tf_op jit(solution)/shard_map/psum | solution.py:164
  165.2 15.9 %psum.31 = f32[16]{0:T(128)S(1)} all-reduce(f32[16]{0:T(128)S(1)} %psum.30), channel_id=1, replica_groups=mesh['y'=4,'z'=8,'core'=2,'x'=4] {'z'}, use_global_device_ids=true, to_apply=%region_4.5 | all-reduce | flops 16 | bytes 128 | tf_op jit(solution)/shard_map/psum | solution.py:164
  181.0 0.1 multiply_convert_fusion.4
  181.1 0.6 copy.43
  181.7 1.7 fusion.10
  183.4 2.4 %pad_maximum_fusion = bf16[1,2,1024,1024]{3,2,1,0:T(8,128)(2,1)} fusion(bf16[1,1,1024,1024]{3,2,1,0:T(8,128)(2,1)S(1)} %fusion.10, bf16[1,1,1024,1024]{3,2,1,0:T(8,128)(2,1)S(1)} %fusion.9), kind=kLoop, calls=%fused_computation.11 | loop fusion | flops 2097152 | bytes 8388608 | tf_op jit(solution)/shard_map/stack | solution.py:159
  (4 shorter events, 0.0 us)
Async XLA Ops:
  2.3 14.5 %copy-start.1 = (s32[256]{0:T(256)S(1)}, s32[256]{0:T(256)}, u32[]{:S(2)}) copy-start(s32[256]{0:T(256)} %param.11) | copy-start | bytes 3076
  2.3 14.5 %copy-start.2 = (s32[256]{0:T(256)S(1)}, s32[256]{0:T(256)}, u32[]{:S(2)}) copy-start(s32[256]{0:T(256)} %param.10) | copy-start | bytes 3076
  77.3 47.1 %copy-start = (s32[16,512]{1,0:T(8,128)S(1)}, s32[16,512]{1,0:T(8,128)}, u32[]{:S(2)}) copy-start(s32[16,512]{1,0:T(8,128)} %param.15) | copy-start | bytes 98308
  77.3 47.2 %copy-start.3 = (s32[16,512]{1,0:T(8,128)S(1)}, s32[16,512]{1,0:T(8,128)}, u32[]{:S(2)}) copy-start(s32[16,512]{1,0:T(8,128)} %param.14) | copy-start | bytes 98308
  119.5 19.1 %all-to-all-start.1 = ((bf16[2,1,4,64,1,4,256]{6,5,3,0,4,1,2:T(4,128)(2,1)}), bf16[2,1,4,64,1,4,256]{6,5,3,0,4,1,2:T(4,128)(2,1)S(1)}, u32[]{:S(2)}, u32[]{:S(2)}) async-start(bf16[2,1,4,64,1,4,256]{6,5,3,0,4,1,2:T(4,128)(2,1)} %copy.38), calls=%async_computation.1 | async-start | bytes 2097152 | tf_op jit(solution)/shard_map/all_to_all | solution.py:146

commit v5 on v4

--- a/solution.py
+++ b/solution.py
@@ -14,6 +14,7 @@
 
 STN_AXES = ("y", "z", "core")
 PHYSICAL_AXES = ("core", "x", "y", "z")
+ALL_AXES = ("y", "z", "core", "x")
 
 
 def make_tables(channel_of, points):
@@ -142,14 +143,8 @@
     cos_table, sin_table = lax.optimization_barrier(make_tables(channel_of, points))
     weight_re, weight_im = make_weights(beam_stations, beam_codes, STATIONS)
     spectra_all = spectrum(filtered, cos_table, sin_table, slot_gain)
-    outgoing = spectra_all.reshape(2, stn_count, sec_count, 1, 1, inputs_here, 2 * spectra)
-    turned = lax.all_to_all(
-        lax.all_to_all(outgoing, STN_AXES, split_axis=1, concat_axis=3, tiled=True),
-        "x",
-        split_axis=2,
-        concat_axis=4,
-        tiled=True,
-    )
+    outgoing = spectra_all.reshape(2, device_count, inputs_here, 2 * spectra)
+    turned = lax.all_to_all(outgoing, ALL_AXES, split_axis=1, concat_axis=1, tiled=True)
     received = turned.reshape(2, device_count * inputs_here, 2 * spectra)
     cor_data = received[0]
     beam_data = received[1:2]

time: 186 us -> 170 us (0.914)
  blocking collectives: 77.1 us -> 35.1 us
  waiting for transfers between devices: 7.63 us -> 25.2 us
  starting transfers between devices: 4.82 us -> 14.7 us
  local copies, waits for them, and re-layouts: 22.3 us -> 19.1 us
    all_to_all x1 -> x0, blocking collectives: 40.1 us -> none  [per_device(): lax.all_to_all(outgoing, STN_AXES, split_axis=1, concat_axis=3, tiled=True)]
    all_to_all x1, waiting for transfers between devices: 7.63 us -> 25.2 us  [per_device(): lax.all_to_all(outgoing, ALL_AXES, split_axis=1, concat_axis=1, tiled=True)]
    all_to_all x1, starting transfers between devices: 4.82 us -> 14.7 us  [per_device(): lax.all_to_all(outgoing, ALL_AXES, split_axis=1, concat_axis=1, tiled=True)]
where the time goes in v5:
time: 170 us
  Pallas kernels  39.2 us (23%)
  blocking collectives  35.1 us (21%)
  waiting for transfers between devices  25.2 us (15%)
  matrix products  22.9 us (13%)
  local copies, waits for them, and re-layouts  19.1 us (11%)
  starting transfers between devices  14.7 us (9%)
  other arithmetic  12.5 us (7%)
    pallas_call x1, Pallas kernels, polyphase(): pl.pallas_call(fir_kernel, grid=(components * inputs_here,), in_specs=[pl...  39.2 us
    psum x4, blocking collectives, per_device(): summed_power = lax.psum(summed_power, axis)  35.1 us
    all_to_all x1, waiting for transfers between devices, per_device(): lax.all_to_all(outgoing, ALL_AXES, split_axis=1, concat_axis=1, tiled=True)  25.2 us
    dot_general x3, matrix products, contract(): lax.dot_general(left_rows, right_rows, contract_dims, preferred_element_t...  16.1 us
    all_to_all x1, starting transfers between devices, per_device(): lax.all_to_all(outgoing, ALL_AXES, split_axis=1, concat_axis=1, tiled=True)  14.7 us
    reshape x1, local copies, waits for them, and re-layouts, polyphase(): framed = in_block.reshape(components, inputs_here, frames, points)  14.5 us
    convert_element_type x1, other arithmetic, make_tables(): sin_table = ((sa * cb + ca * sb) * table_scale).astype(jnp.bfloat16)  5.32 us
  transfers between devices with their start and end apart: 1, of which 1 were waited for; matrix products, arithmetic and copies ran while one was open for 4% of the time, Pallas kernels for 0%

profile of v5, /device:TPU:2, one launch (start us, length us, event | category | flops | bytes accessed | tf_op | source)
XLA Modules:
  0.0 169.6 jit_solution(15842300180780123296)
XLA Ops:
  0.6 0.7 pad_maximum_fusion.3
  1.3 0.1 copy.21
  1.5 0.0 copy-start.1
  1.5 0.0 copy-start.2
  1.5 14.5 %reshape.251.x_ref = bf16[2,4,139,4096]{3,2,1,0:T(8,128)(2,1)} reshape(bf16[2,4,569344]{2,1,0:T(4,128)(2,1)} %param.8) | data formatting | bytes 18219008 | tf_op jit(solution)/shard_map/reshape | solution.py:81
  16.0 0.0 copy-done.1
  16.0 0.0 copy-done.2
  16.0 1.0 fusion.31
  17.0 5.3 %multiply_convert_fusion = (bf16[512,64,64]{0,2,1:T(8,128)(2,1)}, bf16[512,64,64]{0,2,1:T(8,128)(2,1)}) fusion(f32[512,64]{0,1:T(8,128)S(1)} %get-tuple-element.28, f32[512,64]{0,1:T(8,128)S(1)} %get-tuple-element.27, f32[512,64]{0,1:T(8,128)S(1)} %get-tuple-element.29, f32[512,64]{0,1:T(8,128)S(1)} %get-tuple-element.26), kind=kLoop, calls=%fused_computation.9 | loop fusion | flops 20971520 | bytes 8912896 | tf_op jit(solution)/shard_map/convert_element_type | solution.py:34
  22.4 39.2 %shard_map.95 = bf16[2,4,128,4096]{3,2,1,0:T(8,128)(2,1)} custom-call(bf16[2,4,139,4096]{3,2,1,0:T(8,128)(2,1)} %reshape.251.x_ref, f32[12,4096]{1,0:T(8,128)} %h_ref.1), custom_call_target="tpu_custom_call" | custom-call | tf_op jit(solution)/shard_map/pallas_call | solution.py:82
  61.6 13.7 %fusion.2 = f32[1024,1024]{1,0:T(8,128)S(1)} fusion(bf16[1024,4096]{1,0:T(8,128)(2,1)} %bitcast.43, bf16[512,4096]{0,1:T(8,128)(2,1)} %bitcast.44, bf16[512,4096]{0,1:T(8,128)(2,1)} %bitcast.45), kind=kOutput, calls=%fused_computation.3 | convolution fusion | flops 8606711808 | bytes 20971520 | tf_op jit(solution)/shard_map/dot_general | solution.py:101
  75.3 0.5 slice_add_fusion
  75.8 0.4 concatenate.50
  76.1 0.0 copy-start
  76.1 0.0 copy-start.3
  76.1 0.4 concatenate.49
  76.5 1.5 fusion.8
  78.0 14.7 %all-to-all-start = ((bf16[2,256,4,256]{3,2,0,1:T(4,128)(2,1)}), bf16[2,256,4,256]{3,2,0,1:T(4,128)(2,1)S(1)}, u32[]{:S(2)}, u32[]{:S(2)}) async-start(bf16[2,256,4,256]{3,2,0,1:T(4,128)(2,1)} %fusion.8), calls=%async_computation | async-start | bytes 2097152 | tf_op jit(solution)/shard_map/all_to_all | solution.py:147
  92.7 0.0 copy-done
  92.7 0.2 multiply_bitcast_fusion.1
  92.9 0.0 copy-done.3
  92.9 3.2 %fusion = bf16[16,1,512]{2,1,0:T(2,128)(2,1)S(1)} fusion(s32[16,512]{1,0:T(8,128)S(1)} %copy-done.3, bf16[16,512,1]{1,0,2:T(8,128)(2,1)S(1)} %get-tuple-element.25), kind=kOutput, calls=%fused_computation.1 | convolution fusion | flops 12582912 | bytes 65536 | tf_op jit(solution)/shard_map/bk,bks->bs/dot_general | solution.py:45
  96.1 3.2 %fusion.1 = bf16[16,1,512]{2,1,0:T(2,128)(2,1)S(1)} fusion(s32[16,512]{1,0:T(8,128)S(1)} %copy-done.3, bf16[16,512,1]{1,0,2:T(8,128)(2,1)S(1)} %get-tuple-element.24), kind=kOutput, calls=%fused_computation.2 | convolution fusion | flops 12582912 | bytes 65536 | tf_op jit(solution)/shard_map/bk,bks->bs/dot_general | solution.py:44
  99.3 25.2 %all-to-all-done = bf16[2,256,4,256]{3,2,0,1:T(4,128)(2,1)S(1)} async-done(((bf16[2,256,4,256]{3,2,0,1:T(4,128)(2,1)}), bf16[2,256,4,256]{3,2,0,1:T(4,128)(2,1)S(1)}, u32[]{:S(2)}, u32[]{:S(2)}) %all-to-all-start) | async-done | bytes 1048608 | tf_op jit(solution)/shard_map/all_to_all | solution.py:147
  124.6 1.2 fusion.46
  125.7 0.1 squeeze.3
  125.9 0.8 fusion.47
  126.6 0.7 fusion.9
  127.4 1.8 %reshape.253 = bf16[512,2,256]{2,1,0:T(2,128)(2,1)S(1)} reshape(bf16[1,256,4,256]{3,2,0,1:T(4,128)(2,1)} %get-tuple-element.16) | data formatting | bytes 1048576 | tf_op jit(solution)/shard_map/reshape.4
  129.2 0.2 convolution_bitcast_fusion
  129.4 0.2 convolution_bitcast_fusion.1
  129.6 0.1 multiply_reduce_fusion
  129.7 2.5 %psum.28 = f32[16]{0:T(128)S(1)} all-reduce(f32[16]{0:T(128)S(1)} %multiply_reduce_fusion), channel_id=1, replica_groups=mesh['y'=4,'z'=8,'core'=2,'x'=4] {'core'}, use_global_device_ids=true, to_apply=%region_1.2 | all-reduce | flops 16 | bytes 128 | tf_op jit(solution)/shard_map/psum | solution.py:159
  132.2 9.1 %psum.29 = f32[16]{0:T(128)S(1)} all-reduce(f32[16]{0:T(128)S(1)} %psum.28), channel_id=1, replica_groups=mesh['y'=4,'z'=8,'core'=2,'x'=4] {'x'}, use_global_device_ids=true, to_apply=%region_2.3 | all-reduce | flops 16 | bytes 128 | tf_op jit(solution)/shard_map/psum | solution.py:159
  141.3 8.5 %psum.30 = f32[16]{0:T(128)S(1)} all-reduce(f32[16]{0:T(128)S(1)} %psum.29), channel_id=1, replica_groups=mesh['y'=4,'z'=8,'core'=2,'x'=4] {'y'}, use_global_device_ids=true, to_apply=%region_3.4 | all-reduce | flops 16 | bytes 128 | tf_op jit(solution)/shard_map/psum | solution.py:159
  149.8 15.1 %psum.31 = f32[16]{0:T(128)S(1)} all-reduce(f32[16]{0:T(128)S(1)} %psum.30), channel_id=1, replica_groups=mesh['y'=4,'z'=8,'core'=2,'x'=4] {'z'}, use_global_device_ids=true, to_apply=%region_4.5 | all-reduce | flops 16 | bytes 128 | tf_op jit(solution)/shard_map/psum | solution.py:159
  164.8 0.1 multiply_convert_fusion.4
  164.9 0.6 copy.24
  165.5 1.7 fusion.10
  167.2 2.4 %pad_maximum_fusion = bf16[1,2,1024,1024]{3,2,1,0:T(8,128)(2,1)} fusion(bf16[1,1,1024,1024]{3,2,1,0:T(8,128)(2,1)S(1)} %fusion.10, bf16[1,1,1024,1024]{3,2,1,0:T(8,128)(2,1)S(1)} %fusion.9), kind=kLoop, calls=%fused_computation.11 | loop fusion | flops 2097152 | bytes 8388608 | tf_op jit(solution)/shard_map/stack | solution.py:154
  (4 shorter events, 0.0 us)
Async XLA Ops:
  1.5 14.5 %copy-start.1 = (s32[256]{0:T(256)S(1)}, s32[256]{0:T(256)}, u32[]{:S(2)}) copy-start(s32[256]{0:T(256)} %param.11) | copy-start | bytes 3076
  1.5 14.5 %copy-start.2 = (s32[256]{0:T(256)S(1)}, s32[256]{0:T(256)}, u32[]{:S(2)}) copy-start(s32[256]{0:T(256)} %param.10) | copy-start | bytes 3076
  76.1 16.6 %copy-start = (s32[16,512]{1,0:T(8,128)S(1)}, s32[16,512]{1,0:T(8,128)}, u32[]{:S(2)}) copy-start(s32[16,512]{1,0:T(8,128)} %param.15) | copy-start | bytes 98308
  76.1 16.8 %copy-start.3 = (s32[16,512]{1,0:T(8,128)S(1)}, s32[16,512]{1,0:T(8,128)}, u32[]{:S(2)}) copy-start(s32[16,512]{1,0:T(8,128)} %param.14) | copy-start | bytes 98308
  78.0 46.5 %all-to-all-start = ((bf16[2,256,4,256]{3,2,0,1:T(4,128)(2,1)}), bf16[2,256,4,256]{3,2,0,1:T(4,128)(2,1)S(1)}, u32[]{:S(2)}, u32[]{:S(2)}) async-start(bf16[2,256,4,256]{3,2,0,1:T(4,128)(2,1)} %fusion.8), calls=%async_computation | async-start | bytes 2097152 | tf_op jit(solution)/shard_map/all_to_all | solution.py:147

commit v6 on v5

--- a/solution.py
+++ b/solution.py
@@ -154,9 +154,9 @@
     visibilities = jnp.stack([vis_re, vis_im])[None].astype(jnp.bfloat16)
     raw_beams = form_beams(beam_data, weight_re, weight_im)
     local_power = jnp.sum(raw_beams * raw_beams, axis=(0, 2, 3))
-    summed_power = local_power
-    for axis in PHYSICAL_AXES:
-        summed_power = lax.psum(summed_power, axis)
+    spread_power = jnp.broadcast_to(local_power[None], (device_count, local_power.shape[0]))
+    gathered_power = lax.all_to_all(spread_power, ALL_AXES, split_axis=0, concat_axis=0, tiled=True)
+    summed_power = jnp.sum(gathered_power, axis=0)
     beam_power = summed_power / (device_count * raw_beams.shape[2] * raw_beams.shape[3])
     beams = (raw_beams * lax.rsqrt(beam_power + epsilon)[None, :, None, None]).astype(jnp.bfloat16)
     return (visibilities, beams)

time: 170 us -> 152 us (0.89)
  blocking collectives: 35.1 us -> 0 us
  waiting for transfers between devices: 25.2 us -> 33.6 us
  starting transfers between devices: 14.7 us -> 21.2 us
    psum x4 -> x0, blocking collectives: 35.1 us -> none  [per_device(): summed_power = lax.psum(summed_power, axis)]
    all_to_all x0 -> x1, waiting for transfers between devices: none -> 8.34 us  [per_device(): lax.all_to_all(spread_power, ALL_AXES, split_axis=0, concat_axis=0, tiled...]
    all_to_all x0 -> x1, starting transfers between devices: none -> 6.46 us  [per_device(): lax.all_to_all(spread_power, ALL_AXES, split_axis=0, concat_axis=0, tiled...]
  transfers between devices with their start and end apart: 1 -> 2, of which waited for: 1 -> 2; matrix products, arithmetic and copies ran while one was open for 4% -> 7% of each run, Pallas kernels for 0% -> 0%
where the time goes in v6:
time: 152 us; the launch traced here: 150 us
  Pallas kernels  39.2 us (26%)
  waiting for transfers between devices  33.6 us (22%)
  matrix products  22.9 us (15%)
  starting transfers between devices  21.2 us (14%)
  local copies, waits for them, and re-layouts  19.8 us (13%)
  other arithmetic  12.9 us (8%)
    pallas_call x1, Pallas kernels, polyphase(): pl.pallas_call(fir_kernel, grid=(components * inputs_here,), in_specs=[pl...  39.2 us
    all_to_all x1, waiting for transfers between devices, per_device(): lax.all_to_all(outgoing, ALL_AXES, split_axis=1, concat_axis=1, tiled=True)  25.2 us
    dot_general x3, matrix products, contract(): lax.dot_general(left_rows, right_rows, contract_dims, preferred_element_t...  16.1 us
    all_to_all x1, starting transfers between devices, per_device(): lax.all_to_all(outgoing, ALL_AXES, split_axis=1, concat_axis=1, tiled=True)  14.7 us
    reshape x1, local copies, waits for them, and re-layouts, polyphase(): framed = in_block.reshape(components, inputs_here, frames, points)  14.5 us
    all_to_all x1, waiting for transfers between devices, per_device(): lax.all_to_all(spread_power, ALL_AXES, split_axis=0, concat_axis=0, tiled...  8.34 us
    all_to_all x1, starting transfers between devices, per_device(): lax.all_to_all(spread_power, ALL_AXES, split_axis=0, concat_axis=0, tiled...  6.46 us
    convert_element_type x1, other arithmetic, make_tables(): sin_table = ((sa * cb + ca * sb) * table_scale).astype(jnp.bfloat16)  5.33 us
  transfers between devices with their start and end apart: 2, of which 2 were waited for; matrix products, arithmetic and copies ran while one was open for 7% of the time, Pallas kernels for 0%

profile of v6, /device:TPU:2, one launch (start us, length us, event | category | flops | bytes accessed | tf_op | source)
XLA Modules:
  0.0 150.3 jit_solution(3404965248007378002)
XLA Ops:
  0.6 0.7 pad_maximum_fusion.3
  1.3 0.1 copy.33
  1.5 0.0 copy-start.1
  1.5 0.0 copy-start.2
  1.5 14.5 %reshape.261.x_ref = bf16[2,4,139,4096]{3,2,1,0:T(8,128)(2,1)} reshape(bf16[2,4,569344]{2,1,0:T(4,128)(2,1)} %param.8) | data formatting | bytes 18219008 | tf_op jit(solution)/shard_map/reshape | solution.py:81
  16.0 0.0 copy-done.1
  16.0 0.0 copy-done.2
  16.0 1.0 fusion.31
  17.1 5.3 %multiply_convert_fusion = (bf16[512,64,64]{0,2,1:T(8,128)(2,1)}, bf16[512,64,64]{0,2,1:T(8,128)(2,1)}) fusion(f32[512,64]{0,1:T(8,128)S(1)} %get-tuple-element.32, f32[512,64]{0,1:T(8,128)S(1)} %get-tuple-element.31, f32[512,64]{0,1:T(8,128)S(1)} %get-tuple-element.33, f32[512,64]{0,1:T(8,128)S(1)} %get-tuple-element.30), kind=kLoop, calls=%fused_computation.9 | loop fusion | flops 20971520 | bytes 8912896 | tf_op jit(solution)/shard_map/convert_element_type | solution.py:34
  22.4 39.2 %shard_map.95 = bf16[2,4,128,4096]{3,2,1,0:T(8,128)(2,1)} custom-call(bf16[2,4,139,4096]{3,2,1,0:T(8,128)(2,1)} %reshape.261.x_ref, f32[12,4096]{1,0:T(8,128)} %h_ref.1), custom_call_target="tpu_custom_call" | custom-call | tf_op jit(solution)/shard_map/pallas_call | solution.py:82
  61.6 13.7 %fusion.2 = f32[1024,1024]{1,0:T(8,128)S(1)} fusion(bf16[1024,4096]{1,0:T(8,128)(2,1)} %bitcast.43, bf16[512,4096]{0,1:T(8,128)(2,1)} %bitcast.44, bf16[512,4096]{0,1:T(8,128)(2,1)} %bitcast.45), kind=kOutput, calls=%fused_computation.3 | convolution fusion | flops 8606711808 | bytes 20971520 | tf_op jit(solution)/shard_map/dot_general | solution.py:101
  75.3 0.5 slice_add_fusion
  75.8 0.4 concatenate.50
  76.1 0.0 copy-start
  76.1 0.0 copy-start.3
  76.1 0.4 concatenate.49
  76.5 1.5 %fusion.8 = bf16[2,256,4,256]{3,2,0,1:T(4,128)(2,1)} fusion(f32[2,256]{0,1:T(8,128)S(1)} %copy.33, f32[2,256,4,128]{3,2,1,0:T(4,128)S(1)} %concatenate.50, f32[2,256,4,128]{3,2,1,0:T(4,128)S(1)} %concatenate.49), kind=kLoop, calls=%fused_computation.16 | loop fusion | flops 1572864 | bytes 3147776 | tf_op jit(solution)/shard_map/convert_element_type | solution.py:118
  78.0 14.7 %all-to-all-start = ((bf16[2,256,4,256]{3,2,0,1:T(4,128)(2,1)}), bf16[2,256,4,256]{3,2,0,1:T(4,128)(2,1)S(1)}, u32[]{:S(2)}, u32[]{:S(2)}) async-start(bf16[2,256,4,256]{3,2,0,1:T(4,128)(2,1)} %fusion.8), calls=%async_computation | async-start | bytes 2097152 | tf_op jit(solution)/shard_map/all_to_all | solution.py:147
  92.7 0.0 copy-done
  92.7 0.2 multiply_bitcast_fusion.1
  92.9 0.0 copy-done.3
  92.9 3.2 %fusion = bf16[16,1,512]{2,1,0:T(2,128)(2,1)S(1)} fusion(s32[16,512]{1,0:T(8,128)S(1)} %copy-done.3, bf16[16,512,1]{1,0,2:T(8,128)(2,1)S(1)} %get-tuple-element.29), kind=kOutput, calls=%fused_computation.1 | convolution fusion | flops 12582912 | bytes 65536 | tf_op jit(solution)/shard_map/bk,bks->bs/dot_general | solution.py:45
  96.1 3.2 %fusion.1 = bf16[16,1,512]{2,1,0:T(2,128)(2,1)S(1)} fusion(s32[16,512]{1,0:T(8,128)S(1)} %copy-done.3, bf16[16,512,1]{1,0,2:T(8,128)(2,1)S(1)} %get-tuple-element.28), kind=kOutput, calls=%fused_computation.2 | convolution fusion | flops 12582912 | bytes 65536 | tf_op jit(solution)/shard_map/bk,bks->bs/dot_general | solution.py:44
  99.4 25.2 %all-to-all-done = bf16[2,256,4,256]{3,2,0,1:T(4,128)(2,1)S(1)} async-done(((bf16[2,256,4,256]{3,2,0,1:T(4,128)(2,1)}), bf16[2,256,4,256]{3,2,0,1:T(4,128)(2,1)S(1)}, u32[]{:S(2)}, u32[]{:S(2)}) %all-to-all-start) | async-done | bytes 1048608 | tf_op jit(solution)/shard_map/all_to_all | solution.py:147
  124.6 1.2 fusion.46
  125.7 0.1 squeeze.3
  125.9 0.8 fusion.47
  126.6 0.7 fusion.9
  127.4 1.8 %reshape.263 = bf16[512,2,256]{2,1,0:T(2,128)(2,1)S(1)} reshape(bf16[1,256,4,256]{3,2,0,1:T(4,128)(2,1)} %get-tuple-element.20) | data formatting | bytes 1048576 | tf_op jit(solution)/shard_map/reshape.4
  129.2 0.2 convolution_bitcast_fusion
  129.4 0.2 convolution_bitcast_fusion.1
  129.6 0.1 multiply_reduce_fusion
  129.7 0.7 broadcast_in_dim.2
  130.4 6.5 %all-to-all-start.1 = ((f32[256,1,16]{2,1,0:T(1,128)}), f32[256,1,16]{2,1,0:T(1,128)S(1)}, u32[]{:S(2)}, u32[]{:S(2)}) async-start(f32[256,1,16]{2,1,0:T(1,128)} %broadcast_in_dim.2), calls=%async_computation.1 | async-start | bytes 262144 | tf_op jit(solution)/shard_map/all_to_all | solution.py:158
  136.9 1.7 %fusion.10 = bf16[1,1,1024,1024]{3,2,1,0:T(8,128)(2,1)S(1)} fusion(bf16[1024,256]{1,0:T(8,128)(2,1)S(1)} %squeeze.3, bf16[1024,128]{1,0:T(8,128)(2,1)} %get-tuple-element.23, bf16[1024,128]{1,0:T(8,128)(2,1)S(1)} %get-tuple-element.22), kind=kOutput, calls=%fused_computation.18 | convolution fusion | flops 540016640 | bytes 3145728 | tf_op jit(solution)/shard_map/dot_general | solution.py:101
  138.6 2.4 %pad_maximum_fusion = bf16[1,2,1024,1024]{3,2,1,0:T(8,128)(2,1)} fusion(bf16[1,1,1024,1024]{3,2,1,0:T(8,128)(2,1)S(1)} %fusion.10, bf16[1,1,1024,1024]{3,2,1,0:T(8,128)(2,1)S(1)} %fusion.9), kind=kLoop, calls=%fused_computation.11 | loop fusion | flops 2097152 | bytes 8388608 | tf_op jit(solution)/shard_map/stack | solution.py:154
  141.0 8.3 %all-to-all-done.1 = f32[256,1,16]{2,1,0:T(1,128)S(1)} async-done(((f32[256,1,16]{2,1,0:T(1,128)}), f32[256,1,16]{2,1,0:T(1,128)S(1)}, u32[]{:S(2)}, u32[]{:S(2)}) %all-to-all-start.1) | async-done | bytes 16416 | tf_op jit(solution)/shard_map/all_to_all | solution.py:158
  149.3 0.3 reduce_sum.19
  149.6 0.1 multiply_convert_fusion.4
  149.7 0.6 copy.37
  (4 shorter events, 0.0 us)
Async XLA Ops:
  1.5 14.5 %copy-start.1 = (s32[256]{0:T(256)S(1)}, s32[256]{0:T(256)}, u32[]{:S(2)}) copy-start(s32[256]{0:T(256)} %param.11) | copy-start | bytes 3076
  1.5 14.5 %copy-start.2 = (s32[256]{0:T(256)S(1)}, s32[256]{0:T(256)}, u32[]{:S(2)}) copy-start(s32[256]{0:T(256)} %param.10) | copy-start | bytes 3076
  76.1 16.6 %copy-start = (s32[16,512]{1,0:T(8,128)S(1)}, s32[16,512]{1,0:T(8,128)}, u32[]{:S(2)}) copy-start(s32[16,512]{1,0:T(8,128)} %param.15) | copy-start | bytes 98308
  76.1 16.8 %copy-start.3 = (s32[16,512]{1,0:T(8,128)S(1)}, s32[16,512]{1,0:T(8,128)}, u32[]{:S(2)}) copy-start(s32[16,512]{1,0:T(8,128)} %param.14) | copy-start | bytes 98308
  78.0 46.5 %all-to-all-start = ((bf16[2,256,4,256]{3,2,0,1:T(4,128)(2,1)}), bf16[2,256,4,256]{3,2,0,1:T(4,128)(2,1)S(1)}, u32[]{:S(2)}, u32[]{:S(2)}) async-start(bf16[2,256,4,256]{3,2,0,1:T(4,128)(2,1)} %fusion.8), calls=%async_computation | async-start | bytes 2097152 | tf_op jit(solution)/shard_map/all_to_all | solution.py:147
  130.4 18.9 %all-to-all-start.1 = ((f32[256,1,16]{2,1,0:T(1,128)}), f32[256,1,16]{2,1,0:T(1,128)S(1)}, u32[]{:S(2)}, u32[]{:S(2)}) async-start(f32[256,1,16]{2,1,0:T(1,128)} %broadcast_in_dim.2), calls=%async_computation.1 | async-start | bytes 262144 | tf_op jit(solution)/shard_map/all_to_all | solution.py:158

commit v7 on v6

--- a/solution.py
+++ b/solution.py
@@ -46,32 +46,33 @@
     return (weight_re.astype(jnp.bfloat16), weight_im.astype(jnp.bfloat16))
 
 
-def fir_kernel(x_ref, h_ref, o_ref, xs_ref):
+def fir_kernel(x_ref, h_ref, o_ref, xs_ref, os_ref):
     tap_count = h_ref.shape[0]
     frames = x_ref.shape[2]
     spectra = o_ref.shape[2]
-    lanes = 256
-    xs_ref[pl.ds(0, frames), :] = x_ref[0, 0].astype(jnp.float32)
+    stride = 16
+    depth = spectra // stride
+    lanes = 128
 
     def lane_body(lane_block, carry):
         n0 = pl.multiple_of(lane_block * lanes, lanes)
+        xs_ref[pl.ds(0, frames), :] = x_ref[0, 0, :, pl.ds(n0, lanes)].astype(jnp.float32)
+        groups = [
+            xs_ref[pl.ds(g, depth, stride=stride), :] for g in range(stride + tap_count - 1)
+        ]
         taps = [
-            jnp.broadcast_to(h_ref[pl.ds(t, 1), pl.ds(n0, lanes)], (8, lanes))
+            jnp.broadcast_to(h_ref[pl.ds(t, 1), pl.ds(n0, lanes)], (depth, lanes))
             for t in range(tap_count)
         ]
-        for pair in range(spectra // 16):
-            halves = []
-            for half in range(2):
-                s0 = 16 * pair + 8 * half
-                acc = taps[0] * xs_ref[pl.ds(s0, 8), pl.ds(n0, lanes)]
-                for t in range(1, tap_count):
-                    acc = acc + taps[t] * xs_ref[pl.ds(s0 + t, 8), pl.ds(n0, lanes)]
-                halves.append(acc)
-            block = jnp.concatenate(halves, axis=0).astype(o_ref.dtype)
-            o_ref[0, 0, pl.ds(16 * pair, 16), pl.ds(n0, lanes)] = block
+        for q in range(stride):
+            acc = taps[0] * groups[q]
+            for t in range(1, tap_count):
+                acc = acc + taps[t] * groups[q + t]
+            os_ref[pl.ds(q, depth, stride=stride), :] = acc
+        o_ref[0, 0, :, pl.ds(n0, lanes)] = os_ref[...].astype(o_ref.dtype)
         return carry
 
-    lax.fori_loop(0, xs_ref.shape[1] // lanes, lane_body, 0)
+    lax.fori_loop(0, h_ref.shape[1] // lanes, lane_body, 0)
 
 
 def polyphase(in_block, fir_taps, spectra):
@@ -92,7 +93,10 @@
             (1, 1, spectra, points), lambda r: (r // inputs_here, r % inputs_here, 0, 0)
         ),
         out_shape=jax.ShapeDtypeStruct((components, inputs_here, spectra, points), jnp.bfloat16),
-        scratch_shapes=[pltpu.VMEM((8 * pl.cdiv(frames, 8), points), jnp.float32)],
+        scratch_shapes=[
+            pltpu.VMEM((8 * pl.cdiv(frames, 8), 128), jnp.float32),
+            pltpu.VMEM((spectra, 128), jnp.float32),
+        ],
     )(framed, fir_taps)
 
 

time: 152 us -> 140 us (0.921)
  Pallas kernels: 39.2 us -> 27.2 us
    pallas_call x1, Pallas kernels: 39.2 us -> 27.2 us  [polyphase(): pl.pallas_call(fir_kernel, grid=(components * inputs_here,), in_specs=[pl...]
  transfers between devices with their start and end apart: 2 -> 2, of which waited for: 2 -> 2; matrix products, arithmetic and copies ran while one was open for 7% -> 8% of each run, Pallas kernels for 0% -> 0%
where the time goes in v7:
time: 140 us; the launch traced here: 138 us
  waiting for transfers between devices  33.6 us (24%)
  Pallas kernels  27.2 us (19%)
  matrix products  22.9 us (16%)
  starting transfers between devices  21.2 us (15%)
  local copies, waits for them, and re-layouts  19.8 us (14%)
  other arithmetic  12.9 us (9%)
    pallas_call x1, Pallas kernels, polyphase(): pl.pallas_call(fir_kernel, grid=(components * inputs_here,), in_specs=[pl...  27.2 us
    all_to_all x1, waiting for transfers between devices, per_device(): lax.all_to_all(outgoing, ALL_AXES, split_axis=1, concat_axis=1, tiled=True)  25.2 us
    dot_general x3, matrix products, contract(): lax.dot_general(left_rows, right_rows, contract_dims, preferred_element_t...  16.1 us
    all_to_all x1, starting transfers between devices, per_device(): lax.all_to_all(outgoing, ALL_AXES, split_axis=1, concat_axis=1, tiled=True)  14.7 us
    reshape x1, local copies, waits for them, and re-layouts, polyphase(): framed = in_block.reshape(components, inputs_here, frames, points)  14.5 us
    all_to_all x1, waiting for transfers between devices, per_device(): lax.all_to_all(spread_power, ALL_AXES, split_axis=0, concat_axis=0, tiled...  8.34 us
    all_to_all x1, starting transfers between devices, per_device(): lax.all_to_all(spread_power, ALL_AXES, split_axis=0, concat_axis=0, tiled...  6.46 us
    convert_element_type x1, other arithmetic, make_tables(): sin_table = ((sa * cb + ca * sb) * table_scale).astype(jnp.bfloat16)  5.33 us
  transfers between devices with their start and end apart: 2, of which 2 were waited for; matrix products, arithmetic and copies ran while one was open for 8% of the time, Pallas kernels for 0%

profile of v7, /device:TPU:2, one launch (start us, length us, event | category | flops | bytes accessed | tf_op | source)
XLA Modules:
  0.0 138.3 jit_solution(8298717579716653516)
XLA Ops:
  0.6 0.7 pad_maximum_fusion.3
  1.3 0.1 copy.33
  1.5 0.0 copy-start.1
  1.5 0.0 copy-start.2
  1.5 14.5 %reshape.261.x_ref = bf16[2,4,139,4096]{3,2,1,0:T(8,128)(2,1)} reshape(bf16[2,4,569344]{2,1,0:T(4,128)(2,1)} %param.8) | data formatting | bytes 18219008 | tf_op jit(solution)/shard_map/reshape | solution.py:82
  16.0 0.0 copy-done.1
  16.0 0.0 copy-done.2
  16.0 1.0 fusion.31
  17.1 5.3 %multiply_convert_fusion = (bf16[512,64,64]{0,2,1:T(8,128)(2,1)}, bf16[512,64,64]{0,2,1:T(8,128)(2,1)}) fusion(f32[512,64]{0,1:T(8,128)S(1)} %get-tuple-element.32, f32[512,64]{0,1:T(8,128)S(1)} %get-tuple-element.31, f32[512,64]{0,1:T(8,128)S(1)} %get-tuple-element.33, f32[512,64]{0,1:T(8,128)S(1)} %get-tuple-element.30), kind=kLoop, calls=%fused_computation.9 | loop fusion | flops 20971520 | bytes 8912896 | tf_op jit(solution)/shard_map/convert_element_type | solution.py:34
  22.4 27.2 %shard_map.95 = bf16[2,4,128,4096]{3,2,1,0:T(8,128)(2,1)} custom-call(bf16[2,4,139,4096]{3,2,1,0:T(8,128)(2,1)} %reshape.261.x_ref, f32[12,4096]{1,0:T(8,128)} %h_ref.1), custom_call_target="tpu_custom_call" | custom-call | tf_op jit(solution)/shard_map/pallas_call | solution.py:83
  49.5 13.7 %fusion.2 = f32[1024,1024]{1,0:T(8,128)S(1)} fusion(bf16[1024,4096]{1,0:T(8,128)(2,1)} %bitcast.43, bf16[512,4096]{0,1:T(8,128)(2,1)} %bitcast.44, bf16[512,4096]{0,1:T(8,128)(2,1)} %bitcast.45), kind=kOutput, calls=%fused_computation.3 | convolution fusion | flops 8606711808 | bytes 20971520 | tf_op jit(solution)/shard_map/dot_general | solution.py:105
  63.2 0.5 slice_add_fusion
  63.7 0.4 concatenate.50
  64.1 0.0 copy-start
  64.1 0.0 copy-start.3
  64.1 0.4 concatenate.49
  64.5 1.5 %fusion.8 = bf16[2,256,4,256]{3,2,0,1:T(4,128)(2,1)} fusion(f32[2,256]{0,1:T(8,128)S(1)} %copy.33, f32[2,256,4,128]{3,2,1,0:T(4,128)S(1)} %concatenate.50, f32[2,256,4,128]{3,2,1,0:T(4,128)S(1)} %concatenate.49), kind=kLoop, calls=%fused_computation.16 | loop fusion | flops 1572864 | bytes 3147776 | tf_op jit(solution)/shard_map/convert_element_type | solution.py:122
  66.0 14.7 %all-to-all-start = ((bf16[2,256,4,256]{3,2,0,1:T(4,128)(2,1)}), bf16[2,256,4,256]{3,2,0,1:T(4,128)(2,1)S(1)}, u32[]{:S(2)}, u32[]{:S(2)}) async-start(bf16[2,256,4,256]{3,2,0,1:T(4,128)(2,1)} %fusion.8), calls=%async_computation | async-start | bytes 2097152 | tf_op jit(solution)/shard_map/all_to_all | solution.py:151
  80.7 0.0 copy-done
  80.7 0.2 multiply_bitcast_fusion.1
  80.9 0.0 copy-done.3
  80.9 3.2 %fusion = bf16[16,1,512]{2,1,0:T(2,128)(2,1)S(1)} fusion(s32[16,512]{1,0:T(8,128)S(1)} %copy-done.3, bf16[16,512,1]{1,0,2:T(8,128)(2,1)S(1)} %get-tuple-element.29), kind=kOutput, calls=%fused_computation.1 | convolution fusion | flops 12582912 | bytes 65536 | tf_op jit(solution)/shard_map/bk,bks->bs/dot_general | solution.py:45
  84.1 3.2 %fusion.1 = bf16[16,1,512]{2,1,0:T(2,128)(2,1)S(1)} fusion(s32[16,512]{1,0:T(8,128)S(1)} %copy-done.3, bf16[16,512,1]{1,0,2:T(8,128)(2,1)S(1)} %get-tuple-element.28), kind=kOutput, calls=%fused_computation.2 | convolution fusion | flops 12582912 | bytes 65536 | tf_op jit(solution)/shard_map/bk,bks->bs/dot_general | solution.py:44
  87.3 25.2 %all-to-all-done = bf16[2,256,4,256]{3,2,0,1:T(4,128)(2,1)S(1)} async-done(((bf16[2,256,4,256]{3,2,0,1:T(4,128)(2,1)}), bf16[2,256,4,256]{3,2,0,1:T(4,128)(2,1)S(1)}, u32[]{:S(2)}, u32[]{:S(2)}) %all-to-all-start) | async-done | bytes 1048608 | tf_op jit(solution)/shard_map/all_to_all | solution.py:151
  112.5 1.2 fusion.46
  113.7 0.1 squeeze.3
  113.8 0.8 fusion.47
  114.6 0.7 fusion.9
  115.3 1.8 %reshape.263 = bf16[512,2,256]{2,1,0:T(2,128)(2,1)S(1)} reshape(bf16[1,256,4,256]{3,2,0,1:T(4,128)(2,1)} %get-tuple-element.20) | data formatting | bytes 1048576 | tf_op jit(solution)/shard_map/reshape.4
  117.2 0.2 convolution_bitcast_fusion
  117.3 0.2 convolution_bitcast_fusion.1
  117.5 0.1 multiply_reduce_fusion
  117.7 0.7 broadcast_in_dim.2
  118.4 6.5 %all-to-all-start.1 = ((f32[256,1,16]{2,1,0:T(1,128)}), f32[256,1,16]{2,1,0:T(1,128)S(1)}, u32[]{:S(2)}, u32[]{:S(2)}) async-start(f32[256,1,16]{2,1,0:T(1,128)} %broadcast_in_dim.2), calls=%async_computation.1 | async-start | bytes 262144 | tf_op jit(solution)/shard_map/all_to_all | solution.py:162
  124.8 1.7 %fusion.10 = bf16[1,1,1024,1024]{3,2,1,0:T(8,128)(2,1)S(1)} fusion(bf16[1024,256]{1,0:T(8,128)(2,1)S(1)} %squeeze.3, bf16[1024,128]{1,0:T(8,128)(2,1)} %get-tuple-element.23, bf16[1024,128]{1,0:T(8,128)(2,1)S(1)} %get-tuple-element.22), kind=kOutput, calls=%fused_computation.18 | convolution fusion | flops 540016640 | bytes 3145728 | tf_op jit(solution)/shard_map/dot_general | solution.py:105
  126.5 2.4 %pad_maximum_fusion = bf16[1,2,1024,1024]{3,2,1,0:T(8,128)(2,1)} fusion(bf16[1,1,1024,1024]{3,2,1,0:T(8,128)(2,1)S(1)} %fusion.10, bf16[1,1,1024,1024]{3,2,1,0:T(8,128)(2,1)S(1)} %fusion.9), kind=kLoop, calls=%fused_computation.11 | loop fusion | flops 2097152 | bytes 8388608 | tf_op jit(solution)/shard_map/stack | solution.py:158
  128.9 8.3 %all-to-all-done.1 = f32[256,1,16]{2,1,0:T(1,128)S(1)} async-done(((f32[256,1,16]{2,1,0:T(1,128)}), f32[256,1,16]{2,1,0:T(1,128)S(1)}, u32[]{:S(2)}, u32[]{:S(2)}) %all-to-all-start.1) | async-done | bytes 16416 | tf_op jit(solution)/shard_map/all_to_all | solution.py:162
  137.3 0.3 reduce_sum.19
  137.6 0.1 multiply_convert_fusion.4
  137.6 0.6 copy.37
  (4 shorter events, 0.0 us)
Async XLA Ops:
  1.5 14.5 %copy-start.1 = (s32[256]{0:T(256)S(1)}, s32[256]{0:T(256)}, u32[]{:S(2)}) copy-start(s32[256]{0:T(256)} %param.11) | copy-start | bytes 3076
  1.5 14.5 %copy-start.2 = (s32[256]{0:T(256)S(1)}, s32[256]{0:T(256)}, u32[]{:S(2)}) copy-start(s32[256]{0:T(256)} %param.10) | copy-start | bytes 3076
  64.1 16.6 %copy-start = (s32[16,512]{1,0:T(8,128)S(1)}, s32[16,512]{1,0:T(8,128)}, u32[]{:S(2)}) copy-start(s32[16,512]{1,0:T(8,128)} %param.15) | copy-start | bytes 98308
  64.1 16.8 %copy-start.3 = (s32[16,512]{1,0:T(8,128)S(1)}, s32[16,512]{1,0:T(8,128)}, u32[]{:S(2)}) copy-start(s32[16,512]{1,0:T(8,128)} %param.14) | copy-start | bytes 98308
  66.0 46.5 %all-to-all-start = ((bf16[2,256,4,256]{3,2,0,1:T(4,128)(2,1)}), bf16[2,256,4,256]{3,2,0,1:T(4,128)(2,1)S(1)}, u32[]{:S(2)}, u32[]{:S(2)}) async-start(bf16[2,256,4,256]{3,2,0,1:T(4,128)(2,1)} %fusion.8), calls=%async_computation | async-start | bytes 2097152 | tf_op jit(solution)/shard_map/all_to_all | solution.py:151
  118.4 18.9 %all-to-all-start.1 = ((f32[256,1,16]{2,1,0:T(1,128)}), f32[256,1,16]{2,1,0:T(1,128)S(1)}, u32[]{:S(2)}, u32[]{:S(2)}) async-start(f32[256,1,16]{2,1,0:T(1,128)} %broadcast_in_dim.2), calls=%async_computation.1 | async-start | bytes 262144 | tf_op jit(solution)/shard_map/all_to_all | solution.py:162

commit v8 on v7

--- a/solution.py
+++ b/solution.py
@@ -46,19 +46,23 @@
     return (weight_re.astype(jnp.bfloat16), weight_im.astype(jnp.bfloat16))
 
 
-def fir_kernel(x_ref, h_ref, o_ref, xs_ref, os_ref):
-    tap_count = h_ref.shape[0]
-    frames = x_ref.shape[2]
+def fir_kernel(x_ref, h_ref, o_ref, os_ref):
+    tap_count, points = h_ref.shape
+    inputs_here = o_ref.shape[1]
     spectra = o_ref.shape[2]
     stride = 16
     depth = spectra // stride
     lanes = 128
+    frame_rows = points // lanes * inputs_here
 
-    def lane_body(lane_block, carry):
+    def lane_body(step, carry):
+        input_index = step % inputs_here
+        lane_block = step // inputs_here
         n0 = pl.multiple_of(lane_block * lanes, lanes)
-        xs_ref[pl.ds(0, frames), :] = x_ref[0, 0, :, pl.ds(n0, lanes)].astype(jnp.float32)
+        first = lane_block * inputs_here + input_index
         groups = [
-            xs_ref[pl.ds(g, depth, stride=stride), :] for g in range(stride + tap_count - 1)
+            x_ref[0, pl.ds(first + g * frame_rows, depth, stride=stride * frame_rows), :]
+            for g in range(stride + tap_count - 1)
         ]
         taps = [
             jnp.broadcast_to(h_ref[pl.ds(t, 1), pl.ds(n0, lanes)], (depth, lanes))
@@ -69,35 +73,31 @@
             for t in range(1, tap_count):
                 acc = acc + taps[t] * groups[q + t]
             os_ref[pl.ds(q, depth, stride=stride), :] = acc
-        o_ref[0, 0, :, pl.ds(n0, lanes)] = os_ref[...].astype(o_ref.dtype)
+        o_ref[0, input_index, :, pl.ds(n0, lanes)] = os_ref[...].astype(o_ref.dtype)
         return carry
 
-    lax.fori_loop(0, h_ref.shape[1] // lanes, lane_body, 0)
+    lax.fori_loop(0, points // lanes * inputs_here, lane_body, 0)
 
 
 def polyphase(in_block, fir_taps, spectra):
     tap_count, points = fir_taps.shape
-    components, inputs_here = in_block.shape[0], in_block.shape[1]
-    frames = in_block.shape[2] // points
-    framed = in_block.reshape(components, inputs_here, frames, points)
+    components, inputs_here, samples = in_block.shape
+    lanes = 128
+    rows = samples // lanes * inputs_here
+    tiles = in_block.reshape(components, inputs_here, samples // lanes, lanes)
+    tiles = jnp.transpose(tiles, (0, 2, 1, 3)).reshape(components, rows, lanes)
+    tiles = tiles.astype(jnp.float32)
     return pl.pallas_call(
         fir_kernel,
-        grid=(components * inputs_here,),
+        grid=(components,),
         in_specs=[
-            pl.BlockSpec(
-                (1, 1, frames, points), lambda r: (r // inputs_here, r % inputs_here, 0, 0)
-            ),
-            pl.BlockSpec((tap_count, points), lambda r: (0, 0)),
+            pl.BlockSpec((1, rows, lanes), lambda c: (c, 0, 0)),
+            pl.BlockSpec((tap_count, points), lambda c: (0, 0)),
         ],
-        out_specs=pl.BlockSpec(
-            (1, 1, spectra, points), lambda r: (r // inputs_here, r % inputs_here, 0, 0)
-        ),
+        out_specs=pl.BlockSpec((1, inputs_here, spectra, points), lambda c: (c, 0, 0, 0)),
         out_shape=jax.ShapeDtypeStruct((components, inputs_here, spectra, points), jnp.bfloat16),
-        scratch_shapes=[
-            pltpu.VMEM((8 * pl.cdiv(frames, 8), 128), jnp.float32),
-            pltpu.VMEM((spectra, 128), jnp.float32),
-        ],
-    )(framed, fir_taps)
+        scratch_shapes=[pltpu.VMEM((spectra, lanes), jnp.float32)],
+    )(tiles, fir_taps)
 
 
 def contract(left_rows, right_rows):

time: 140 us -> 160 us (1.14)
  Pallas kernels: 27.2 us -> 51.9 us
  local copies, waits for them, and re-layouts: 19.8 us -> 5.34 us
  other arithmetic: 12.9 us -> 22.9 us
    pallas_call x1, Pallas kernels: 27.2 us -> 51.9 us  [polyphase(): pl.pallas_call(fir_kernel, grid=(components,), in_specs=[pl.BlockSpec((1,...]
    reshape x1 -> x0, local copies, waits for them, and re-layouts: 14.5 us -> none  [polyphase(): framed = in_block.reshape(components, inputs_here, frames, points)]
    convert_element_type x0 -> x1, other arithmetic: none -> 10.1 us  [polyphase(): tiles = tiles.astype(jnp.float32)]
  transfers between devices with their start and end apart: 2 -> 2, of which waited for: 2 -> 2; matrix products, arithmetic and copies ran while one was open for 8% -> 7% of each run, Pallas kernels for 0% -> 0%
where the time goes in v8:
time: 160 us; the launch traced here: 159 us
  Pallas kernels  51.9 us (32%)
  waiting for transfers between devices  33.6 us (21%)
  other arithmetic  22.9 us (14%)
  matrix products  22.9 us (14%)
  starting transfers between devices  21.2 us (13%)
  local copies, waits for them, and re-layouts  5.34 us (3%)
    pallas_call x1, Pallas kernels, polyphase(): pl.pallas_call(fir_kernel, grid=(components,), in_specs=[pl.BlockSpec((1,...  51.9 us
    all_to_all x1, waiting for transfers between devices, per_device(): lax.all_to_all(outgoing, ALL_AXES, split_axis=1, concat_axis=1, tiled=True)  25.2 us
    dot_general x3, matrix products, contract(): lax.dot_general(left_rows, right_rows, contract_dims, preferred_element_t...  16.1 us
    all_to_all x1, starting transfers between devices, per_device(): lax.all_to_all(outgoing, ALL_AXES, split_axis=1, concat_axis=1, tiled=True)  14.7 us
    convert_element_type x1, other arithmetic, polyphase(): tiles = tiles.astype(jnp.float32)  10.1 us
    all_to_all x1, waiting for transfers between devices, per_device(): lax.all_to_all(spread_power, ALL_AXES, split_axis=0, concat_axis=0, tiled...  8.34 us
    all_to_all x1, starting transfers between devices, per_device(): lax.all_to_all(spread_power, ALL_AXES, split_axis=0, concat_axis=0, tiled...  6.46 us
    convert_element_type x1, other arithmetic, make_tables(): sin_table = ((sa * cb + ca * sb) * table_scale).astype(jnp.bfloat16)  5.31 us
  transfers between devices with their start and end apart: 2, of which 2 were waited for; matrix products, arithmetic and copies ran while one was open for 7% of the time, Pallas kernels for 0%

profile of v8, /device:TPU:2, one launch (start us, length us, event | category | flops | bytes accessed | tf_op | source)
XLA Modules:
  0.0 158.6 jit_solution(908056953871258668)
XLA Ops:
  0.6 0.7 pad_maximum_fusion.3
  1.3 0.1 copy.39
  1.5 0.0 copy-start.1
  1.5 0.0 copy-start.2
  1.5 10.1 %bitcast_convert_fusion = f32[2,4,4448,128]{3,1,2,0:T(4,128)} fusion(bf16[2,4,569344]{2,1,0:T(4,128)(2,1)} %param.8), kind=kLoop, calls=%fused_computation.3 | loop fusion | flops 4554752 | bytes 27328512 | tf_op jit(solution)/shard_map/convert_element_type | solution.py:89
  11.6 0.0 copy-done.1
  11.6 0.0 copy-done.2
  11.6 1.0 fusion.31
  12.6 5.3 %multiply_convert_fusion = (bf16[512,64,64]{0,2,1:T(8,128)(2,1)}, bf16[512,64,64]{0,2,1:T(8,128)(2,1)}) fusion(f32[512,64]{0,1:T(8,128)S(1)} %get-tuple-element.32, f32[512,64]{0,1:T(8,128)S(1)} %get-tuple-element.31, f32[512,64]{0,1:T(8,128)S(1)} %get-tuple-element.33, f32[512,64]{0,1:T(8,128)S(1)} %get-tuple-element.30), kind=kLoop, calls=%fused_computation.10 | loop fusion | flops 20971520 | bytes 8912896 | tf_op jit(solution)/shard_map/convert_element_type | solution.py:34
  18.0 51.9 %shard_map.95 = bf16[2,4,128,4096]{3,2,1,0:T(8,128)(2,1)} custom-call(f32[2,17792,128]{2,1,0:T(8,128)} %bitcast.49, f32[12,4096]{1,0:T(8,128)} %h_ref.1), custom_call_target="tpu_custom_call" | custom-call | tf_op jit(solution)/shard_map/pallas_call | solution.py:90
  69.8 13.7 %fusion.2 = f32[1024,1024]{1,0:T(8,128)S(1)} fusion(bf16[1024,4096]{1,0:T(8,128)(2,1)} %bitcast.50, bf16[512,4096]{0,1:T(8,128)(2,1)} %bitcast.51, bf16[512,4096]{0,1:T(8,128)(2,1)} %bitcast.52), kind=kOutput, calls=%fused_computation.4 | convolution fusion | flops 8606711808 | bytes 20971520 | tf_op jit(solution)/shard_map/dot_general | solution.py:105
  83.5 0.5 slice_add_fusion
  84.0 0.4 concatenate.50
  84.4 0.0 copy-start
  84.4 0.0 copy-start.3
  84.4 0.4 concatenate.49
  84.8 1.5 fusion.8
  86.3 14.7 %all-to-all-start = ((bf16[2,256,4,256]{3,2,0,1:T(4,128)(2,1)}), bf16[2,256,4,256]{3,2,0,1:T(4,128)(2,1)S(1)}, u32[]{:S(2)}, u32[]{:S(2)}) async-start(bf16[2,256,4,256]{3,2,0,1:T(4,128)(2,1)} %fusion.8), calls=%async_computation | async-start | bytes 2097152 | tf_op jit(solution)/shard_map/all_to_all | solution.py:151
  101.0 0.0 copy-done
  101.0 0.2 multiply_bitcast_fusion.1
  101.2 0.0 copy-done.3
  101.2 3.2 %fusion = bf16[16,1,512]{2,1,0:T(2,128)(2,1)S(1)} fusion(s32[16,512]{1,0:T(8,128)S(1)} %copy-done.3, bf16[16,512,1]{1,0,2:T(8,128)(2,1)S(1)} %get-tuple-element.29), kind=kOutput, calls=%fused_computation.1 | convolution fusion | flops 12582912 | bytes 65536 | tf_op jit(solution)/shard_map/bk,bks->bs/dot_general | solution.py:45
  104.4 3.2 %fusion.1 = bf16[16,1,512]{2,1,0:T(2,128)(2,1)S(1)} fusion(s32[16,512]{1,0:T(8,128)S(1)} %copy-done.3, bf16[16,512,1]{1,0,2:T(8,128)(2,1)S(1)} %get-tuple-element.28), kind=kOutput, calls=%fused_computation.2 | convolution fusion | flops 12582912 | bytes 65536 | tf_op jit(solution)/shard_map/bk,bks->bs/dot_general | solution.py:44
  107.6 25.2 %all-to-all-done = bf16[2,256,4,256]{3,2,0,1:T(4,128)(2,1)S(1)} async-done(((bf16[2,256,4,256]{3,2,0,1:T(4,128)(2,1)}), bf16[2,256,4,256]{3,2,0,1:T(4,128)(2,1)S(1)}, u32[]{:S(2)}, u32[]{:S(2)}) %all-to-all-start) | async-done | bytes 1048608 | tf_op jit(solution)/shard_map/all_to_all | solution.py:151
  132.8 1.2 fusion.46
  134.0 0.1 squeeze.3
  134.1 0.8 fusion.47
  134.9 0.7 fusion.9
  135.6 1.8 %reshape.265 = bf16[512,2,256]{2,1,0:T(2,128)(2,1)S(1)} reshape(bf16[1,256,4,256]{3,2,0,1:T(4,128)(2,1)} %get-tuple-element.20) | data formatting | bytes 1048576 | tf_op jit(solution)/shard_map/reshape.4
  137.4 0.2 convolution_bitcast_fusion
  137.6 0.2 convolution_bitcast_fusion.1
  137.8 0.1 multiply_reduce_fusion
  137.9 0.7 broadcast_in_dim.2
  138.7 6.5 %all-to-all-start.1 = ((f32[256,1,16]{2,1,0:T(1,128)}), f32[256,1,16]{2,1,0:T(1,128)S(1)}, u32[]{:S(2)}, u32[]{:S(2)}) async-start(f32[256,1,16]{2,1,0:T(1,128)} %broadcast_in_dim.2), calls=%async_computation.1 | async-start | bytes 262144 | tf_op jit(solution)/shard_map/all_to_all | solution.py:162
  145.1 1.7 %fusion.10 = bf16[1,1,1024,1024]{3,2,1,0:T(8,128)(2,1)S(1)} fusion(bf16[1024,256]{1,0:T(8,128)(2,1)S(1)} %squeeze.3, bf16[1024,128]{1,0:T(8,128)(2,1)} %get-tuple-element.23, bf16[1024,128]{1,0:T(8,128)(2,1)S(1)} %get-tuple-element.22), kind=kOutput, calls=%fused_computation.19 | convolution fusion | flops 540016640 | bytes 3145728 | tf_op jit(solution)/shard_map/dot_general | solution.py:105
  146.8 2.4 %pad_maximum_fusion = bf16[1,2,1024,1024]{3,2,1,0:T(8,128)(2,1)} fusion(bf16[1,1,1024,1024]{3,2,1,0:T(8,128)(2,1)S(1)} %fusion.10, bf16[1,1,1024,1024]{3,2,1,0:T(8,128)(2,1)S(1)} %fusion.9), kind=kLoop, calls=%fused_computation.12 | loop fusion | flops 2097152 | bytes 8388608 | tf_op jit(solution)/shard_map/stack | solution.py:158
  149.2 8.3 %all-to-all-done.1 = f32[256,1,16]{2,1,0:T(1,128)S(1)} async-done(((f32[256,1,16]{2,1,0:T(1,128)}), f32[256,1,16]{2,1,0:T(1,128)S(1)}, u32[]{:S(2)}, u32[]{:S(2)}) %all-to-all-start.1) | async-done | bytes 16416 | tf_op jit(solution)/shard_map/all_to_all | solution.py:162
  157.6 0.3 reduce_sum.19
  157.9 0.1 multiply_convert_fusion.4
  157.9 0.6 copy.43
  (4 shorter events, 0.0 us)
Async XLA Ops:
  1.5 10.1 %copy-start.1 = (s32[256]{0:T(256)S(1)}, s32[256]{0:T(256)}, u32[]{:S(2)}) copy-start(s32[256]{0:T(256)} %param.11) | copy-start | bytes 3076
  1.5 10.1 %copy-start.2 = (s32[256]{0:T(256)S(1)}, s32[256]{0:T(256)}, u32[]{:S(2)}) copy-start(s32[256]{0:T(256)} %param.10) | copy-start | bytes 3076
  84.4 16.6 %copy-start = (s32[16,512]{1,0:T(8,128)S(1)}, s32[16,512]{1,0:T(8,128)}, u32[]{:S(2)}) copy-start(s32[16,512]{1,0:T(8,128)} %param.15) | copy-start | bytes 98308
  84.4 16.8 %copy-start.3 = (s32[16,512]{1,0:T(8,128)S(1)}, s32[16,512]{1,0:T(8,128)}, u32[]{:S(2)}) copy-start(s32[16,512]{1,0:T(8,128)} %param.14) | copy-start | bytes 98308
  86.3 46.5 %all-to-all-start = ((bf16[2,256,4,256]{3,2,0,1:T(4,128)(2,1)}), bf16[2,256,4,256]{3,2,0,1:T(4,128)(2,1)S(1)}, u32[]{:S(2)}, u32[]{:S(2)}) async-start(bf16[2,256,4,256]{3,2,0,1:T(4,128)(2,1)} %fusion.8), calls=%async_computation | async-start | bytes 2097152 | tf_op jit(solution)/shard_map/all_to_all | solution.py:151
  138.7 18.9 %all-to-all-start.1 = ((f32[256,1,16]{2,1,0:T(1,128)}), f32[256,1,16]{2,1,0:T(1,128)S(1)}, u32[]{:S(2)}, u32[]{:S(2)}) async-start(f32[256,1,16]{2,1,0:T(1,128)} %broadcast_in_dim.2), calls=%async_computation.1 | async-start | bytes 262144 | tf_op jit(solution)/shard_map/all_to_all | solution.py:162

commit v9 on v8

--- a/solution.py
+++ b/solution.py
@@ -47,56 +47,53 @@
 
 
 def fir_kernel(x_ref, h_ref, o_ref, os_ref):
-    tap_count, points = h_ref.shape
+    tap_count = h_ref.shape[0]
+    blocks, rows, lanes = x_ref.shape[1], x_ref.shape[2], x_ref.shape[3]
     inputs_here = o_ref.shape[1]
     spectra = o_ref.shape[2]
-    stride = 16
-    depth = spectra // stride
-    lanes = 128
-    frame_rows = points // lanes * inputs_here
-
-    def lane_body(step, carry):
-        input_index = step % inputs_here
-        lane_block = step // inputs_here
-        n0 = pl.multiple_of(lane_block * lanes, lanes)
-        first = lane_block * inputs_here + input_index
-        groups = [
-            x_ref[0, pl.ds(first + g * frame_rows, depth, stride=stride * frame_rows), :]
-            for g in range(stride + tap_count - 1)
-        ]
+    for block in range(blocks):
         taps = [
-            jnp.broadcast_to(h_ref[pl.ds(t, 1), pl.ds(n0, lanes)], (depth, lanes))
+            jnp.broadcast_to(h_ref[pl.ds(t, 1), pl.ds(block * lanes, lanes)], (rows, lanes))
             for t in range(tap_count)
         ]
-        for q in range(stride):
-            acc = taps[0] * groups[q]
+
+        def frame_body(s, carry):
+            acc = taps[0] * x_ref[s, block]
             for t in range(1, tap_count):
-                acc = acc + taps[t] * groups[q + t]
-            os_ref[pl.ds(q, depth, stride=stride), :] = acc
-        o_ref[0, input_index, :, pl.ds(n0, lanes)] = os_ref[...].astype(o_ref.dtype)
-        return carry
+                acc = acc + taps[t] * x_ref[s + t, block]
+            os_ref[pl.ds(s, rows, stride=spectra), :] = acc
+            return carry
 
-    lax.fori_loop(0, points // lanes * inputs_here, lane_body, 0)
+        lax.fori_loop(0, spectra, frame_body, 0, unroll=8)
+        for r in range(rows):
+            o_ref[r // inputs_here, r % inputs_here, :, pl.ds(block * lanes, lanes)] = os_ref[
+                pl.ds(r * spectra, spectra), :
+            ].astype(o_ref.dtype)
 
 
 def polyphase(in_block, fir_taps, spectra):
     tap_count, points = fir_taps.shape
     components, inputs_here, samples = in_block.shape
+    rows = components * inputs_here
     lanes = 128
-    rows = samples // lanes * inputs_here
+    frames = samples // points
+    per_frame = points // lanes
     tiles = in_block.reshape(components, inputs_here, samples // lanes, lanes)
-    tiles = jnp.transpose(tiles, (0, 2, 1, 3)).reshape(components, rows, lanes)
-    tiles = tiles.astype(jnp.float32)
+    tiles = jnp.transpose(tiles, (2, 0, 1, 3)).astype(jnp.float32)
+    tiles = tiles.reshape(frames, per_frame, rows, lanes)
+    blocks = 4
     return pl.pallas_call(
         fir_kernel,
-        grid=(components,),
+        grid=(per_frame // blocks,),
         in_specs=[
-            pl.BlockSpec((1, rows, lanes), lambda c: (c, 0, 0)),
-            pl.BlockSpec((tap_count, points), lambda c: (0, 0)),
+            pl.BlockSpec((frames, blocks, rows, lanes), lambda b: (0, b, 0, 0)),
+            pl.BlockSpec((tap_count, blocks * lanes), lambda b: (0, b)),
         ],
-        out_specs=pl.BlockSpec((1, inputs_here, spectra, points), lambda c: (c, 0, 0, 0)),
+        out_specs=pl.BlockSpec(
+            (components, inputs_here, spectra, blocks * lanes), lambda b: (0, 0, 0, b)
+        ),
         out_shape=jax.ShapeDtypeStruct((components, inputs_here, spectra, points), jnp.bfloat16),
-        scratch_shapes=[pltpu.VMEM((spectra, lanes), jnp.float32)],
+        scratch_shapes=[pltpu.VMEM((rows * spectra, lanes), jnp.float32)],
     )(tiles, fir_taps)
 
 

time: 160 us -> 132 us (0.82)
  Pallas kernels: 51.9 us -> 23.3 us
    pallas_call x1, Pallas kernels: 51.9 us -> 23.3 us  [polyphase(): pl.pallas_call(fir_kernel, grid=(per_frame // blocks,), in_specs=[pl.Bloc...]
    convert_element_type x1 -> x0, other arithmetic: 10.1 us -> none  [polyphase(): tiles = tiles.astype(jnp.float32)]
    reshape x0 -> x1, other arithmetic: none -> 10.1 us  [polyphase(): tiles = tiles.reshape(frames, per_frame, rows, lanes)]
  transfers between devices with their start and end apart: 2 -> 2, of which waited for: 2 -> 2; matrix products, arithmetic and copies ran while one was open for 7% -> 8% of each run, Pallas kernels for 0% -> 0%
where the time goes in v9:
time: 132 us; the launch traced here: 130 us
  waiting for transfers between devices  33.6 us (25%)
  Pallas kernels  23.3 us (18%)
  other arithmetic  22.9 us (17%)
  matrix products  22.9 us (17%)
  starting transfers between devices  21.2 us (16%)
  local copies, waits for them, and re-layouts  5.34 us (4%)
    all_to_all x1, waiting for transfers between devices, per_device(): lax.all_to_all(outgoing, ALL_AXES, split_axis=1, concat_axis=1, tiled=True)  25.2 us
    pallas_call x1, Pallas kernels, polyphase(): pl.pallas_call(fir_kernel, grid=(per_frame // blocks,), in_specs=[pl.Bloc...  23.3 us
    dot_general x3, matrix products, contract(): lax.dot_general(left_rows, right_rows, contract_dims, preferred_element_t...  16.1 us
    all_to_all x1, starting transfers between devices, per_device(): lax.all_to_all(outgoing, ALL_AXES, split_axis=1, concat_axis=1, tiled=True)  14.7 us
    reshape x1, other arithmetic, polyphase(): tiles = tiles.reshape(frames, per_frame, rows, lanes)  10.1 us
    all_to_all x1, waiting for transfers between devices, per_device(): lax.all_to_all(spread_power, ALL_AXES, split_axis=0, concat_axis=0, tiled...  8.34 us
    all_to_all x1, starting transfers between devices, per_device(): lax.all_to_all(spread_power, ALL_AXES, split_axis=0, concat_axis=0, tiled...  6.47 us
    convert_element_type x1, other arithmetic, make_tables(): sin_table = ((sa * cb + ca * sb) * table_scale).astype(jnp.bfloat16)  5.31 us
  transfers between devices with their start and end apart: 2, of which 2 were waited for; matrix products, arithmetic and copies ran while one was open for 8% of the time, Pallas kernels for 0%

profile of v9, /device:TPU:2, one launch (start us, length us, event | category | flops | bytes accessed | tf_op | source)
XLA Modules:
  0.0 129.9 jit_solution(3623454930243058151)
XLA Ops:
  0.6 0.7 pad_maximum_fusion.3
  1.3 0.1 copy.39
  1.5 0.0 copy-start.1
  1.5 0.0 copy-start.2
  1.5 10.1 %copy_bitcast_fusion = f32[2,4,4448,128]{3,1,0,2:T(4,128)} fusion(bf16[2,4,569344]{2,1,0:T(4,128)(2,1)} %param.8), kind=kLoop, calls=%fused_computation | loop fusion | flops 4554752 | bytes 27328512 | tf_op jit(solution)/shard_map/reshape | solution.py:83
  11.6 0.0 copy-done.1
  11.6 0.0 copy-done.2
  11.6 1.0 fusion.31
  12.6 5.3 %multiply_convert_fusion = (bf16[512,64,64]{0,2,1:T(8,128)(2,1)}, bf16[512,64,64]{0,2,1:T(8,128)(2,1)}) fusion(f32[512,64]{0,1:T(8,128)S(1)} %get-tuple-element.32, f32[512,64]{0,1:T(8,128)S(1)} %get-tuple-element.31, f32[512,64]{0,1:T(8,128)S(1)} %get-tuple-element.33, f32[512,64]{0,1:T(8,128)S(1)} %get-tuple-element.30), kind=kLoop, calls=%fused_computation.11 | loop fusion | flops 20971520 | bytes 8912896 | tf_op jit(solution)/shard_map/convert_element_type | solution.py:34
  17.9 23.3 %shard_map.95 = bf16[2,4,128,4096]{3,2,1,0:T(8,128)(2,1)} custom-call(f32[139,32,8,128]{3,2,1,0:T(8,128)} %bitcast.51, f32[12,4096]{1,0:T(8,128)} %h_ref.1), custom_call_target="tpu_custom_call" | custom-call | tf_op jit(solution)/shard_map/pallas_call | solution.py:85
  41.2 13.7 %fusion.2 = f32[1024,1024]{1,0:T(8,128)S(1)} fusion(bf16[1024,4096]{1,0:T(8,128)(2,1)} %bitcast.52, bf16[512,4096]{0,1:T(8,128)(2,1)} %bitcast.53, bf16[512,4096]{0,1:T(8,128)(2,1)} %bitcast.54), kind=kOutput, calls=%fused_computation.5 | convolution fusion | flops 8606711808 | bytes 20971520 | tf_op jit(solution)/shard_map/dot_general | solution.py:102
  54.9 0.5 slice_add_fusion
  55.4 0.4 concatenate.50
  55.7 0.0 copy-start
  55.7 0.0 copy-start.3
  55.8 0.4 concatenate.49
  56.1 1.5 %fusion.8 = bf16[2,256,4,256]{3,2,0,1:T(4,128)(2,1)} fusion(f32[2,256]{0,1:T(8,128)S(1)} %copy.39, f32[2,256,4,128]{3,2,1,0:T(4,128)S(1)} %concatenate.50, f32[2,256,4,128]{3,2,1,0:T(4,128)S(1)} %concatenate.49), kind=kLoop, calls=%fused_computation.18 | loop fusion | flops 1572864 | bytes 3147776 | tf_op jit(solution)/shard_map/convert_element_type | solution.py:119
  57.6 14.7 %all-to-all-start = ((bf16[2,256,4,256]{3,2,0,1:T(4,128)(2,1)}), bf16[2,256,4,256]{3,2,0,1:T(4,128)(2,1)S(1)}, u32[]{:S(2)}, u32[]{:S(2)}) async-start(bf16[2,256,4,256]{3,2,0,1:T(4,128)(2,1)} %fusion.8), calls=%async_computation | async-start | bytes 2097152 | tf_op jit(solution)/shard_map/all_to_all | solution.py:148
  72.3 0.0 copy-done
  72.3 0.2 multiply_bitcast_fusion.1
  72.5 0.0 copy-done.3
  72.5 3.2 %fusion = bf16[16,1,512]{2,1,0:T(2,128)(2,1)S(1)} fusion(s32[16,512]{1,0:T(8,128)S(1)} %copy-done.3, bf16[16,512,1]{1,0,2:T(8,128)(2,1)S(1)} %get-tuple-element.29), kind=kOutput, calls=%fused_computation.3 | convolution fusion | flops 12582912 | bytes 65536 | tf_op jit(solution)/shard_map/bk,bks->bs/dot_general | solution.py:45
  75.7 3.2 %fusion.1 = bf16[16,1,512]{2,1,0:T(2,128)(2,1)S(1)} fusion(s32[16,512]{1,0:T(8,128)S(1)} %copy-done.3, bf16[16,512,1]{1,0,2:T(8,128)(2,1)S(1)} %get-tuple-element.28), kind=kOutput, calls=%fused_computation.4 | convolution fusion | flops 12582912 | bytes 65536 | tf_op jit(solution)/shard_map/bk,bks->bs/dot_general | solution.py:44
  79.0 25.2 %all-to-all-done = bf16[2,256,4,256]{3,2,0,1:T(4,128)(2,1)S(1)} async-done(((bf16[2,256,4,256]{3,2,0,1:T(4,128)(2,1)}), bf16[2,256,4,256]{3,2,0,1:T(4,128)(2,1)S(1)}, u32[]{:S(2)}, u32[]{:S(2)}) %all-to-all-start) | async-done | bytes 1048608 | tf_op jit(solution)/shard_map/all_to_all | solution.py:148
  104.2 1.2 fusion.46
  105.3 0.1 squeeze.3
  105.5 0.8 fusion.47
  106.2 0.7 fusion.9
  107.0 1.8 %reshape.269 = bf16[512,2,256]{2,1,0:T(2,128)(2,1)S(1)} reshape(bf16[1,256,4,256]{3,2,0,1:T(4,128)(2,1)} %get-tuple-element.20) | data formatting | bytes 1048576 | tf_op jit(solution)/shard_map/reshape.4
  108.8 0.2 convolution_bitcast_fusion
  109.0 0.2 convolution_bitcast_fusion.1
  109.2 0.1 multiply_reduce_fusion
  109.3 0.7 broadcast_in_dim.2
  110.0 6.5 %all-to-all-start.1 = ((f32[256,1,16]{2,1,0:T(1,128)}), f32[256,1,16]{2,1,0:T(1,128)S(1)}, u32[]{:S(2)}, u32[]{:S(2)}) async-start(f32[256,1,16]{2,1,0:T(1,128)} %broadcast_in_dim.2), calls=%async_computation.1 | async-start | bytes 262144 | tf_op jit(solution)/shard_map/all_to_all | solution.py:159
  116.5 1.7 %fusion.10 = bf16[1,1,1024,1024]{3,2,1,0:T(8,128)(2,1)S(1)} fusion(bf16[1024,256]{1,0:T(8,128)(2,1)S(1)} %squeeze.3, bf16[1024,128]{1,0:T(8,128)(2,1)} %get-tuple-element.23, bf16[1024,128]{1,0:T(8,128)(2,1)S(1)} %get-tuple-element.22), kind=kOutput, calls=%fused_computation.20 | convolution fusion | flops 540016640 | bytes 3145728 | tf_op jit(solution)/shard_map/dot_general | solution.py:102
  118.2 2.4 %pad_maximum_fusion = bf16[1,2,1024,1024]{3,2,1,0:T(8,128)(2,1)} fusion(bf16[1,1,1024,1024]{3,2,1,0:T(8,128)(2,1)S(1)} %fusion.10, bf16[1,1,1024,1024]{3,2,1,0:T(8,128)(2,1)S(1)} %fusion.9), kind=kLoop, calls=%fused_computation.13 | loop fusion | flops 2097152 | bytes 8388608 | tf_op jit(solution)/shard_map/stack | solution.py:155
  120.6 8.3 %all-to-all-done.1 = f32[256,1,16]{2,1,0:T(1,128)S(1)} async-done(((f32[256,1,16]{2,1,0:T(1,128)}), f32[256,1,16]{2,1,0:T(1,128)S(1)}, u32[]{:S(2)}, u32[]{:S(2)}) %all-to-all-start.1) | async-done | bytes 16416 | tf_op jit(solution)/shard_map/all_to_all | solution.py:159
  128.9 0.3 reduce_sum.19
  129.2 0.1 multiply_convert_fusion.4
  129.3 0.6 copy.43
  (4 shorter events, 0.0 us)
Async XLA Ops:
  1.5 10.1 %copy-start.1 = (s32[256]{0:T(256)S(1)}, s32[256]{0:T(256)}, u32[]{:S(2)}) copy-start(s32[256]{0:T(256)} %param.11) | copy-start | bytes 3076
  1.5 10.1 %copy-start.2 = (s32[256]{0:T(256)S(1)}, s32[256]{0:T(256)}, u32[]{:S(2)}) copy-start(s32[256]{0:T(256)} %param.10) | copy-start | bytes 3076
  55.7 16.6 %copy-start = (s32[16,512]{1,0:T(8,128)S(1)}, s32[16,512]{1,0:T(8,128)}, u32[]{:S(2)}) copy-start(s32[16,512]{1,0:T(8,128)} %param.15) | copy-start | bytes 98308
  55.7 16.8 %copy-start.3 = (s32[16,512]{1,0:T(8,128)S(1)}, s32[16,512]{1,0:T(8,128)}, u32[]{:S(2)}) copy-start(s32[16,512]{1,0:T(8,128)} %param.14) | copy-start | bytes 98308
  57.6 46.5 %all-to-all-start = ((bf16[2,256,4,256]{3,2,0,1:T(4,128)(2,1)}), bf16[2,256,4,256]{3,2,0,1:T(4,128)(2,1)S(1)}, u32[]{:S(2)}, u32[]{:S(2)}) async-start(bf16[2,256,4,256]{3,2,0,1:T(4,128)(2,1)} %fusion.8), calls=%async_computation | async-start | bytes 2097152 | tf_op jit(solution)/shard_map/all_to_all | solution.py:148
  110.0 18.9 %all-to-all-start.1 = ((f32[256,1,16]{2,1,0:T(1,128)}), f32[256,1,16]{2,1,0:T(1,128)S(1)}, u32[]{:S(2)}, u32[]{:S(2)}) async-start(f32[256,1,16]{2,1,0:T(1,128)} %broadcast_in_dim.2), calls=%async_computation.1 | async-start | bytes 262144 | tf_op jit(solution)/shard_map/all_to_all | solution.py:159

commit v10 on v9

--- a/solution.py
+++ b/solution.py
@@ -15,6 +15,7 @@
 STN_AXES = ("y", "z", "core")
 PHYSICAL_AXES = ("core", "x", "y", "z")
 ALL_AXES = ("y", "z", "core", "x")
+FRAME_GROUP = 8
 
 
 def make_tables(channel_of, points):
@@ -57,14 +58,17 @@
             for t in range(tap_count)
         ]
 
-        def frame_body(s, carry):
-            acc = taps[0] * x_ref[s, block]
-            for t in range(1, tap_count):
-                acc = acc + taps[t] * x_ref[s + t, block]
-            os_ref[pl.ds(s, rows, stride=spectra), :] = acc
+        def frame_body(step, carry):
+            first = pl.multiple_of(step * FRAME_GROUP, FRAME_GROUP)
+            window = [x_ref[first + f, block] for f in range(FRAME_GROUP + tap_count - 1)]
+            for k in range(FRAME_GROUP):
+                acc = taps[0] * window[k]
+                for t in range(1, tap_count):
+                    acc = acc + taps[t] * window[k + t]
+                os_ref[pl.ds(first + k, rows, stride=spectra), :] = acc
             return carry
 
-        lax.fori_loop(0, spectra, frame_body, 0, unroll=8)
+        lax.fori_loop(0, spectra // FRAME_GROUP, frame_body, 0)
         for r in range(rows):
             o_ref[r // inputs_here, r % inputs_here, :, pl.ds(block * lanes, lanes)] = os_ref[
                 pl.ds(r * spectra, spectra), :

time: 132 us -> 132 us (level)
  no operation moved by 1% of the time
where the time goes in v10:
time: 132 us; the launch traced here: 130 us
  waiting for transfers between devices  33.6 us (25%)
  Pallas kernels  23.3 us (18%)
  other arithmetic  22.9 us (17%)
  matrix products  22.9 us (17%)
  starting transfers between devices  21.2 us (16%)
  local copies, waits for them, and re-layouts  5.34 us (4%)
    all_to_all x1, waiting for transfers between devices, per_device(): lax.all_to_all(outgoing, ALL_AXES, split_axis=1, concat_axis=1, tiled=True)  25.2 us
    pallas_call x1, Pallas kernels, polyphase(): pl.pallas_call(fir_kernel, grid=(per_frame // blocks,), in_specs=[pl.Bloc...  23.3 us
    dot_general x3, matrix products, contract(): lax.dot_general(left_rows, right_rows, contract_dims, preferred_element_t...  16.1 us
    all_to_all x1, starting transfers between devices, per_device(): lax.all_to_all(outgoing, ALL_AXES, split_axis=1, concat_axis=1, tiled=True)  14.7 us
    reshape x1, other arithmetic, polyphase(): tiles = tiles.reshape(frames, per_frame, rows, lanes)  10.1 us
    all_to_all x1, waiting for transfers between devices, per_device(): lax.all_to_all(spread_power, ALL_AXES, split_axis=0, concat_axis=0, tiled...  8.34 us
    all_to_all x1, starting transfers between devices, per_device(): lax.all_to_all(spread_power, ALL_AXES, split_axis=0, concat_axis=0, tiled...  6.47 us
    convert_element_type x1, other arithmetic, make_tables(): sin_table = ((sa * cb + ca * sb) * table_scale).astype(jnp.bfloat16)  5.31 us
  transfers between devices with their start and end apart: 2, of which 2 were waited for; matrix products, arithmetic and copies ran while one was open for 8% of the time, Pallas kernels for 0%

profile of v10, /device:TPU:2, one launch (start us, length us, event | category | flops | bytes accessed | tf_op | source)
XLA Modules:
  0.0 129.9 jit_solution(8925881054807024192)
XLA Ops:
  0.6 0.7 pad_maximum_fusion.3
  1.3 0.1 copy.39
  1.5 0.0 copy-start.1
  1.5 0.0 copy-start.2
  1.5 10.1 %copy_bitcast_fusion = f32[2,4,4448,128]{3,1,0,2:T(4,128)} fusion(bf16[2,4,569344]{2,1,0:T(4,128)(2,1)} %param.8), kind=kLoop, calls=%fused_computation | loop fusion | flops 4554752 | bytes 27328512 | tf_op jit(solution)/shard_map/reshape | solution.py:87
  11.6 0.0 copy-done.1
  11.6 0.0 copy-done.2
  11.6 1.0 fusion.31
  12.6 5.3 %multiply_convert_fusion = (bf16[512,64,64]{0,2,1:T(8,128)(2,1)}, bf16[512,64,64]{0,2,1:T(8,128)(2,1)}) fusion(f32[512,64]{0,1:T(8,128)S(1)} %get-tuple-element.32, f32[512,64]{0,1:T(8,128)S(1)} %get-tuple-element.31, f32[512,64]{0,1:T(8,128)S(1)} %get-tuple-element.33, f32[512,64]{0,1:T(8,128)S(1)} %get-tuple-element.30), kind=kLoop, calls=%fused_computation.11 | loop fusion | flops 20971520 | bytes 8912896 | tf_op jit(solution)/shard_map/convert_element_type | solution.py:35
  17.9 23.3 %shard_map.95 = bf16[2,4,128,4096]{3,2,1,0:T(8,128)(2,1)} custom-call(f32[139,32,8,128]{3,2,1,0:T(8,128)} %bitcast.51, f32[12,4096]{1,0:T(8,128)} %h_ref.1), custom_call_target="tpu_custom_call" | custom-call | tf_op jit(solution)/shard_map/pallas_call | solution.py:89
  41.2 13.7 %fusion.2 = f32[1024,1024]{1,0:T(8,128)S(1)} fusion(bf16[1024,4096]{1,0:T(8,128)(2,1)} %bitcast.52, bf16[512,4096]{0,1:T(8,128)(2,1)} %bitcast.53, bf16[512,4096]{0,1:T(8,128)(2,1)} %bitcast.54), kind=kOutput, calls=%fused_computation.5 | convolution fusion | flops 8606711808 | bytes 20971520 | tf_op jit(solution)/shard_map/dot_general | solution.py:106
  54.9 0.5 slice_add_fusion
  55.4 0.4 concatenate.50
  55.7 0.0 copy-start
  55.7 0.0 copy-start.3
  55.8 0.4 concatenate.49
  56.1 1.5 %fusion.8 = bf16[2,256,4,256]{3,2,0,1:T(4,128)(2,1)} fusion(f32[2,256]{0,1:T(8,128)S(1)} %copy.39, f32[2,256,4,128]{3,2,1,0:T(4,128)S(1)} %concatenate.50, f32[2,256,4,128]{3,2,1,0:T(4,128)S(1)} %concatenate.49), kind=kLoop, calls=%fused_computation.18 | loop fusion | flops 1572864 | bytes 3147776 | tf_op jit(solution)/shard_map/convert_element_type | solution.py:123
  57.6 14.7 %all-to-all-start = ((bf16[2,256,4,256]{3,2,0,1:T(4,128)(2,1)}), bf16[2,256,4,256]{3,2,0,1:T(4,128)(2,1)S(1)}, u32[]{:S(2)}, u32[]{:S(2)}) async-start(bf16[2,256,4,256]{3,2,0,1:T(4,128)(2,1)} %fusion.8), calls=%async_computation | async-start | bytes 2097152 | tf_op jit(solution)/shard_map/all_to_all | solution.py:152
  72.3 0.0 copy-done
  72.3 0.2 multiply_bitcast_fusion.1
  72.5 0.0 copy-done.3
  72.5 3.2 %fusion = bf16[16,1,512]{2,1,0:T(2,128)(2,1)S(1)} fusion(s32[16,512]{1,0:T(8,128)S(1)} %copy-done.3, bf16[16,512,1]{1,0,2:T(8,128)(2,1)S(1)} %get-tuple-element.29), kind=kOutput, calls=%fused_computation.3 | convolution fusion | flops 12582912 | bytes 65536 | tf_op jit(solution)/shard_map/bk,bks->bs/dot_general | solution.py:46
  75.7 3.2 %fusion.1 = bf16[16,1,512]{2,1,0:T(2,128)(2,1)S(1)} fusion(s32[16,512]{1,0:T(8,128)S(1)} %copy-done.3, bf16[16,512,1]{1,0,2:T(8,128)(2,1)S(1)} %get-tuple-element.28), kind=kOutput, calls=%fused_computation.4 | convolution fusion | flops 12582912 | bytes 65536 | tf_op jit(solution)/shard_map/bk,bks->bs/dot_general | solution.py:45
  79.0 25.2 %all-to-all-done = bf16[2,256,4,256]{3,2,0,1:T(4,128)(2,1)S(1)} async-done(((bf16[2,256,4,256]{3,2,0,1:T(4,128)(2,1)}), bf16[2,256,4,256]{3,2,0,1:T(4,128)(2,1)S(1)}, u32[]{:S(2)}, u32[]{:S(2)}) %all-to-all-start) | async-done | bytes 1048608 | tf_op jit(solution)/shard_map/all_to_all | solution.py:152
  104.2 1.2 fusion.46
  105.3 0.1 squeeze.3
  105.5 0.8 fusion.47
  106.2 0.7 fusion.9
  107.0 1.8 %reshape.269 = bf16[512,2,256]{2,1,0:T(2,128)(2,1)S(1)} reshape(bf16[1,256,4,256]{3,2,0,1:T(4,128)(2,1)} %get-tuple-element.20) | data formatting | bytes 1048576 | tf_op jit(solution)/shard_map/reshape.4
  108.8 0.2 convolution_bitcast_fusion
  109.0 0.2 convolution_bitcast_fusion.1
  109.2 0.1 multiply_reduce_fusion
  109.3 0.7 broadcast_in_dim.2
  110.0 6.5 %all-to-all-start.1 = ((f32[256,1,16]{2,1,0:T(1,128)}), f32[256,1,16]{2,1,0:T(1,128)S(1)}, u32[]{:S(2)}, u32[]{:S(2)}) async-start(f32[256,1,16]{2,1,0:T(1,128)} %broadcast_in_dim.2), calls=%async_computation.1 | async-start | bytes 262144 | tf_op jit(solution)/shard_map/all_to_all | solution.py:163
  116.5 1.7 %fusion.10 = bf16[1,1,1024,1024]{3,2,1,0:T(8,128)(2,1)S(1)} fusion(bf16[1024,256]{1,0:T(8,128)(2,1)S(1)} %squeeze.3, bf16[1024,128]{1,0:T(8,128)(2,1)} %get-tuple-element.23, bf16[1024,128]{1,0:T(8,128)(2,1)S(1)} %get-tuple-element.22), kind=kOutput, calls=%fused_computation.20 | convolution fusion | flops 540016640 | bytes 3145728 | tf_op jit(solution)/shard_map/dot_general | solution.py:106
  118.2 2.4 %pad_maximum_fusion = bf16[1,2,1024,1024]{3,2,1,0:T(8,128)(2,1)} fusion(bf16[1,1,1024,1024]{3,2,1,0:T(8,128)(2,1)S(1)} %fusion.10, bf16[1,1,1024,1024]{3,2,1,0:T(8,128)(2,1)S(1)} %fusion.9), kind=kLoop, calls=%fused_computation.13 | loop fusion | flops 2097152 | bytes 8388608 | tf_op jit(solution)/shard_map/stack | solution.py:159
  120.6 8.3 %all-to-all-done.1 = f32[256,1,16]{2,1,0:T(1,128)S(1)} async-done(((f32[256,1,16]{2,1,0:T(1,128)}), f32[256,1,16]{2,1,0:T(1,128)S(1)}, u32[]{:S(2)}, u32[]{:S(2)}) %all-to-all-start.1) | async-done | bytes 16416 | tf_op jit(solution)/shard_map/all_to_all | solution.py:163
  128.9 0.3 reduce_sum.19
  129.2 0.1 multiply_convert_fusion.4
  129.3 0.6 copy.43
  (4 shorter events, 0.0 us)
Async XLA Ops:
  1.5 10.1 %copy-start.1 = (s32[256]{0:T(256)S(1)}, s32[256]{0:T(256)}, u32[]{:S(2)}) copy-start(s32[256]{0:T(256)} %param.11) | copy-start | bytes 3076
  1.5 10.1 %copy-start.2 = (s32[256]{0:T(256)S(1)}, s32[256]{0:T(256)}, u32[]{:S(2)}) copy-start(s32[256]{0:T(256)} %param.10) | copy-start | bytes 3076
  55.7 16.6 %copy-start = (s32[16,512]{1,0:T(8,128)S(1)}, s32[16,512]{1,0:T(8,128)}, u32[]{:S(2)}) copy-start(s32[16,512]{1,0:T(8,128)} %param.15) | copy-start | bytes 98308
  55.7 16.8 %copy-start.3 = (s32[16,512]{1,0:T(8,128)S(1)}, s32[16,512]{1,0:T(8,128)}, u32[]{:S(2)}) copy-start(s32[16,512]{1,0:T(8,128)} %param.14) | copy-start | bytes 98308
  57.6 46.5 %all-to-all-start = ((bf16[2,256,4,256]{3,2,0,1:T(4,128)(2,1)}), bf16[2,256,4,256]{3,2,0,1:T(4,128)(2,1)S(1)}, u32[]{:S(2)}, u32[]{:S(2)}) async-start(bf16[2,256,4,256]{3,2,0,1:T(4,128)(2,1)} %fusion.8), calls=%async_computation | async-start | bytes 2097152 | tf_op jit(solution)/shard_map/all_to_all | solution.py:152
  110.0 18.9 %all-to-all-start.1 = ((f32[256,1,16]{2,1,0:T(1,128)}), f32[256,1,16]{2,1,0:T(1,128)S(1)}, u32[]{:S(2)}, u32[]{:S(2)}) async-start(f32[256,1,16]{2,1,0:T(1,128)} %broadcast_in_dim.2), calls=%async_computation.1 | async-start | bytes 262144 | tf_op jit(solution)/shard_map/all_to_all | solution.py:163

commit v11 on v9

--- a/solution.py
+++ b/solution.py
@@ -149,14 +149,14 @@
     received = turned.reshape(2, device_count * inputs_here, 2 * spectra)
     cor_data = received[0]
     beam_data = received[1:2]
-    swapped = jnp.concatenate([cor_data[:, spectra:], -cor_data[:, :spectra]], axis=1)
-    vis_re = contract(cor_data, cor_data) / spectra
-    vis_im = contract(swapped, cor_data) / spectra
-    visibilities = jnp.stack([vis_re, vis_im])[None].astype(jnp.bfloat16)
     raw_beams = form_beams(beam_data, weight_re, weight_im)
     local_power = jnp.sum(raw_beams * raw_beams, axis=(0, 2, 3))
     spread_power = jnp.broadcast_to(local_power[None], (device_count, local_power.shape[0]))
+    spread_power, cor_data = lax.optimization_barrier((spread_power, cor_data))
     gathered_power = lax.all_to_all(spread_power, ALL_AXES, split_axis=0, concat_axis=0, tiled=True)
+    swapped = jnp.concatenate([cor_data[:, spectra:], -cor_data[:, :spectra]], axis=1)
+    both = contract(jnp.concatenate([cor_data, swapped], axis=0), cor_data) / spectra
+    visibilities = both.reshape(1, 2, cor_data.shape[0], cor_data.shape[0]).astype(jnp.bfloat16)
     summed_power = jnp.sum(gathered_power, axis=0)
     beam_power = summed_power / (device_count * raw_beams.shape[2] * raw_beams.shape[3])
     beams = (raw_beams * lax.rsqrt(beam_power + epsilon)[None, :, None, None]).astype(jnp.bfloat16)

time: 132 us -> 128 us (0.970)
  other arithmetic: 22.9 us -> 19.8 us
  local copies, waits for them, and re-layouts: 5.34 us -> 2.94 us
    another operation x1 -> x0, other arithmetic: 2.38 us -> none  [per_device(): visibilities = jnp.stack([vis_re, vis_im])[None].astype(jnp.bfloat16)]
    another operation x1, local copies, waits for them, and re-layouts: 1.82 us -> 0.26 us
    dot_general x3 -> x2, matrix products: 16.1 us -> 17 us  [contract(): lax.dot_general(left_rows, right_rows, contract_dims, preferred_element_t...]
where the time goes in v11:
time: 128 us; the launch traced here: 126 us
  waiting for transfers between devices  34.4 us (27%)
  matrix products  23.8 us (19%)
  Pallas kernels  23.3 us (18%)
  starting transfers between devices  21.3 us (17%)
  other arithmetic  19.8 us (15%)
  local copies, waits for them, and re-layouts  2.94 us (2%)
    all_to_all x1, waiting for transfers between devices, per_device(): lax.all_to_all(outgoing, ALL_AXES, split_axis=1, concat_axis=1, tiled=True)  25.2 us
    pallas_call x1, Pallas kernels, polyphase(): pl.pallas_call(fir_kernel, grid=(per_frame // blocks,), in_specs=[pl.Bloc...  23.3 us
    dot_general x2, matrix products, contract(): lax.dot_general(left_rows, right_rows, contract_dims, preferred_element_t...  17 us
    all_to_all x1, starting transfers between devices, per_device(): lax.all_to_all(outgoing, ALL_AXES, split_axis=1, concat_axis=1, tiled=True)  14.7 us
    reshape x1, other arithmetic, polyphase(): tiles = tiles.reshape(frames, per_frame, rows, lanes)  10.1 us
    all_to_all x1, waiting for transfers between devices, per_device(): lax.all_to_all(spread_power, ALL_AXES, split_axis=0, concat_axis=0, tiled...  9.16 us
    all_to_all x1, starting transfers between devices, per_device(): lax.all_to_all(spread_power, ALL_AXES, split_axis=0, concat_axis=0, tiled...  6.63 us
    convert_element_type x1, other arithmetic, make_tables(): sin_table = ((sa * cb + ca * sb) * table_scale).astype(jnp.bfloat16)  5.31 us
  transfers between devices with their start and end apart: 2, of which 2 were waited for; matrix products, arithmetic and copies ran while one was open for 8% of the time, Pallas kernels for 0%

profile of v11, /device:TPU:2, one launch (start us, length us, event | category | flops | bytes accessed | tf_op | source)
XLA Modules:
  0.0 126.3 jit_solution(7836231424859985213)
XLA Ops:
  0.6 0.7 pad_maximum_fusion.2
  1.3 0.1 copy.25
  1.5 0.0 copy-start.1
  1.5 0.0 copy-start.2
  1.5 10.1 %copy_bitcast_fusion = f32[2,4,4448,128]{3,1,0,2:T(4,128)} fusion(bf16[2,4,569344]{2,1,0:T(4,128)(2,1)} %param.8), kind=kLoop, calls=%fused_computation | loop fusion | flops 4554752 | bytes 27328512 | tf_op jit(solution)/shard_map/reshape | solution.py:83
  11.6 0.0 copy-done.1
  11.6 0.0 copy-done.2
  11.6 1.0 fusion.31
  12.6 5.3 %multiply_convert_fusion.1 = (bf16[512,64,64]{0,2,1:T(8,128)(2,1)}, bf16[512,64,64]{0,2,1:T(8,128)(2,1)}) fusion(f32[512,64]{0,1:T(8,128)S(1)} %get-tuple-element.32, f32[512,64]{0,1:T(8,128)S(1)} %get-tuple-element.31, f32[512,64]{0,1:T(8,128)S(1)} %get-tuple-element.33, f32[512,64]{0,1:T(8,128)S(1)} %get-tuple-element.30), kind=kLoop, calls=%fused_computation.12 | loop fusion | flops 20971520 | bytes 8912896 | tf_op jit(solution)/shard_map/convert_element_type | solution.py:34
  17.9 23.3 %shard_map.95 = bf16[2,4,128,4096]{3,2,1,0:T(8,128)(2,1)} custom-call(f32[139,32,8,128]{3,2,1,0:T(8,128)} %bitcast.47, f32[12,4096]{1,0:T(8,128)} %h_ref.1), custom_call_target="tpu_custom_call" | custom-call | tf_op jit(solution)/shard_map/pallas_call | solution.py:85
  41.2 13.7 %fusion.2 = f32[1024,1024]{1,0:T(8,128)S(1)} fusion(bf16[1024,4096]{1,0:T(8,128)(2,1)} %bitcast.48, bf16[512,4096]{0,1:T(8,128)(2,1)} %bitcast.49, bf16[512,4096]{0,1:T(8,128)(2,1)} %bitcast.50), kind=kOutput, calls=%fused_computation.5 | convolution fusion | flops 8606711808 | bytes 20971520 | tf_op jit(solution)/shard_map/dot_general | solution.py:102
  54.9 0.0 copy-start
  54.9 0.0 copy-start.3
  54.9 0.5 slice_add_fusion
  55.4 0.4 concatenate.45
  55.8 0.4 concatenate.44
  56.1 1.5 %fusion.8 = bf16[2,256,4,256]{3,2,0,1:T(4,128)(2,1)} fusion(f32[2,256]{0,1:T(8,128)S(1)} %copy.25, f32[2,256,4,128]{3,2,1,0:T(4,128)S(1)} %concatenate.45, f32[2,256,4,128]{3,2,1,0:T(4,128)S(1)} %concatenate.44), kind=kLoop, calls=%fused_computation.16 | loop fusion | flops 1572864 | bytes 3147776 | tf_op jit(solution)/shard_map/convert_element_type | solution.py:119
  57.6 14.7 %all-to-all-start = ((bf16[2,256,4,256]{3,2,0,1:T(4,128)(2,1)}), bf16[2,256,4,256]{3,2,0,1:T(4,128)(2,1)S(1)}, u32[]{:S(2)}, u32[]{:S(2)}) async-start(bf16[2,256,4,256]{3,2,0,1:T(4,128)(2,1)} %fusion.8), calls=%async_computation | async-start | bytes 2097152 | tf_op jit(solution)/shard_map/all_to_all | solution.py:148
  72.3 0.0 copy-done
  72.3 0.2 multiply_bitcast_fusion.1
  72.5 0.0 copy-done.3
  72.5 3.2 %fusion = bf16[16,1,512]{2,1,0:T(2,128)(2,1)S(1)} fusion(s32[16,512]{1,0:T(8,128)S(1)} %copy-done.3, bf16[16,512,1]{1,0,2:T(8,128)(2,1)S(1)} %get-tuple-element.29), kind=kOutput, calls=%fused_computation.3 | convolution fusion | flops 12582912 | bytes 65536 | tf_op jit(solution)/shard_map/bk,bks->bs/dot_general | solution.py:45
  75.7 3.2 %fusion.1 = bf16[16,1,512]{2,1,0:T(2,128)(2,1)S(1)} fusion(s32[16,512]{1,0:T(8,128)S(1)} %copy-done.3, bf16[16,512,1]{1,0,2:T(8,128)(2,1)S(1)} %get-tuple-element.28), kind=kOutput, calls=%fused_computation.4 | convolution fusion | flops 12582912 | bytes 65536 | tf_op jit(solution)/shard_map/bk,bks->bs/dot_general | solution.py:44
  78.9 25.2 %all-to-all-done = bf16[2,256,4,256]{3,2,0,1:T(4,128)(2,1)S(1)} async-done(((bf16[2,256,4,256]{3,2,0,1:T(4,128)(2,1)}), bf16[2,256,4,256]{3,2,0,1:T(4,128)(2,1)S(1)}, u32[]{:S(2)}, u32[]{:S(2)}) %all-to-all-start) | async-done | bytes 1048608 | tf_op jit(solution)/shard_map/all_to_all | solution.py:148
  104.2 0.4 fusion.46
  104.5 0.3 reshape.246
  104.8 0.2 convolution_bitcast_fusion
  105.0 0.2 convolution_bitcast_fusion.1
  105.2 0.1 squeeze.3
  105.3 0.1 multiply_reduce_fusion
  105.4 0.7 broadcast_in_dim.2
  106.1 0.1 fusion.47
  106.2 6.6 %all-to-all-start.1 = ((f32[256,1,16]{2,1,0:T(1,128)}), f32[256,1,16]{2,1,0:T(1,128)S(1)}, u32[]{:S(2)}, u32[]{:S(2)}) async-start(f32[256,1,16]{2,1,0:T(1,128)} %bitcast.18), calls=%async_computation.1 | async-start | bytes 262144 | tf_op jit(solution)/shard_map/all_to_all | solution.py:156
  112.8 3.3 %multiply_convert_fusion = bf16[2048,1024]{1,0:T(8,128)(2,1)} fusion(bf16[1024,256]{1,0:T(8,128)(2,1)S(1)} %squeeze.3, bf16[1024,128]{1,0:T(8,128)(2,1)S(1)} %get-tuple-element.23, bf16[1024,128]{1,0:T(8,128)(2,1)S(1)} %get-tuple-element.22), kind=kOutput, calls=%fused_computation.9 | convolution fusion | flops 1081081856 | bytes 5242880 | tf_op jit(solution)/shard_map/dot_general | solution.py:102
  116.1 9.2 %all-to-all-done.1 = f32[256,1,16]{2,1,0:T(1,128)S(1)} async-done(((f32[256,1,16]{2,1,0:T(1,128)}), f32[256,1,16]{2,1,0:T(1,128)S(1)}, u32[]{:S(2)}, u32[]{:S(2)}) %all-to-all-start.1) | async-done | bytes 16416 | tf_op jit(solution)/shard_map/all_to_all | solution.py:156
  125.3 0.3 reduce_sum.19
  125.6 0.1 multiply_convert_fusion.3
  125.6 0.6 copy.28
  (4 shorter events, 0.0 us)
Async XLA Ops:
  1.5 10.1 %copy-start.1 = (s32[256]{0:T(256)S(1)}, s32[256]{0:T(256)}, u32[]{:S(2)}) copy-start(s32[256]{0:T(256)} %param.11) | copy-start | bytes 3076
  1.5 10.1 %copy-start.2 = (s32[256]{0:T(256)S(1)}, s32[256]{0:T(256)}, u32[]{:S(2)}) copy-start(s32[256]{0:T(256)} %param.10) | copy-start | bytes 3076
  54.9 17.5 %copy-start = (s32[16,512]{1,0:T(8,128)S(1)}, s32[16,512]{1,0:T(8,128)}, u32[]{:S(2)}) copy-start(s32[16,512]{1,0:T(8,128)} %param.15) | copy-start | bytes 98308
  54.9 17.6 %copy-start.3 = (s32[16,512]{1,0:T(8,128)S(1)}, s32[16,512]{1,0:T(8,128)}, u32[]{:S(2)}) copy-start(s32[16,512]{1,0:T(8,128)} %param.14) | copy-start | bytes 98308
  57.6 46.5 %all-to-all-start = ((bf16[2,256,4,256]{3,2,0,1:T(4,128)(2,1)}), bf16[2,256,4,256]{3,2,0,1:T(4,128)(2,1)S(1)}, u32[]{:S(2)}, u32[]{:S(2)}) async-start(bf16[2,256,4,256]{3,2,0,1:T(4,128)(2,1)} %fusion.8), calls=%async_computation | async-start | bytes 2097152 | tf_op jit(solution)/shard_map/all_to_all | solution.py:148
  106.2 19.1 %all-to-all-start.1 = ((f32[256,1,16]{2,1,0:T(1,128)}), f32[256,1,16]{2,1,0:T(1,128)S(1)}, u32[]{:S(2)}, u32[]{:S(2)}) async-start(f32[256,1,16]{2,1,0:T(1,128)} %bitcast.18), calls=%async_computation.1 | async-start | bytes 262144 | tf_op jit(solution)/shard_map/all_to_all | solution.py:156

commit v12 on v11

--- a/solution.py
+++ b/solution.py
@@ -139,16 +139,15 @@
     inputs_here = voltages.shape[1]
     spectra = voltages.shape[2] // points - tap_count + 1
     filtered = polyphase(voltages, fir_taps, spectra)
-    channel_of = jnp.concatenate([cor_channels, beam_channels])
-    slot_gain = jnp.concatenate([cor_gain, beam_gain])
+    channel_of = jnp.stack([cor_channels, beam_channels], axis=1).reshape(-1)
+    slot_gain = jnp.stack([cor_gain, beam_gain], axis=1).reshape(-1)
     cos_table, sin_table = lax.optimization_barrier(make_tables(channel_of, points))
     weight_re, weight_im = make_weights(beam_stations, beam_codes, STATIONS)
     spectra_all = spectrum(filtered, cos_table, sin_table, slot_gain)
-    outgoing = spectra_all.reshape(2, device_count, inputs_here, 2 * spectra)
-    turned = lax.all_to_all(outgoing, ALL_AXES, split_axis=1, concat_axis=1, tiled=True)
-    received = turned.reshape(2, device_count * inputs_here, 2 * spectra)
-    cor_data = received[0]
-    beam_data = received[1:2]
+    outgoing = spectra_all.reshape(device_count, 2, inputs_here, 2 * spectra)
+    turned = lax.all_to_all(outgoing, ALL_AXES, split_axis=0, concat_axis=0, tiled=True)
+    cor_data = turned[:, 0].reshape(device_count * inputs_here, 2 * spectra)
+    beam_data = turned[:, 1].reshape(1, device_count * inputs_here, 2 * spectra)
     raw_beams = form_beams(beam_data, weight_re, weight_im)
     local_power = jnp.sum(raw_beams * raw_beams, axis=(0, 2, 3))
     spread_power = jnp.broadcast_to(local_power[None], (device_count, local_power.shape[0]))

time: 128 us -> 128 us (level)
  no operation moved by 1% of the time
where the time goes in v12:
time: 128 us; the launch traced here: 126 us
  waiting for transfers between devices  34.3 us (27%)
  matrix products  23.8 us (19%)
  Pallas kernels  23.3 us (18%)
  starting transfers between devices  21.3 us (17%)
  other arithmetic  19.1 us (15%)
  local copies, waits for them, and re-layouts  3.2 us (2%)
    all_to_all x1, waiting for transfers between devices, per_device(): lax.all_to_all(outgoing, ALL_AXES, split_axis=0, concat_axis=0, tiled=True)  25.2 us
    pallas_call x1, Pallas kernels, polyphase(): pl.pallas_call(fir_kernel, grid=(per_frame // blocks,), in_specs=[pl.Bloc...  23.3 us
    dot_general x2, matrix products, contract(): lax.dot_general(left_rows, right_rows, contract_dims, preferred_element_t...  17 us
    all_to_all x1, starting transfers between devices, per_device(): lax.all_to_all(outgoing, ALL_AXES, split_axis=0, concat_axis=0, tiled=True)  14.7 us
    reshape x1, other arithmetic, polyphase(): tiles = tiles.reshape(frames, per_frame, rows, lanes)  10.1 us
    all_to_all x1, waiting for transfers between devices, per_device(): lax.all_to_all(spread_power, ALL_AXES, split_axis=0, concat_axis=0, tiled...  9.12 us
    all_to_all x1, starting transfers between devices, per_device(): lax.all_to_all(spread_power, ALL_AXES, split_axis=0, concat_axis=0, tiled...  6.64 us
    convert_element_type x1, other arithmetic, make_tables(): sin_table = ((sa * cb + ca * sb) * table_scale).astype(jnp.bfloat16)  5.31 us
  transfers between devices with their start and end apart: 2, of which 2 were waited for; matrix products, arithmetic and copies ran while one was open for 8% of the time, Pallas kernels for 0%

profile of v12, /device:TPU:2, one launch (start us, length us, event | category | flops | bytes accessed | tf_op | source)
XLA Modules:
  0.0 125.9 jit_solution(2976888999025952673)
XLA Ops:
  0.6 0.0 copy-start.1
  0.6 0.0 copy-start.2
  0.6 10.1 %copy_bitcast_fusion = f32[2,4,4448,128]{3,1,0,2:T(4,128)} fusion(bf16[2,4,569344]{2,1,0:T(4,128)(2,1)} %param.8), kind=kLoop, calls=%fused_computation | loop fusion | flops 4554752 | bytes 27328512 | tf_op jit(solution)/shard_map/reshape | solution.py:83
  10.7 0.0 copy-done.1
  10.7 0.0 copy-done.2
  10.7 0.1 copy.19
  10.9 0.1 mul.177
  11.0 1.0 fusion.31
  12.0 5.3 %multiply_convert_fusion.1 = (bf16[512,64,64]{0,2,1:T(8,128)(2,1)}, bf16[512,64,64]{0,2,1:T(8,128)(2,1)}) fusion(f32[512,64]{0,1:T(8,128)S(1)} %get-tuple-element.30, f32[512,64]{0,1:T(8,128)S(1)} %get-tuple-element.29, f32[512,64]{0,1:T(8,128)S(1)} %get-tuple-element.31, f32[512,64]{0,1:T(8,128)S(1)} %get-tuple-element.28), kind=kLoop, calls=%fused_computation.12 | loop fusion | flops 20971520 | bytes 8912896 | tf_op jit(solution)/shard_map/convert_element_type | solution.py:34
  17.4 23.3 %shard_map.95 = bf16[2,4,128,4096]{3,2,1,0:T(8,128)(2,1)} custom-call(f32[139,32,8,128]{3,2,1,0:T(8,128)} %bitcast.47, f32[12,4096]{1,0:T(8,128)} %h_ref.1), custom_call_target="tpu_custom_call" | custom-call | tf_op jit(solution)/shard_map/pallas_call | solution.py:85
  40.7 13.7 %fusion.2 = f32[1024,1024]{1,0:T(8,128)S(1)} fusion(bf16[1024,4096]{1,0:T(8,128)(2,1)} %bitcast.48, bf16[512,4096]{0,1:T(8,128)(2,1)} %bitcast.49, bf16[512,4096]{0,1:T(8,128)(2,1)} %bitcast.50), kind=kOutput, calls=%fused_computation.5 | convolution fusion | flops 8606711808 | bytes 20971520 | tf_op jit(solution)/shard_map/dot_general | solution.py:102
  54.3 0.0 copy-start.3
  54.3 0.0 copy-start.4
  54.4 0.0 copy-start
  54.4 0.0 copy-start.5
  54.4 0.5 slice_add_fusion
  54.9 0.4 concatenate.38
  55.2 0.4 concatenate.37
  55.6 0.0 copy-done.3
  55.6 0.0 copy-done.4
  55.6 0.1 copy.21
  55.8 1.5 %fusion.8 = bf16[256,2,4,256]{3,2,1,0:T(4,128)(2,1)} fusion(f32[256,2,4,128]{3,2,1,0:T(4,128)S(1)} %concatenate.38, f32[256,2,4,128]{3,2,1,0:T(4,128)S(1)} %concatenate.37, f32[256,2]{1,0:T(8,128)S(1)} %copy.21), kind=kLoop, calls=%fused_computation.15 | loop fusion | flops 1572864 | bytes 3147776 | tf_op jit(solution)/shard_map/convert_element_type | solution.py:119
  57.3 14.7 %all-to-all-start = ((bf16[256,2,4,256]{3,2,1,0:T(4,128)(2,1)}), bf16[256,2,4,256]{3,2,1,0:T(4,128)(2,1)S(1)}, u32[]{:S(2)}, u32[]{:S(2)}) async-start(bf16[256,2,4,256]{3,2,1,0:T(4,128)(2,1)} %fusion.8), calls=%async_computation | async-start | bytes 2097152 | tf_op jit(solution)/shard_map/all_to_all | solution.py:148
  72.0 0.0 copy-done
  72.0 0.2 multiply_bitcast_fusion.1
  72.2 0.0 copy-done.5
  72.2 3.2 %fusion = bf16[16,1,512]{2,1,0:T(2,128)(2,1)S(1)} fusion(s32[16,512]{1,0:T(8,128)S(1)} %copy-done.5, bf16[16,512,1]{1,0,2:T(8,128)(2,1)S(1)} %get-tuple-element.27), kind=kOutput, calls=%fused_computation.3 | convolution fusion | flops 12582912 | bytes 65536 | tf_op jit(solution)/shard_map/bk,bks->bs/dot_general | solution.py:45
  75.4 3.2 %fusion.1 = bf16[16,1,512]{2,1,0:T(2,128)(2,1)S(1)} fusion(s32[16,512]{1,0:T(8,128)S(1)} %copy-done.5, bf16[16,512,1]{1,0,2:T(8,128)(2,1)S(1)} %get-tuple-element.26), kind=kOutput, calls=%fused_computation.4 | convolution fusion | flops 12582912 | bytes 65536 | tf_op jit(solution)/shard_map/bk,bks->bs/dot_general | solution.py:44
  78.6 25.2 %all-to-all-done = bf16[256,2,4,256]{3,2,1,0:T(4,128)(2,1)S(1)} async-done(((bf16[256,2,4,256]{3,2,1,0:T(4,128)(2,1)}), bf16[256,2,4,256]{3,2,1,0:T(4,128)(2,1)S(1)}, u32[]{:S(2)}, u32[]{:S(2)}) %all-to-all-start) | async-done | bytes 1048608 | tf_op jit(solution)/shard_map/all_to_all | solution.py:148
  103.8 0.4 fusion.46
  104.2 0.3 reshape.255
  104.5 0.2 convolution_bitcast_fusion
  104.7 0.2 convolution_bitcast_fusion.1
  104.8 0.1 reshape_squeeze.3
  105.0 0.1 multiply_reduce_fusion
  105.1 0.7 broadcast_in_dim.2
  105.8 0.1 fusion.47
  105.8 6.6 %all-to-all-start.1 = ((f32[256,1,16]{2,1,0:T(1,128)}), f32[256,1,16]{2,1,0:T(1,128)S(1)}, u32[]{:S(2)}, u32[]{:S(2)}) async-start(f32[256,1,16]{2,1,0:T(1,128)} %bitcast.22), calls=%async_computation.1 | async-start | bytes 262144 | tf_op jit(solution)/shard_map/all_to_all | solution.py:155
  112.5 3.3 %multiply_convert_fusion = bf16[2048,1024]{1,0:T(8,128)(2,1)} fusion(bf16[1024,256]{1,0:T(8,128)(2,1)S(1)} %reshape_squeeze.3, bf16[1024,128]{1,0:T(8,128)(2,1)S(1)} %get-tuple-element.21, bf16[1024,128]{1,0:T(8,128)(2,1)S(1)} %get-tuple-element.20), kind=kOutput, calls=%fused_computation.9 | convolution fusion | flops 1081081856 | bytes 5242880 | tf_op jit(solution)/shard_map/dot_general | solution.py:102
  115.8 9.1 %all-to-all-done.1 = f32[256,1,16]{2,1,0:T(1,128)S(1)} async-done(((f32[256,1,16]{2,1,0:T(1,128)}), f32[256,1,16]{2,1,0:T(1,128)S(1)}, u32[]{:S(2)}, u32[]{:S(2)}) %all-to-all-start.1) | async-done | bytes 16416 | tf_op jit(solution)/shard_map/all_to_all | solution.py:155
  124.9 0.3 reduce_sum.19
  125.2 0.1 multiply_convert_fusion.3
  125.3 0.6 copy.24
  (4 shorter events, 0.0 us)
Async XLA Ops:
  0.6 10.1 %copy-start.1 = (s32[256]{0:T(256)S(1)}, s32[256]{0:T(256)}, u32[]{:S(2)}) copy-start(s32[256]{0:T(256)} %param.11) | copy-start | bytes 3076
  0.6 10.1 %copy-start.2 = (s32[256]{0:T(256)S(1)}, s32[256]{0:T(256)}, u32[]{:S(2)}) copy-start(s32[256]{0:T(256)} %param.10) | copy-start | bytes 3076
  54.3 1.3 %copy-start.3 = (f32[256]{0:T(256)S(1)}, f32[256]{0:T(256)}, u32[]{:S(2)}) copy-start(f32[256]{0:T(256)} %param.13) | copy-start | bytes 3076
  54.3 1.3 %copy-start.4 = (f32[256]{0:T(256)S(1)}, f32[256]{0:T(256)}, u32[]{:S(2)}) copy-start(f32[256]{0:T(256)} %param.12) | copy-start | bytes 3076
  54.4 17.6 %copy-start = (s32[16,512]{1,0:T(8,128)S(1)}, s32[16,512]{1,0:T(8,128)}, u32[]{:S(2)}) copy-start(s32[16,512]{1,0:T(8,128)} %param.15) | copy-start | bytes 98308
  54.4 17.8 %copy-start.5 = (s32[16,512]{1,0:T(8,128)S(1)}, s32[16,512]{1,0:T(8,128)}, u32[]{:S(2)}) copy-start(s32[16,512]{1,0:T(8,128)} %param.14) | copy-start | bytes 98308
  57.3 46.6 %all-to-all-start = ((bf16[256,2,4,256]{3,2,1,0:T(4,128)(2,1)}), bf16[256,2,4,256]{3,2,1,0:T(4,128)(2,1)S(1)}, u32[]{:S(2)}, u32[]{:S(2)}) async-start(bf16[256,2,4,256]{3,2,1,0:T(4,128)(2,1)} %fusion.8), calls=%async_computation | async-start | bytes 2097152 | tf_op jit(solution)/shard_map/all_to_all | solution.py:148
  105.8 19.1 %all-to-all-start.1 = ((f32[256,1,16]{2,1,0:T(1,128)}), f32[256,1,16]{2,1,0:T(1,128)S(1)}, u32[]{:S(2)}, u32[]{:S(2)}) async-start(f32[256,1,16]{2,1,0:T(1,128)} %bitcast.22), calls=%async_computation.1 | async-start | bytes 262144 | tf_op jit(solution)/shard_map/all_to_all | solution.py:155

commit v13 on v12

--- a/solution.py
+++ b/solution.py
@@ -27,11 +27,12 @@
     b_turns = channel_of[:, None] * b_index[None, :] % points
     a_angle = a_turns.astype(jnp.float32) * step
     b_angle = b_turns.astype(jnp.float32) * step
-    ca, sa = jnp.cos(a_angle)[:, :, None], jnp.sin(a_angle)[:, :, None]
+    table_scale = 1.0 / math.sqrt(points)
+    ca = (jnp.cos(a_angle) * table_scale)[:, :, None]
+    sa = (jnp.sin(a_angle) * table_scale)[:, :, None]
     cb, sb = jnp.cos(b_angle)[:, None, :], jnp.sin(b_angle)[:, None, :]
-    table_scale = 1.0 / math.sqrt(points)
-    cos_table = ((ca * cb - sa * sb) * table_scale).astype(jnp.bfloat16)
-    sin_table = ((sa * cb + ca * sb) * table_scale).astype(jnp.bfloat16)
+    cos_table = (ca * cb - sa * sb).astype(jnp.bfloat16)
+    sin_table = (sa * cb + ca * sb).astype(jnp.bfloat16)
     slots = channel_of.shape[0]
     return (cos_table.reshape(slots, points), sin_table.reshape(slots, points))
 

time: 128 us -> 128 us (level)
  no operation moved by 1% of the time
where the time goes in v13:
time: 128 us; the launch traced here: 126 us
  waiting for transfers between devices  34.3 us (27%)
  matrix products  23.8 us (19%)
  Pallas kernels  23.3 us (18%)
  starting transfers between devices  21.3 us (17%)
  other arithmetic  19.1 us (15%)
  local copies, waits for them, and re-layouts  3.2 us (2%)
    all_to_all x1, waiting for transfers between devices, per_device(): lax.all_to_all(outgoing, ALL_AXES, split_axis=0, concat_axis=0, tiled=True)  25.2 us
    pallas_call x1, Pallas kernels, polyphase(): pl.pallas_call(fir_kernel, grid=(per_frame // blocks,), in_specs=[pl.Bloc...  23.3 us
    dot_general x2, matrix products, contract(): lax.dot_general(left_rows, right_rows, contract_dims, preferred_element_t...  17 us
    all_to_all x1, starting transfers between devices, per_device(): lax.all_to_all(outgoing, ALL_AXES, split_axis=0, concat_axis=0, tiled=True)  14.7 us
    reshape x1, other arithmetic, polyphase(): tiles = tiles.reshape(frames, per_frame, rows, lanes)  10.1 us
    all_to_all x1, waiting for transfers between devices, per_device(): lax.all_to_all(spread_power, ALL_AXES, split_axis=0, concat_axis=0, tiled...  9.11 us
    all_to_all x1, starting transfers between devices, per_device(): lax.all_to_all(spread_power, ALL_AXES, split_axis=0, concat_axis=0, tiled...  6.64 us
    convert_element_type x1, other arithmetic, make_tables(): sin_table = (sa * cb + ca * sb).astype(jnp.bfloat16)  5.3 us
  transfers between devices with their start and end apart: 2, of which 2 were waited for; matrix products, arithmetic and copies ran while one was open for 8% of the time, Pallas kernels for 0%

profile of v13, /device:TPU:2, one launch (start us, length us, event | category | flops | bytes accessed | tf_op | source)
XLA Modules:
  0.0 125.9 jit_solution(2976746912995229182)
XLA Ops:
  0.6 0.0 copy-start.1
  0.6 0.0 copy-start.2
  0.6 10.1 %copy_bitcast_fusion = f32[2,4,4448,128]{3,1,0,2:T(4,128)} fusion(bf16[2,4,569344]{2,1,0:T(4,128)(2,1)} %param.8), kind=kLoop, calls=%fused_computation | loop fusion | flops 4554752 | bytes 27328512 | tf_op jit(solution)/shard_map/reshape | solution.py:84
  10.7 0.0 copy-done.1
  10.7 0.0 copy-done.2
  10.7 0.1 copy.19
  10.9 0.1 mul.181
  11.0 1.0 cosine_multiply_fusion
  12.1 5.3 %add_convert_fusion = (bf16[512,64,64]{0,2,1:T(8,128)(2,1)}, bf16[512,64,64]{0,2,1:T(8,128)(2,1)}) fusion(f32[512,64]{0,1:T(8,128)S(1)} %get-tuple-element.30, f32[512,64]{0,1:T(8,128)S(1)} %get-tuple-element.29, f32[512,64]{0,1:T(8,128)S(1)} %get-tuple-element.31, f32[512,64]{0,1:T(8,128)S(1)} %get-tuple-element.28), kind=kLoop, calls=%fused_computation.12 | loop fusion | flops 16777216 | bytes 8912896 | tf_op jit(solution)/shard_map/convert_element_type | solution.py:35
  17.4 23.3 %shard_map.95 = bf16[2,4,128,4096]{3,2,1,0:T(8,128)(2,1)} custom-call(f32[139,32,8,128]{3,2,1,0:T(8,128)} %bitcast.47, f32[12,4096]{1,0:T(8,128)} %h_ref.1), custom_call_target="tpu_custom_call" | custom-call | tf_op jit(solution)/shard_map/pallas_call | solution.py:86
  40.6 13.7 %fusion.2 = f32[1024,1024]{1,0:T(8,128)S(1)} fusion(bf16[1024,4096]{1,0:T(8,128)(2,1)} %bitcast.48, bf16[512,4096]{0,1:T(8,128)(2,1)} %bitcast.49, bf16[512,4096]{0,1:T(8,128)(2,1)} %bitcast.50), kind=kOutput, calls=%fused_computation.5 | convolution fusion | flops 8606711808 | bytes 20971520 | tf_op jit(solution)/shard_map/dot_general | solution.py:103
  54.3 0.0 copy-start.3
  54.3 0.0 copy-start.4
  54.4 0.0 copy-start
  54.4 0.0 copy-start.5
  54.4 0.5 slice_add_fusion
  54.9 0.4 concatenate.38
  55.2 0.4 concatenate.37
  55.6 0.0 copy-done.3
  55.6 0.0 copy-done.4
  55.6 0.1 copy.21
  55.8 1.5 %fusion.8 = bf16[256,2,4,256]{3,2,1,0:T(4,128)(2,1)} fusion(f32[256,2,4,128]{3,2,1,0:T(4,128)S(1)} %concatenate.38, f32[256,2,4,128]{3,2,1,0:T(4,128)S(1)} %concatenate.37, f32[256,2]{1,0:T(8,128)S(1)} %copy.21), kind=kLoop, calls=%fused_computation.15 | loop fusion | flops 1572864 | bytes 3147776 | tf_op jit(solution)/shard_map/convert_element_type | solution.py:120
  57.3 14.7 %all-to-all-start = ((bf16[256,2,4,256]{3,2,1,0:T(4,128)(2,1)}), bf16[256,2,4,256]{3,2,1,0:T(4,128)(2,1)S(1)}, u32[]{:S(2)}, u32[]{:S(2)}) async-start(bf16[256,2,4,256]{3,2,1,0:T(4,128)(2,1)} %fusion.8), calls=%async_computation | async-start | bytes 2097152 | tf_op jit(solution)/shard_map/all_to_all | solution.py:149
  72.0 0.0 copy-done
  72.0 0.2 multiply_bitcast_fusion.1
  72.2 0.0 copy-done.5
  72.2 3.2 %fusion = bf16[16,1,512]{2,1,0:T(2,128)(2,1)S(1)} fusion(s32[16,512]{1,0:T(8,128)S(1)} %copy-done.5, bf16[16,512,1]{1,0,2:T(8,128)(2,1)S(1)} %get-tuple-element.27), kind=kOutput, calls=%fused_computation.3 | convolution fusion | flops 12582912 | bytes 65536 | tf_op jit(solution)/shard_map/bk,bks->bs/dot_general | solution.py:46
  75.4 3.2 %fusion.1 = bf16[16,1,512]{2,1,0:T(2,128)(2,1)S(1)} fusion(s32[16,512]{1,0:T(8,128)S(1)} %copy-done.5, bf16[16,512,1]{1,0,2:T(8,128)(2,1)S(1)} %get-tuple-element.26), kind=kOutput, calls=%fused_computation.4 | convolution fusion | flops 12582912 | bytes 65536 | tf_op jit(solution)/shard_map/bk,bks->bs/dot_general | solution.py:45
  78.6 25.2 %all-to-all-done = bf16[256,2,4,256]{3,2,1,0:T(4,128)(2,1)S(1)} async-done(((bf16[256,2,4,256]{3,2,1,0:T(4,128)(2,1)}), bf16[256,2,4,256]{3,2,1,0:T(4,128)(2,1)S(1)}, u32[]{:S(2)}, u32[]{:S(2)}) %all-to-all-start) | async-done | bytes 1048608 | tf_op jit(solution)/shard_map/all_to_all | solution.py:149
  103.8 0.4 fusion.44
  104.2 0.3 reshape.253
  104.5 0.2 convolution_bitcast_fusion
  104.7 0.2 convolution_bitcast_fusion.1
  104.8 0.1 reshape_squeeze.3
  105.0 0.1 multiply_reduce_fusion
  105.1 0.7 broadcast_in_dim.2
  105.8 0.1 fusion.45
  105.8 6.6 %all-to-all-start.1 = ((f32[256,1,16]{2,1,0:T(1,128)}), f32[256,1,16]{2,1,0:T(1,128)S(1)}, u32[]{:S(2)}, u32[]{:S(2)}) async-start(f32[256,1,16]{2,1,0:T(1,128)} %bitcast.22), calls=%async_computation.1 | async-start | bytes 262144 | tf_op jit(solution)/shard_map/all_to_all | solution.py:156
  112.5 3.3 %multiply_convert_fusion = bf16[2048,1024]{1,0:T(8,128)(2,1)} fusion(bf16[1024,256]{1,0:T(8,128)(2,1)S(1)} %reshape_squeeze.3, bf16[1024,128]{1,0:T(8,128)(2,1)S(1)} %get-tuple-element.21, bf16[1024,128]{1,0:T(8,128)(2,1)S(1)} %get-tuple-element.20), kind=kOutput, calls=%fused_computation.9 | convolution fusion | flops 1081081856 | bytes 5242880 | tf_op jit(solution)/shard_map/dot_general | solution.py:103
  115.8 9.1 %all-to-all-done.1 = f32[256,1,16]{2,1,0:T(1,128)S(1)} async-done(((f32[256,1,16]{2,1,0:T(1,128)}), f32[256,1,16]{2,1,0:T(1,128)S(1)}, u32[]{:S(2)}, u32[]{:S(2)}) %all-to-all-start.1) | async-done | bytes 16416 | tf_op jit(solution)/shard_map/all_to_all | solution.py:156
  124.9 0.3 reduce_sum.19
  125.2 0.1 multiply_convert_fusion.1
  125.3 0.6 copy.24
  (4 shorter events, 0.0 us)
Async XLA Ops:
  0.6 10.1 %copy-start.1 = (s32[256]{0:T(256)S(1)}, s32[256]{0:T(256)}, u32[]{:S(2)}) copy-start(s32[256]{0:T(256)} %param.11) | copy-start | bytes 3076
  0.6 10.1 %copy-start.2 = (s32[256]{0:T(256)S(1)}, s32[256]{0:T(256)}, u32[]{:S(2)}) copy-start(s32[256]{0:T(256)} %param.10) | copy-start | bytes 3076
  54.3 1.3 %copy-start.3 = (f32[256]{0:T(256)S(1)}, f32[256]{0:T(256)}, u32[]{:S(2)}) copy-start(f32[256]{0:T(256)} %param.13) | copy-start | bytes 3076
  54.3 1.3 %copy-start.4 = (f32[256]{0:T(256)S(1)}, f32[256]{0:T(256)}, u32[]{:S(2)}) copy-start(f32[256]{0:T(256)} %param.12) | copy-start | bytes 3076
  54.4 17.6 %copy-start = (s32[16,512]{1,0:T(8,128)S(1)}, s32[16,512]{1,0:T(8,128)}, u32[]{:S(2)}) copy-start(s32[16,512]{1,0:T(8,128)} %param.15) | copy-start | bytes 98308
  54.4 17.8 %copy-start.5 = (s32[16,512]{1,0:T(8,128)S(1)}, s32[16,512]{1,0:T(8,128)}, u32[]{:S(2)}) copy-start(s32[16,512]{1,0:T(8,128)} %param.14) | copy-start | bytes 98308
  57.3 46.5 %all-to-all-start = ((bf16[256,2,4,256]{3,2,1,0:T(4,128)(2,1)}), bf16[256,2,4,256]{3,2,1,0:T(4,128)(2,1)S(1)}, u32[]{:S(2)}, u32[]{:S(2)}) async-start(bf16[256,2,4,256]{3,2,1,0:T(4,128)(2,1)} %fusion.8), calls=%async_computation | async-start | bytes 2097152 | tf_op jit(solution)/shard_map/all_to_all | solution.py:149
  105.8 19.1 %all-to-all-start.1 = ((f32[256,1,16]{2,1,0:T(1,128)}), f32[256,1,16]{2,1,0:T(1,128)S(1)}, u32[]{:S(2)}, u32[]{:S(2)}) async-start(f32[256,1,16]{2,1,0:T(1,128)} %bitcast.22), calls=%async_computation.1 | async-start | bytes 262144 | tf_op jit(solution)/shard_map/all_to_all | solution.py:156

commit v14 on v12

--- a/solution.py
+++ b/solution.py
@@ -57,14 +57,19 @@
             for t in range(tap_count)
         ]
 
-        def frame_body(s, carry):
-            acc = taps[0] * x_ref[s, block]
-            for t in range(1, tap_count):
-                acc = acc + taps[t] * x_ref[s + t, block]
-            os_ref[pl.ds(s, rows, stride=spectra), :] = acc
+        def frame_body(step, carry):
+            first = pl.multiple_of(step * 8, 8)
+            window = [
+                x_ref[first + f, block].astype(jnp.float32) for f in range(8 + tap_count - 1)
+            ]
+            for k in range(8):
+                acc = taps[0] * window[k]
+                for t in range(1, tap_count):
+                    acc = acc + taps[t] * window[k + t]
+                os_ref[pl.ds(first + k, rows, stride=spectra), :] = acc
             return carry
 
-        lax.fori_loop(0, spectra, frame_body, 0, unroll=8)
+        lax.fori_loop(0, spectra // 8, frame_body, 0)
         for r in range(rows):
             o_ref[r // inputs_here, r % inputs_here, :, pl.ds(block * lanes, lanes)] = os_ref[
                 pl.ds(r * spectra, spectra), :
@@ -79,7 +84,7 @@
     frames = samples // points
     per_frame = points // lanes
     tiles = in_block.reshape(components, inputs_here, samples // lanes, lanes)
-    tiles = jnp.transpose(tiles, (2, 0, 1, 3)).astype(jnp.float32)
+    tiles = jnp.transpose(tiles, (2, 0, 1, 3))
     tiles = tiles.reshape(frames, per_frame, rows, lanes)
     blocks = 4
     return pl.pallas_call(

time: 128 us -> 126 us (0.984)
  other arithmetic: 19.1 us -> 9.09 us
  local copies, waits for them, and re-layouts: 3.2 us -> 11.6 us
    reshape x1 -> x0, other arithmetic: 10.1 us -> none  [polyphase(): tiles = tiles.reshape(frames, per_frame, rows, lanes)]
    reshape x1 -> x2, local copies, waits for them, and re-layouts: 0.26 us -> 8.66 us  [the longest x1 8.39 us: polyphase(): tiles = in_block.reshape(components, inputs_here, samples // lanes, lanes)]
where the time goes in v14:
time: 126 us; the launch traced here: 125 us
  waiting for transfers between devices  34.4 us (27%)
  matrix products  23.8 us (19%)
  Pallas kernels  23.7 us (19%)
  starting transfers between devices  21.3 us (17%)
  local copies, waits for them, and re-layouts  11.6 us (9%)
  other arithmetic  9.09 us (7%)
    all_to_all x1, waiting for transfers between devices, per_device(): lax.all_to_all(outgoing, ALL_AXES, split_axis=0, concat_axis=0, tiled=True)  25.2 us
    pallas_call x1, Pallas kernels, polyphase(): pl.pallas_call(fir_kernel, grid=(per_frame // blocks,), in_specs=[pl.Bloc...  23.7 us
    dot_general x2, matrix products, contract(): lax.dot_general(left_rows, right_rows, contract_dims, preferred_element_t...  17 us
    all_to_all x1, starting transfers between devices, per_device(): lax.all_to_all(outgoing, ALL_AXES, split_axis=0, concat_axis=0, tiled=True)  14.7 us
    all_to_all x1, waiting for transfers between devices, per_device(): lax.all_to_all(spread_power, ALL_AXES, split_axis=0, concat_axis=0, tiled...  9.12 us
    reshape x1, local copies, waits for them, and re-layouts, polyphase(): tiles = in_block.reshape(components, inputs_here, samples // lanes, lanes)  8.39 us
    all_to_all x1, starting transfers between devices, per_device(): lax.all_to_all(spread_power, ALL_AXES, split_axis=0, concat_axis=0, tiled...  6.64 us
    convert_element_type x1, other arithmetic, make_tables(): sin_table = ((sa * cb + ca * sb) * table_scale).astype(jnp.bfloat16)  5.34 us
  transfers between devices with their start and end apart: 2, of which 2 were waited for; matrix products, arithmetic and copies ran while one was open for 8% of the time, Pallas kernels for 0%

profile of v14, /device:TPU:2, one launch (start us, length us, event | category | flops | bytes accessed | tf_op | source)
XLA Modules:
  0.0 124.6 jit_solution(13329782050703956402)
XLA Ops:
  0.6 0.0 copy-start.1
  0.6 0.0 copy-start.2
  0.6 8.4 %copy_bitcast_fusion = bf16[2,4,4448,128]{3,1,0,2:T(4,128)(2,1)} fusion(bf16[2,4,569344]{2,1,0:T(4,128)(2,1)} %param.8), kind=kLoop, calls=%fused_computation.3 | loop fusion | bytes 18219008 | tf_op jit(solution)/shard_map/reshape | solution.py:86
  9.0 0.0 copy-done.1
  9.0 0.0 copy-done.2
  9.1 0.1 copy.19
  9.2 0.1 mul.177
  9.3 1.0 fusion.31
  10.4 5.3 %multiply_convert_fusion.1 = (bf16[512,64,64]{0,2,1:T(8,128)(2,1)}, bf16[512,64,64]{0,2,1:T(8,128)(2,1)}) fusion(f32[512,64]{0,1:T(8,128)S(1)} %get-tuple-element.30, f32[512,64]{0,1:T(8,128)S(1)} %get-tuple-element.29, f32[512,64]{0,1:T(8,128)S(1)} %get-tuple-element.31, f32[512,64]{0,1:T(8,128)S(1)} %get-tuple-element.28), kind=kLoop, calls=%fused_computation.11 | loop fusion | flops 20971520 | bytes 8912896 | tf_op jit(solution)/shard_map/convert_element_type | solution.py:34
  15.7 23.7 %shard_map.95 = bf16[2,4,128,4096]{3,2,1,0:T(8,128)(2,1)} custom-call(bf16[139,32,8,128]{3,2,1,0:T(8,128)(2,1)} %bitcast.47, f32[12,4096]{1,0:T(8,128)} %h_ref.1), custom_call_target="tpu_custom_call" | custom-call | tf_op jit(solution)/shard_map/pallas_call | solution.py:90
  39.4 13.7 %fusion.2 = f32[1024,1024]{1,0:T(8,128)S(1)} fusion(bf16[1024,4096]{1,0:T(8,128)(2,1)} %bitcast.48, bf16[512,4096]{0,1:T(8,128)(2,1)} %bitcast.49, bf16[512,4096]{0,1:T(8,128)(2,1)} %bitcast.50), kind=kOutput, calls=%fused_computation.4 | convolution fusion | flops 8606711808 | bytes 20971520 | tf_op jit(solution)/shard_map/dot_general | solution.py:107
  53.1 0.0 copy-start.3
  53.1 0.0 copy-start.4
  53.1 0.0 copy-start
  53.1 0.0 copy-start.5
  53.1 0.5 slice_add_fusion
  53.6 0.4 concatenate.38
  54.0 0.4 concatenate.37
  54.3 0.0 copy-done.3
  54.3 0.0 copy-done.4
  54.4 0.1 copy.21
  54.5 1.5 %fusion.8 = bf16[256,2,4,256]{3,2,1,0:T(4,128)(2,1)} fusion(f32[256,2,4,128]{3,2,1,0:T(4,128)S(1)} %concatenate.38, f32[256,2,4,128]{3,2,1,0:T(4,128)S(1)} %concatenate.37, f32[256,2]{1,0:T(8,128)S(1)} %copy.21), kind=kLoop, calls=%fused_computation.14 | loop fusion | flops 1572864 | bytes 3147776 | tf_op jit(solution)/shard_map/convert_element_type | solution.py:124
  56.0 14.7 %all-to-all-start = ((bf16[256,2,4,256]{3,2,1,0:T(4,128)(2,1)}), bf16[256,2,4,256]{3,2,1,0:T(4,128)(2,1)S(1)}, u32[]{:S(2)}, u32[]{:S(2)}) async-start(bf16[256,2,4,256]{3,2,1,0:T(4,128)(2,1)} %fusion.8), calls=%async_computation | async-start | bytes 2097152 | tf_op jit(solution)/shard_map/all_to_all | solution.py:153
  70.7 0.0 copy-done
  70.7 0.2 multiply_bitcast_fusion.1
  70.9 0.0 copy-done.5
  70.9 3.2 %fusion = bf16[16,1,512]{2,1,0:T(2,128)(2,1)S(1)} fusion(s32[16,512]{1,0:T(8,128)S(1)} %copy-done.5, bf16[16,512,1]{1,0,2:T(8,128)(2,1)S(1)} %get-tuple-element.27), kind=kOutput, calls=%fused_computation.1 | convolution fusion | flops 12582912 | bytes 65536 | tf_op jit(solution)/shard_map/bk,bks->bs/dot_general | solution.py:45
  74.1 3.2 %fusion.1 = bf16[16,1,512]{2,1,0:T(2,128)(2,1)S(1)} fusion(s32[16,512]{1,0:T(8,128)S(1)} %copy-done.5, bf16[16,512,1]{1,0,2:T(8,128)(2,1)S(1)} %get-tuple-element.26), kind=kOutput, calls=%fused_computation.2 | convolution fusion | flops 12582912 | bytes 65536 | tf_op jit(solution)/shard_map/bk,bks->bs/dot_general | solution.py:44
  77.3 25.2 %all-to-all-done = bf16[256,2,4,256]{3,2,1,0:T(4,128)(2,1)S(1)} async-done(((bf16[256,2,4,256]{3,2,1,0:T(4,128)(2,1)}), bf16[256,2,4,256]{3,2,1,0:T(4,128)(2,1)S(1)}, u32[]{:S(2)}, u32[]{:S(2)}) %all-to-all-start) | async-done | bytes 1048608 | tf_op jit(solution)/shard_map/all_to_all | solution.py:153
  102.6 0.4 fusion.46
  102.9 0.3 reshape.253
  103.2 0.2 convolution_bitcast_fusion
  103.4 0.2 convolution_bitcast_fusion.1
  103.6 0.1 reshape_squeeze.3
  103.7 0.1 multiply_reduce_fusion
  103.8 0.7 broadcast_in_dim.2
  104.5 0.1 fusion.47
  104.6 6.6 %all-to-all-start.1 = ((f32[256,1,16]{2,1,0:T(1,128)}), f32[256,1,16]{2,1,0:T(1,128)S(1)}, u32[]{:S(2)}, u32[]{:S(2)}) async-start(f32[256,1,16]{2,1,0:T(1,128)} %bitcast.22), calls=%async_computation.1 | async-start | bytes 262144 | tf_op jit(solution)/shard_map/all_to_all | solution.py:160
  111.2 3.3 %multiply_convert_fusion = bf16[2048,1024]{1,0:T(8,128)(2,1)} fusion(bf16[1024,256]{1,0:T(8,128)(2,1)S(1)} %reshape_squeeze.3, bf16[1024,128]{1,0:T(8,128)(2,1)S(1)} %get-tuple-element.21, bf16[1024,128]{1,0:T(8,128)(2,1)S(1)} %get-tuple-element.20), kind=kOutput, calls=%fused_computation.8 | convolution fusion | flops 1081081856 | bytes 5242880 | tf_op jit(solution)/shard_map/dot_general | solution.py:107
  114.5 9.1 %all-to-all-done.1 = f32[256,1,16]{2,1,0:T(1,128)S(1)} async-done(((f32[256,1,16]{2,1,0:T(1,128)}), f32[256,1,16]{2,1,0:T(1,128)S(1)}, u32[]{:S(2)}, u32[]{:S(2)}) %all-to-all-start.1) | async-done | bytes 16416 | tf_op jit(solution)/shard_map/all_to_all | solution.py:160
  123.6 0.3 reduce_sum.19
  123.9 0.1 multiply_convert_fusion.3
  124.0 0.6 copy.24
  (4 shorter events, 0.0 us)
Async XLA Ops:
  0.6 8.4 %copy-start.1 = (s32[256]{0:T(256)S(1)}, s32[256]{0:T(256)}, u32[]{:S(2)}) copy-start(s32[256]{0:T(256)} %param.11) | copy-start | bytes 3076
  0.6 8.4 %copy-start.2 = (s32[256]{0:T(256)S(1)}, s32[256]{0:T(256)}, u32[]{:S(2)}) copy-start(s32[256]{0:T(256)} %param.10) | copy-start | bytes 3076
  53.1 1.3 %copy-start.3 = (f32[256]{0:T(256)S(1)}, f32[256]{0:T(256)}, u32[]{:S(2)}) copy-start(f32[256]{0:T(256)} %param.13) | copy-start | bytes 3076
  53.1 1.3 %copy-start.4 = (f32[256]{0:T(256)S(1)}, f32[256]{0:T(256)}, u32[]{:S(2)}) copy-start(f32[256]{0:T(256)} %param.12) | copy-start | bytes 3076
  53.1 17.6 %copy-start = (s32[16,512]{1,0:T(8,128)S(1)}, s32[16,512]{1,0:T(8,128)}, u32[]{:S(2)}) copy-start(s32[16,512]{1,0:T(8,128)} %param.15) | copy-start | bytes 98308
  53.1 17.8 %copy-start.5 = (s32[16,512]{1,0:T(8,128)S(1)}, s32[16,512]{1,0:T(8,128)}, u32[]{:S(2)}) copy-start(s32[16,512]{1,0:T(8,128)} %param.14) | copy-start | bytes 98308
  56.0 46.5 %all-to-all-start = ((bf16[256,2,4,256]{3,2,1,0:T(4,128)(2,1)}), bf16[256,2,4,256]{3,2,1,0:T(4,128)(2,1)S(1)}, u32[]{:S(2)}, u32[]{:S(2)}) async-start(bf16[256,2,4,256]{3,2,1,0:T(4,128)(2,1)} %fusion.8), calls=%async_computation | async-start | bytes 2097152 | tf_op jit(solution)/shard_map/all_to_all | solution.py:153
  104.6 19.1 %all-to-all-start.1 = ((f32[256,1,16]{2,1,0:T(1,128)}), f32[256,1,16]{2,1,0:T(1,128)S(1)}, u32[]{:S(2)}, u32[]{:S(2)}) async-start(f32[256,1,16]{2,1,0:T(1,128)} %bitcast.22), calls=%async_computation.1 | async-start | bytes 262144 | tf_op jit(solution)/shard_map/all_to_all | solution.py:160

commit v15 on v14

--- a/solution.py
+++ b/solution.py
@@ -86,7 +86,7 @@
     tiles = in_block.reshape(components, inputs_here, samples // lanes, lanes)
     tiles = jnp.transpose(tiles, (2, 0, 1, 3))
     tiles = tiles.reshape(frames, per_frame, rows, lanes)
-    blocks = 4
+    blocks = 8
     return pl.pallas_call(
         fir_kernel,
         grid=(per_frame // blocks,),

time: 126 us -> 128 us (1.016)
  Pallas kernels: 23.7 us -> 25.6 us
    pallas_call x1, Pallas kernels: 23.7 us -> 25.6 us  [polyphase(): pl.pallas_call(fir_kernel, grid=(per_frame // blocks,), in_specs=[pl.Bloc...]
where the time goes in v15:
time: 128 us; the launch traced here: 126 us
  waiting for transfers between devices  34.3 us (27%)
  Pallas kernels  25.6 us (20%)
  matrix products  23.8 us (19%)
  starting transfers between devices  21.2 us (17%)
  local copies, waits for them, and re-layouts  11.6 us (9%)
  other arithmetic  9.09 us (7%)
    pallas_call x1, Pallas kernels, polyphase(): pl.pallas_call(fir_kernel, grid=(per_frame // blocks,), in_specs=[pl.Bloc...  25.6 us
    all_to_all x1, waiting for transfers between devices, per_device(): lax.all_to_all(outgoing, ALL_AXES, split_axis=0, concat_axis=0, tiled=True)  25.2 us
    dot_general x2, matrix products, contract(): lax.dot_general(left_rows, right_rows, contract_dims, preferred_element_t...  17 us
    all_to_all x1, starting transfers between devices, per_device(): lax.all_to_all(outgoing, ALL_AXES, split_axis=0, concat_axis=0, tiled=True)  14.7 us
    all_to_all x1, waiting for transfers between devices, per_device(): lax.all_to_all(spread_power, ALL_AXES, split_axis=0, concat_axis=0, tiled...  9.11 us
    reshape x1, local copies, waits for them, and re-layouts, polyphase(): tiles = in_block.reshape(components, inputs_here, samples // lanes, lanes)  8.39 us
    all_to_all x1, starting transfers between devices, per_device(): lax.all_to_all(spread_power, ALL_AXES, split_axis=0, concat_axis=0, tiled...  6.46 us
    convert_element_type x1, other arithmetic, make_tables(): sin_table = ((sa * cb + ca * sb) * table_scale).astype(jnp.bfloat16)  5.34 us
  transfers between devices with their start and end apart: 2, of which 2 were waited for; matrix products, arithmetic and copies ran while one was open for 8% of the time, Pallas kernels for 0%

profile of v15, /device:TPU:2, one launch (start us, length us, event | category | flops | bytes accessed | tf_op | source)
XLA Modules:
  0.0 126.3 jit_solution(10473936792910976083)
XLA Ops:
  0.6 0.0 copy-start.1
  0.6 0.0 copy-start.2
  0.6 8.4 %copy_bitcast_fusion = bf16[2,4,4448,128]{3,1,0,2:T(4,128)(2,1)} fusion(bf16[2,4,569344]{2,1,0:T(4,128)(2,1)} %param.8), kind=kLoop, calls=%fused_computation.3 | loop fusion | bytes 18219008 | tf_op jit(solution)/shard_map/reshape | solution.py:86
  9.0 0.0 copy-done.1
  9.0 0.0 copy-done.2
  9.1 0.1 copy.19
  9.2 0.1 mul.177
  9.3 1.0 fusion.31
  10.4 5.3 %multiply_convert_fusion.1 = (bf16[512,64,64]{0,2,1:T(8,128)(2,1)}, bf16[512,64,64]{0,2,1:T(8,128)(2,1)}) fusion(f32[512,64]{0,1:T(8,128)S(1)} %get-tuple-element.30, f32[512,64]{0,1:T(8,128)S(1)} %get-tuple-element.29, f32[512,64]{0,1:T(8,128)S(1)} %get-tuple-element.31, f32[512,64]{0,1:T(8,128)S(1)} %get-tuple-element.28), kind=kLoop, calls=%fused_computation.11 | loop fusion | flops 20971520 | bytes 8912896 | tf_op jit(solution)/shard_map/convert_element_type | solution.py:34
  15.7 25.6 %shard_map.95 = bf16[2,4,128,4096]{3,2,1,0:T(8,128)(2,1)} custom-call(bf16[139,32,8,128]{3,2,1,0:T(8,128)(2,1)} %bitcast.47, f32[12,4096]{1,0:T(8,128)} %h_ref.1), custom_call_target="tpu_custom_call" | custom-call | tf_op jit(solution)/shard_map/pallas_call | solution.py:90
  41.3 13.7 %fusion.2 = f32[1024,1024]{1,0:T(8,128)S(1)} fusion(bf16[1024,4096]{1,0:T(8,128)(2,1)} %bitcast.48, bf16[512,4096]{0,1:T(8,128)(2,1)} %bitcast.49, bf16[512,4096]{0,1:T(8,128)(2,1)} %bitcast.50), kind=kOutput, calls=%fused_computation.4 | convolution fusion | flops 8606711808 | bytes 20971520 | tf_op jit(solution)/shard_map/dot_general | solution.py:107
  55.0 0.0 copy-start.3
  55.0 0.0 copy-start.4
  55.0 0.0 copy-start
  55.0 0.0 copy-start.5
  55.0 0.5 slice_add_fusion
  55.5 0.4 concatenate.38
  55.9 0.4 concatenate.37
  56.2 0.0 copy-done.3
  56.2 0.0 copy-done.4
  56.3 0.1 copy.21
  56.4 1.5 %fusion.8 = bf16[256,2,4,256]{3,2,1,0:T(4,128)(2,1)} fusion(f32[256,2,4,128]{3,2,1,0:T(4,128)S(1)} %concatenate.38, f32[256,2,4,128]{3,2,1,0:T(4,128)S(1)} %concatenate.37, f32[256,2]{1,0:T(8,128)S(1)} %copy.21), kind=kLoop, calls=%fused_computation.14 | loop fusion | flops 1572864 | bytes 3147776 | tf_op jit(solution)/shard_map/convert_element_type | solution.py:124
  57.9 14.7 %all-to-all-start = ((bf16[256,2,4,256]{3,2,1,0:T(4,128)(2,1)}), bf16[256,2,4,256]{3,2,1,0:T(4,128)(2,1)S(1)}, u32[]{:S(2)}, u32[]{:S(2)}) async-start(bf16[256,2,4,256]{3,2,1,0:T(4,128)(2,1)} %fusion.8), calls=%async_computation | async-start | bytes 2097152 | tf_op jit(solution)/shard_map/all_to_all | solution.py:153
  72.6 0.0 copy-done
  72.6 0.2 multiply_bitcast_fusion.1
  72.8 0.0 copy-done.5
  72.8 3.2 %fusion = bf16[16,1,512]{2,1,0:T(2,128)(2,1)S(1)} fusion(s32[16,512]{1,0:T(8,128)S(1)} %copy-done.5, bf16[16,512,1]{1,0,2:T(8,128)(2,1)S(1)} %get-tuple-element.27), kind=kOutput, calls=%fused_computation.1 | convolution fusion | flops 12582912 | bytes 65536 | tf_op jit(solution)/shard_map/bk,bks->bs/dot_general | solution.py:45
  76.0 3.2 %fusion.1 = bf16[16,1,512]{2,1,0:T(2,128)(2,1)S(1)} fusion(s32[16,512]{1,0:T(8,128)S(1)} %copy-done.5, bf16[16,512,1]{1,0,2:T(8,128)(2,1)S(1)} %get-tuple-element.26), kind=kOutput, calls=%fused_computation.2 | convolution fusion | flops 12582912 | bytes 65536 | tf_op jit(solution)/shard_map/bk,bks->bs/dot_general | solution.py:44
  79.2 25.2 %all-to-all-done = bf16[256,2,4,256]{3,2,1,0:T(4,128)(2,1)S(1)} async-done(((bf16[256,2,4,256]{3,2,1,0:T(4,128)(2,1)}), bf16[256,2,4,256]{3,2,1,0:T(4,128)(2,1)S(1)}, u32[]{:S(2)}, u32[]{:S(2)}) %all-to-all-start) | async-done | bytes 1048608 | tf_op jit(solution)/shard_map/all_to_all | solution.py:153
  104.5 0.4 fusion.46
  104.8 0.3 reshape.253
  105.1 0.2 convolution_bitcast_fusion
  105.3 0.2 convolution_bitcast_fusion.1
  105.5 0.1 reshape_squeeze.3
  105.6 0.1 multiply_reduce_fusion
  105.7 0.7 broadcast_in_dim.2
  106.4 0.1 fusion.47
  106.5 6.5 %all-to-all-start.1 = ((f32[256,1,16]{2,1,0:T(1,128)}), f32[256,1,16]{2,1,0:T(1,128)S(1)}, u32[]{:S(2)}, u32[]{:S(2)}) async-start(f32[256,1,16]{2,1,0:T(1,128)} %bitcast.22), calls=%async_computation.1 | async-start | bytes 262144 | tf_op jit(solution)/shard_map/all_to_all | solution.py:160
  112.9 3.3 %multiply_convert_fusion = bf16[2048,1024]{1,0:T(8,128)(2,1)} fusion(bf16[1024,256]{1,0:T(8,128)(2,1)S(1)} %reshape_squeeze.3, bf16[1024,128]{1,0:T(8,128)(2,1)S(1)} %get-tuple-element.21, bf16[1024,128]{1,0:T(8,128)(2,1)S(1)} %get-tuple-element.20), kind=kOutput, calls=%fused_computation.8 | convolution fusion | flops 1081081856 | bytes 5242880 | tf_op jit(solution)/shard_map/dot_general | solution.py:107
  116.2 9.1 %all-to-all-done.1 = f32[256,1,16]{2,1,0:T(1,128)S(1)} async-done(((f32[256,1,16]{2,1,0:T(1,128)}), f32[256,1,16]{2,1,0:T(1,128)S(1)}, u32[]{:S(2)}, u32[]{:S(2)}) %all-to-all-start.1) | async-done | bytes 16416 | tf_op jit(solution)/shard_map/all_to_all | solution.py:160
  125.3 0.3 reduce_sum.19
  125.6 0.1 multiply_convert_fusion.3
  125.7 0.6 copy.24
  (4 shorter events, 0.0 us)
Async XLA Ops:
  0.6 8.4 %copy-start.1 = (s32[256]{0:T(256)S(1)}, s32[256]{0:T(256)}, u32[]{:S(2)}) copy-start(s32[256]{0:T(256)} %param.11) | copy-start | bytes 3076
  0.6 8.4 %copy-start.2 = (s32[256]{0:T(256)S(1)}, s32[256]{0:T(256)}, u32[]{:S(2)}) copy-start(s32[256]{0:T(256)} %param.10) | copy-start | bytes 3076
  55.0 1.3 %copy-start.3 = (f32[256]{0:T(256)S(1)}, f32[256]{0:T(256)}, u32[]{:S(2)}) copy-start(f32[256]{0:T(256)} %param.13) | copy-start | bytes 3076
  55.0 1.3 %copy-start.4 = (f32[256]{0:T(256)S(1)}, f32[256]{0:T(256)}, u32[]{:S(2)}) copy-start(f32[256]{0:T(256)} %param.12) | copy-start | bytes 3076
  55.0 17.6 %copy-start = (s32[16,512]{1,0:T(8,128)S(1)}, s32[16,512]{1,0:T(8,128)}, u32[]{:S(2)}) copy-start(s32[16,512]{1,0:T(8,128)} %param.15) | copy-start | bytes 98308
  55.0 17.8 %copy-start.5 = (s32[16,512]{1,0:T(8,128)S(1)}, s32[16,512]{1,0:T(8,128)}, u32[]{:S(2)}) copy-start(s32[16,512]{1,0:T(8,128)} %param.14) | copy-start | bytes 98308
  57.9 46.6 %all-to-all-start = ((bf16[256,2,4,256]{3,2,1,0:T(4,128)(2,1)}), bf16[256,2,4,256]{3,2,1,0:T(4,128)(2,1)S(1)}, u32[]{:S(2)}, u32[]{:S(2)}) async-start(bf16[256,2,4,256]{3,2,1,0:T(4,128)(2,1)} %fusion.8), calls=%async_computation | async-start | bytes 2097152 | tf_op jit(solution)/shard_map/all_to_all | solution.py:153
  106.5 18.9 %all-to-all-start.1 = ((f32[256,1,16]{2,1,0:T(1,128)}), f32[256,1,16]{2,1,0:T(1,128)S(1)}, u32[]{:S(2)}, u32[]{:S(2)}) async-start(f32[256,1,16]{2,1,0:T(1,128)} %bitcast.22), calls=%async_computation.1 | async-start | bytes 262144 | tf_op jit(solution)/shard_map/all_to_all | solution.py:160

commit v16 on v15

--- a/solution.py
+++ b/solution.py
@@ -86,7 +86,7 @@
     tiles = in_block.reshape(components, inputs_here, samples // lanes, lanes)
     tiles = jnp.transpose(tiles, (2, 0, 1, 3))
     tiles = tiles.reshape(frames, per_frame, rows, lanes)
-    blocks = 8
+    blocks = 2
     return pl.pallas_call(
         fir_kernel,
         grid=(per_frame // blocks,),

time: 128 us -> 126 us (0.984)
  Pallas kernels: 25.6 us -> 23.2 us
    pallas_call x1, Pallas kernels: 25.6 us -> 23.2 us  [polyphase(): pl.pallas_call(fir_kernel, grid=(per_frame // blocks,), in_specs=[pl.Bloc...]
where the time goes in v16:
time: 126 us; the launch traced here: 124 us
  waiting for transfers between devices  34.4 us (27%)
  matrix products  23.8 us (19%)
  Pallas kernels  23.2 us (18%)
  starting transfers between devices  21.3 us (17%)
  local copies, waits for them, and re-layouts  11.6 us (9%)
  other arithmetic  9.09 us (7%)
    all_to_all x1, waiting for transfers between devices, per_device(): lax.all_to_all(outgoing, ALL_AXES, split_axis=0, concat_axis=0, tiled=True)  25.2 us
    pallas_call x1, Pallas kernels, polyphase(): pl.pallas_call(fir_kernel, grid=(per_frame // blocks,), in_specs=[pl.Bloc...  23.2 us
    dot_general x2, matrix products, contract(): lax.dot_general(left_rows, right_rows, contract_dims, preferred_element_t...  17 us
    all_to_all x1, starting transfers between devices, per_device(): lax.all_to_all(outgoing, ALL_AXES, split_axis=0, concat_axis=0, tiled=True)  14.7 us
    all_to_all x1, waiting for transfers between devices, per_device(): lax.all_to_all(spread_power, ALL_AXES, split_axis=0, concat_axis=0, tiled...  9.12 us
    reshape x1, local copies, waits for them, and re-layouts, polyphase(): tiles = in_block.reshape(components, inputs_here, samples // lanes, lanes)  8.39 us
    all_to_all x1, starting transfers between devices, per_device(): lax.all_to_all(spread_power, ALL_AXES, split_axis=0, concat_axis=0, tiled...  6.64 us
    convert_element_type x1, other arithmetic, make_tables(): sin_table = ((sa * cb + ca * sb) * table_scale).astype(jnp.bfloat16)  5.34 us
  transfers between devices with their start and end apart: 2, of which 2 were waited for; matrix products, arithmetic and copies ran while one was open for 8% of the time, Pallas kernels for 0%

profile of v16, /device:TPU:2, one launch (start us, length us, event | category | flops | bytes accessed | tf_op | source)
XLA Modules:
  0.0 124.2 jit_solution(2167250028249824433)
XLA Ops:
  0.6 0.0 copy-start.1
  0.6 0.0 copy-start.2
  0.6 8.4 %copy_bitcast_fusion = bf16[2,4,4448,128]{3,1,0,2:T(4,128)(2,1)} fusion(bf16[2,4,569344]{2,1,0:T(4,128)(2,1)} %param.8), kind=kLoop, calls=%fused_computation.3 | loop fusion | bytes 18219008 | tf_op jit(solution)/shard_map/reshape | solution.py:86
  9.0 0.0 copy-done.1
  9.0 0.0 copy-done.2
  9.1 0.1 copy.19
  9.2 0.1 mul.177
  9.3 1.0 fusion.31
  10.4 5.3 %multiply_convert_fusion.1 = (bf16[512,64,64]{0,2,1:T(8,128)(2,1)}, bf16[512,64,64]{0,2,1:T(8,128)(2,1)}) fusion(f32[512,64]{0,1:T(8,128)S(1)} %get-tuple-element.30, f32[512,64]{0,1:T(8,128)S(1)} %get-tuple-element.29, f32[512,64]{0,1:T(8,128)S(1)} %get-tuple-element.31, f32[512,64]{0,1:T(8,128)S(1)} %get-tuple-element.28), kind=kLoop, calls=%fused_computation.11 | loop fusion | flops 20971520 | bytes 8912896 | tf_op jit(solution)/shard_map/convert_element_type | solution.py:34
  15.7 23.2 %shard_map.95 = bf16[2,4,128,4096]{3,2,1,0:T(8,128)(2,1)} custom-call(bf16[139,32,8,128]{3,2,1,0:T(8,128)(2,1)} %bitcast.47, f32[12,4096]{1,0:T(8,128)} %h_ref.1), custom_call_target="tpu_custom_call" | custom-call | tf_op jit(solution)/shard_map/pallas_call | solution.py:90
  39.0 13.7 %fusion.2 = f32[1024,1024]{1,0:T(8,128)S(1)} fusion(bf16[1024,4096]{1,0:T(8,128)(2,1)} %bitcast.48, bf16[512,4096]{0,1:T(8,128)(2,1)} %bitcast.49, bf16[512,4096]{0,1:T(8,128)(2,1)} %bitcast.50), kind=kOutput, calls=%fused_computation.4 | convolution fusion | flops 8606711808 | bytes 20971520 | tf_op jit(solution)/shard_map/dot_general | solution.py:107
  52.6 0.0 copy-start.3
  52.6 0.0 copy-start.4
  52.7 0.0 copy-start
  52.7 0.0 copy-start.5
  52.7 0.5 slice_add_fusion
  53.2 0.4 concatenate.38
  53.5 0.4 concatenate.37
  53.9 0.0 copy-done.3
  53.9 0.0 copy-done.4
  53.9 0.1 copy.21
  54.1 1.5 %fusion.8 = bf16[256,2,4,256]{3,2,1,0:T(4,128)(2,1)} fusion(f32[256,2,4,128]{3,2,1,0:T(4,128)S(1)} %concatenate.38, f32[256,2,4,128]{3,2,1,0:T(4,128)S(1)} %concatenate.37, f32[256,2]{1,0:T(8,128)S(1)} %copy.21), kind=kLoop, calls=%fused_computation.14 | loop fusion | flops 1572864 | bytes 3147776 | tf_op jit(solution)/shard_map/convert_element_type | solution.py:124
  55.6 14.7 %all-to-all-start = ((bf16[256,2,4,256]{3,2,1,0:T(4,128)(2,1)}), bf16[256,2,4,256]{3,2,1,0:T(4,128)(2,1)S(1)}, u32[]{:S(2)}, u32[]{:S(2)}) async-start(bf16[256,2,4,256]{3,2,1,0:T(4,128)(2,1)} %fusion.8), calls=%async_computation | async-start | bytes 2097152 | tf_op jit(solution)/shard_map/all_to_all | solution.py:153
  70.3 0.0 copy-done
  70.3 0.2 multiply_bitcast_fusion.1
  70.5 0.0 copy-done.5
  70.5 3.2 %fusion = bf16[16,1,512]{2,1,0:T(2,128)(2,1)S(1)} fusion(s32[16,512]{1,0:T(8,128)S(1)} %copy-done.5, bf16[16,512,1]{1,0,2:T(8,128)(2,1)S(1)} %get-tuple-element.27), kind=kOutput, calls=%fused_computation.1 | convolution fusion | flops 12582912 | bytes 65536 | tf_op jit(solution)/shard_map/bk,bks->bs/dot_general | solution.py:45
  73.7 3.2 %fusion.1 = bf16[16,1,512]{2,1,0:T(2,128)(2,1)S(1)} fusion(s32[16,512]{1,0:T(8,128)S(1)} %copy-done.5, bf16[16,512,1]{1,0,2:T(8,128)(2,1)S(1)} %get-tuple-element.26), kind=kOutput, calls=%fused_computation.2 | convolution fusion | flops 12582912 | bytes 65536 | tf_op jit(solution)/shard_map/bk,bks->bs/dot_general | solution.py:44
  76.9 25.2 %all-to-all-done = bf16[256,2,4,256]{3,2,1,0:T(4,128)(2,1)S(1)} async-done(((bf16[256,2,4,256]{3,2,1,0:T(4,128)(2,1)}), bf16[256,2,4,256]{3,2,1,0:T(4,128)(2,1)S(1)}, u32[]{:S(2)}, u32[]{:S(2)}) %all-to-all-start) | async-done | bytes 1048608 | tf_op jit(solution)/shard_map/all_to_all | solution.py:153
  102.1 0.4 fusion.46
  102.5 0.3 reshape.253
  102.8 0.2 convolution_bitcast_fusion
  103.0 0.2 convolution_bitcast_fusion.1
  103.1 0.1 reshape_squeeze.3
  103.3 0.1 multiply_reduce_fusion
  103.4 0.7 broadcast_in_dim.2
  104.1 0.1 fusion.47
  104.1 6.6 %all-to-all-start.1 = ((f32[256,1,16]{2,1,0:T(1,128)}), f32[256,1,16]{2,1,0:T(1,128)S(1)}, u32[]{:S(2)}, u32[]{:S(2)}) async-start(f32[256,1,16]{2,1,0:T(1,128)} %bitcast.22), calls=%async_computation.1 | async-start | bytes 262144 | tf_op jit(solution)/shard_map/all_to_all | solution.py:160
  110.8 3.3 %multiply_convert_fusion = bf16[2048,1024]{1,0:T(8,128)(2,1)} fusion(bf16[1024,256]{1,0:T(8,128)(2,1)S(1)} %reshape_squeeze.3, bf16[1024,128]{1,0:T(8,128)(2,1)S(1)} %get-tuple-element.21, bf16[1024,128]{1,0:T(8,128)(2,1)S(1)} %get-tuple-element.20), kind=kOutput, calls=%fused_computation.8 | convolution fusion | flops 1081081856 | bytes 5242880 | tf_op jit(solution)/shard_map/dot_general | solution.py:107
  114.1 9.1 %all-to-all-done.1 = f32[256,1,16]{2,1,0:T(1,128)S(1)} async-done(((f32[256,1,16]{2,1,0:T(1,128)}), f32[256,1,16]{2,1,0:T(1,128)S(1)}, u32[]{:S(2)}, u32[]{:S(2)}) %all-to-all-start.1) | async-done | bytes 16416 | tf_op jit(solution)/shard_map/all_to_all | solution.py:160
  123.2 0.3 reduce_sum.19
  123.5 0.1 multiply_convert_fusion.3
  123.6 0.6 copy.24
  (4 shorter events, 0.0 us)
Async XLA Ops:
  0.6 8.4 %copy-start.1 = (s32[256]{0:T(256)S(1)}, s32[256]{0:T(256)}, u32[]{:S(2)}) copy-start(s32[256]{0:T(256)} %param.11) | copy-start | bytes 3076
  0.6 8.4 %copy-start.2 = (s32[256]{0:T(256)S(1)}, s32[256]{0:T(256)}, u32[]{:S(2)}) copy-start(s32[256]{0:T(256)} %param.10) | copy-start | bytes 3076
  52.6 1.3 %copy-start.3 = (f32[256]{0:T(256)S(1)}, f32[256]{0:T(256)}, u32[]{:S(2)}) copy-start(f32[256]{0:T(256)} %param.13) | copy-start | bytes 3076
  52.6 1.3 %copy-start.4 = (f32[256]{0:T(256)S(1)}, f32[256]{0:T(256)}, u32[]{:S(2)}) copy-start(f32[256]{0:T(256)} %param.12) | copy-start | bytes 3076
  52.7 17.6 %copy-start = (s32[16,512]{1,0:T(8,128)S(1)}, s32[16,512]{1,0:T(8,128)}, u32[]{:S(2)}) copy-start(s32[16,512]{1,0:T(8,128)} %param.15) | copy-start | bytes 98308
  52.7 17.8 %copy-start.5 = (s32[16,512]{1,0:T(8,128)S(1)}, s32[16,512]{1,0:T(8,128)}, u32[]{:S(2)}) copy-start(s32[16,512]{1,0:T(8,128)} %param.14) | copy-start | bytes 98308
  55.6 46.5 %all-to-all-start = ((bf16[256,2,4,256]{3,2,1,0:T(4,128)(2,1)}), bf16[256,2,4,256]{3,2,1,0:T(4,128)(2,1)S(1)}, u32[]{:S(2)}, u32[]{:S(2)}) async-start(bf16[256,2,4,256]{3,2,1,0:T(4,128)(2,1)} %fusion.8), calls=%async_computation | async-start | bytes 2097152 | tf_op jit(solution)/shard_map/all_to_all | solution.py:153
  104.1 19.1 %all-to-all-start.1 = ((f32[256,1,16]{2,1,0:T(1,128)}), f32[256,1,16]{2,1,0:T(1,128)S(1)}, u32[]{:S(2)}, u32[]{:S(2)}) async-start(f32[256,1,16]{2,1,0:T(1,128)} %bitcast.22), calls=%async_computation.1 | async-start | bytes 262144 | tf_op jit(solution)/shard_map/all_to_all | solution.py:160
